TPU v7x, 512 devices: a whole 4x8x8 slice. The times are simulated.
512 devices in a mesh: ka: 64 (over y, z_hi, x), vert: 8 (over z_lo, core).
Axes of the slice: x: 4, y: 8, z: 8 (z_hi: 2, z_lo: 4; z = z_hi * 4 + z_lo), core: 2. Of those that a mesh axis runs over, the one named last changes fastest.
Arguments:
- trial_vector: bfloat16 [64, 112, 896], P('ka'), may hold values from -6 to 6
- left_factor: bfloat16 [64, 2, 256, 12544], P('ka', None, 'vert'), may hold values from -0.03125 to 0.03125
- right_factor: bfloat16 [64, 2, 256, 12544], P(None, None, 'vert', 'ka'), may hold values from -0.5 to 0.5
- kb_table: int32 [64], replicated, may hold values from 0 to 63, as said below
- vir_energy: float32 [64, 112], replicated, may hold values from 0.2 to 1.5
- pair_energy: float32 [8], replicated, may hold values from -2 to -0.5
Outputs:
- sigma_vector: bfloat16 [64, 112, 896], P('ka', 'vert')
Inputs may be any that keep to these rules, and one draw needn't show every extreme that they name: kb_table[k] = (S - k) mod 64 for one S per draw, the sum of the window's ki and kj.
All inputs are finite; a program needn't handle non-finite values.
Results may differ from a plain program's by a relative error of at most 0.0027.
Values may be sent and summed in bfloat16 or wider, within the bound.
No kernel may reach another device: no remote copies, remote signals or barrier semaphores. Data moves between devices by JAX's collectives and lax.ppermute only.
A program may use at most 64 MiB of HBM per device.

v0:
```python
import jax
import jax.numpy as jnp
from jax import lax
from jax.sharding import PartitionSpec as P


def shifted(value, axis, steps):
    count = lax.axis_size(axis)
    pairs = [(source, (source + steps) % count) for source in range(count)]
    return lax.ppermute(value, axis, pairs)


def trial_block(trial_vector, transfer):
    arrived = shifted(trial_vector, "ka", transfer)
    return arrived[0]


def shards(trial_vector, left_factor, right_factor, kb_table, vir_energy, pair_energy):
    kpoints = vir_energy.shape[0]
    virtuals = vir_energy.shape[1]
    transfers = left_factor.shape[1]
    aux_local = left_factor.shape[2]
    pair_count = trial_vector.shape[2] // virtuals
    ordered = jnp.take(right_factor, kb_table, axis=0)
    arrived = lax.all_to_all(ordered, "ka", split_axis=0, concat_axis=3, tiled=True)[0]
    factors = [arrived[transfer] for transfer in range(transfers)]
    own_block = trial_vector[0]
    ladder_sum = jnp.zeros((virtuals, pair_count * virtuals), jnp.float32)
    for transfer in range(transfers):
        source_block = own_block if transfer == 0 else trial_block(trial_vector, transfer)
        trial_rows = source_block.reshape(virtuals * pair_count, virtuals)
        right_block = factors[transfer].reshape(aux_local, virtuals, virtuals)
        half_sum = jnp.einsum(
            "xd,ldb->lxb", trial_rows, right_block, preferred_element_type=jnp.float32
        ).astype(jnp.bfloat16)
        half_sum = half_sum.reshape(aux_local, virtuals, pair_count * virtuals)
        left_block = left_factor[0, transfer].reshape(aux_local, virtuals, virtuals)
        ladder_sum = ladder_sum + jnp.einsum(
            "lac,lcy->ay", left_block, half_sum, preferred_element_type=jnp.float32
        )
    ladder = lax.psum_scatter(ladder_sum, "vert", scatter_dimension=0, tiled=True)
    slab_width = ladder.shape[0]
    offset = lax.axis_index("vert") * slab_width
    labels = jnp.arange(kpoints, dtype=jnp.int32)
    owner_index = lax.axis_index("ka")
    momentum_b = jnp.sum(jnp.where(labels == owner_index, kb_table, 0))
    energy_rows = jnp.sum(jnp.where((labels == owner_index)[:, None], vir_energy, 0.0), axis=0)
    energy_other = jnp.sum(jnp.where((labels == momentum_b)[:, None], vir_energy, 0.0), axis=0)
    energy_a = lax.dynamic_slice_in_dim(energy_rows, offset, slab_width, 0)
    own_rows = lax.dynamic_slice_in_dim(own_block, offset, slab_width, 0).astype(jnp.float32)
    own_rows = own_rows.reshape(slab_width, pair_count, virtuals)
    shift_energy = (
        energy_a[:, None, None] + energy_other[None, None, :] - pair_energy[None, :, None]
    )
    combined = ladder + (shift_energy * own_rows).reshape(slab_width, pair_count * virtuals)
    return combined.astype(jnp.bfloat16)[None]


def solution(mesh):
    in_specs = (
        P("ka", None, None),
        P("ka", None, "vert", None),
        P(None, None, "vert", "ka"),
        P(),
        P(),
        P(),
    )
    out_specs = P("ka", "vert", None)
    return jax.shard_map(shards, mesh=mesh, in_specs=in_specs, out_specs=out_specs, check_vma=False)
```

profile of v0, /device:TPU:1, one launch (start us, length us, event | category | flops | bytes accessed | tf_op | source)
XLA Modules:
  0.0 193.6 jit_solution(14721806893861032890)
XLA Ops:
  0.0 0.8 compare_and_fusion
  0.8 1.3 compare_select_fusion
  2.1 2.0 %gather_fusion = bf16[64,2,32,196]{3,2,1,0:T(8,128)(2,1)} fusion(bf16[64,2,32,196]{3,2,1,0:T(8,128)(2,1)S(1)} %copy-done, s32[1024]{0:T(1024)S(1)} %pad_clamp_fusion), kind=kCustom, calls=%fused_computation | custom fusion | bytes 3211520 | tf_op jit(solution)/shard_map/jit(_take)/gather | solution.py:24
  4.1 3.2 %broadcast_select_fusion = bf16[64,2,32,196]{3,2,1,0:T(8,128)(2,1)} fusion(bf16[64,2,32,196]{3,2,1,0:T(8,128)(2,1)} %gather_fusion, pred[64]{0:T(512)(128)(4,1)S(1)} %compare_and_fusion), kind=kLoop, calls=%fused_computation.5 | loop fusion | flops 802816 | bytes 3211328 | tf_op jit(solution)/shard_map/jit(_take)/select_n | solution.py:24
  7.3 20.0 %all-to-all-start = ((bf16[64,2,32,196]{3,2,1,0:T(8,128)(2,1)}), bf16[64,2,32,196]{3,2,1,0:T(8,128)(2,1)}, u32[]{:S(2)}, u32[]{:S(2)}) async-start(bf16[64,2,32,196]{3,2,1,0:T(8,128)(2,1)} %broadcast_select_fusion), calls=%async_computation | async-start | bytes 4194304 | tf_op jit(solution)/shard_map/all_to_all | solution.py:25
  27.2 2.8 %collective-permute-start = (bf16[1,112,896]{2,1,0:T(8,128)(2,1)S(1)}, bf16[1,112,896]{2,1,0:T(8,128)(2,1)}, u32[]{:S(2)}, u32[]{:S(2)}) collective-permute-start(bf16[1,112,896]{2,1,0:T(8,128)(2,1)S(1)} %copy-done.2), channel_id=1, source_target_pairs={{0,8},{8,16},{16,24},{24,32},{32,40},{40,48},{48,56},{56,64},{64,7... | collective-permute-start | bytes 602120 | tf_op jit(solution)/shard_map/ppermute | solution.py:10
  30.1 0.3 reshape_squeeze.19
  30.4 2.4 %fusion.10 = (bf16[1,1,32,12544]{3,2,1,0:T(8,128)(2,1)}, bf16[1,1,32,12544]{3,2,1,0:T(8,128)(2,1)S(1)}) fusion(bf16[1,2,32,12544]{3,2,1,0:T(8,128)(2,1)} %param.7), kind=kLoop, calls=%fused_computation.26 | loop fusion | bytes 3211264 | tf_op jit(solution)/shard_map/slice | solution.py:37
  32.7 2.7 %reshape_squeeze.23 = bf16[32,112,112]{2,1,0:T(8,128)(2,1)} reshape(bf16[1,1,32,12544]{3,2,1,0:T(8,128)(2,1)S(1)} %get-tuple-element.10) | data formatting | bytes 1605632 | tf_op jit(solution)/shard_map/reshape;squeeze | solution.py:37
  35.5 2.8 %reshape_squeeze.20 = bf16[32,112,112]{2,1,0:T(8,128)(2,1)S(1)} reshape(bf16[1,1,32,12544]{3,2,1,0:T(8,128)(2,1)} %get-tuple-element.9) | data formatting | bytes 1605632 | tf_op jit(solution)/shard_map/reshape;squeeze | solution.py:37
  38.3 0.7 iota_compare_fusion
  39.2 48.6 %collective-permute-done = bf16[1,112,896]{2,1,0:T(8,128)(2,1)} collective-permute-done((bf16[1,112,896]{2,1,0:T(8,128)(2,1)S(1)}, bf16[1,112,896]{2,1,0:T(8,128)(2,1)}, u32[]{:S(2)}, u32[]{:S(2)}) %collective-permute-start) | collective-permute-done | bytes 200736 | tf_op jit(solution)/shard_map/ppermute | solution.py:10
  87.7 1.2 reshape_squeeze.22
  89.0 2.7 %fusion.9 = (bf16[1,1,32,64,196]{4,2,1,3,0:T(8,128)(2,1)}, bf16[1,1,32,64,196]{4,2,1,3,0:T(8,128)(2,1)S(1)}) fusion(bf16[1,2,32,64,196]{4,2,1,3,0:T(8,128)(2,1)} %bitcast.1), kind=kLoop, calls=%fused_computation.25 | loop fusion | bytes 3211264 | tf_op jit(solution)/shard_map/slice | solution.py:26
  91.7 1.6 copy.20
  93.2 4.0 %reshape_squeeze.21 = bf16[32,112,112]{2,1,0:T(8,128)(2,1)} reshape(bf16[1,1,32,64,196]{4,3,2,1,0:T(8,128)(2,1)} %copy.20) | data formatting | bytes 1605632 | tf_op jit(solution)/shard_map/reshape;squeeze | solution.py:32
  97.2 5.8 %fusion.2 = bf16[32,896,112]{1,2,0:T(8,128)(2,1)} fusion(bf16[32,112,112]{2,1,0:T(8,128)(2,1)} %reshape_squeeze.21, bf16[896,112]{1,0:T(8,128)(2,1)S(1)} %reshape_squeeze.22), kind=kOutput, calls=%fused_computation.4 | convolution fusion | flops 722534400 | bytes 7426048 | tf_op jit(solution)/shard_map/xd,ldb->lxb/dot_general | solution.py:33
  103.0 10.4 %copy.23 = bf16[32,896,112]{2,1,0:T(8,128)(2,1)} copy(bf16[32,896,112]{1,2,0:T(8,128)(2,1)} %fusion.2) | data formatting | bytes 12845056 | tf_op jit(solution)/shard_map/convert_element_type | solution.py:35
  113.4 12.8 %reshape.63 = bf16[32,112,896]{2,1,0:T(8,128)(2,1)} reshape(bf16[32,896,112]{2,1,0:T(8,128)(2,1)} %copy.23) | data formatting | bytes 12845056 | tf_op jit(solution)/shard_map/reshape | solution.py:36
  126.2 2.8 %copy.16 = bf16[1,1,32,64,196]{4,3,2,1,0:T(8,128)(2,1)} copy(bf16[1,1,32,64,196]{4,2,1,3,0:T(8,128)(2,1)} %get-tuple-element.7) | data formatting | bytes 1605632 | tf_op jit(solution)/shard_map/slice | solution.py:26
  129.0 4.0 %reshape_squeeze.18 = bf16[32,112,112]{2,1,0:T(8,128)(2,1)} reshape(bf16[1,1,32,64,196]{4,3,2,1,0:T(8,128)(2,1)} %copy.16) | data formatting | bytes 1605632 | tf_op jit(solution)/shard_map/reshape;squeeze | solution.py:32
  133.0 5.7 %fusion.1 = bf16[32,896,112]{1,2,0:T(8,128)(2,1)} fusion(bf16[32,112,112]{2,1,0:T(8,128)(2,1)} %reshape_squeeze.18, bf16[896,112]{1,0:T(8,128)(2,1)S(1)} %reshape_squeeze.19), kind=kOutput, calls=%fused_computation.3 | convolution fusion | flops 722534400 | bytes 7426048 | tf_op jit(solution)/shard_map/xd,ldb->lxb/dot_general | solution.py:33
  138.6 10.4 %copy.19 = bf16[32,896,112]{2,1,0:T(8,128)(2,1)} copy(bf16[32,896,112]{1,2,0:T(8,128)(2,1)} %fusion.1) | data formatting | bytes 12845056 | tf_op jit(solution)/shard_map/convert_element_type | solution.py:35
  149.0 12.7 %reshape.62 = bf16[32,112,896]{2,1,0:T(8,128)(2,1)} reshape(bf16[32,896,112]{2,1,0:T(8,128)(2,1)} %copy.19) | data formatting | bytes 12845056 | tf_op jit(solution)/shard_map/reshape | solution.py:36
  161.8 4.4 %convolution_bitcast_fusion = f32[896,112]{0,1:T(8,128)S(1)} fusion(bf16[32,112,112]{2,1,0:T(8,128)(2,1)} %reshape_squeeze.23, bf16[32,112,896]{2,1,0:T(8,128)(2,1)} %reshape.63), kind=kOutput, calls=%fused_computation.6 | convolution fusion | flops 719323136 | bytes 7626752 | tf_op jit(solution)/shard_map/lac,lcy->ay/dot_general | solution.py:38
  166.2 0.5 copy-done.1
  166.7 1.3 fusion.4
  168.0 18.7 %fusion = f32[16,896]{1,0:T(8,128)S(1)} fusion(f32[112,896]{1,0:T(8,128)S(1)} %fusion.4), kind=kCustom, calls=%all-reduce-scatter | all-reduce-scatter fusion | flops 114689 | bytes 460800
  186.7 2.2 %collective-permute-start.1 = (f32[14,896]{1,0:T(8,128)S(1)}, f32[14,896]{1,0:T(8,128)S(1)}, u32[]{:S(2)}, u32[]{:S(2)}) collective-permute-start(f32[14,896]{1,0:T(8,128)S(1)} %slice.22), channel_id=1, source_target_pairs={{0,1},{1,2},{2,3},{3,4},{4,5},{5,6},{6,7},{8,9},{9,10},{10,11},{11... | collective-permute-start | bytes 150536
  189.2 1.3 dynamic-slice.5
  191.2 0.8 collective-permute-done.1
  192.1 1.4 fusion.8
  (20 shorter events, 0.7 us)
Async XLA Ops:
  0.0 2.1 %copy-start = (bf16[64,2,32,196]{3,2,1,0:T(8,128)(2,1)S(1)}, bf16[64,2,32,196]{3,2,1,0:T(8,128)(2,1)}, u32[]{:S(2)}) copy-start(bf16[64,2,32,196]{3,2,1,0:T(8,128)(2,1)} %param.8) | copy-start | bytes 4816900
  0.0 27.2 %copy-start.2 = (bf16[1,112,896]{2,1,0:T(8,128)(2,1)S(1)}, bf16[1,112,896]{2,1,0:T(8,128)(2,1)}, u32[]{:S(2)}) copy-start(bf16[1,112,896]{2,1,0:T(8,128)(2,1)} %param.6) | copy-start | bytes 602116
  7.3 31.7 %copy-start.3 = (f32[64,112]{1,0:T(8,128)S(1)}, f32[64,112]{1,0:T(8,128)}, u32[]{:S(2)}) copy-start(f32[64,112]{1,0:T(8,128)} %param.10) | copy-start | bytes 86020
  7.3 81.7 %all-to-all-start = ((bf16[64,2,32,196]{3,2,1,0:T(8,128)(2,1)}), bf16[64,2,32,196]{3,2,1,0:T(8,128)(2,1)}, u32[]{:S(2)}, u32[]{:S(2)}) async-start(bf16[64,2,32,196]{3,2,1,0:T(8,128)(2,1)} %broadcast_select_fusion), calls=%async_computation | async-start | bytes 4194304 | tf_op jit(solution)/shard_map/all_to_all | solution.py:25
  27.2 60.5 %collective-permute-start = (bf16[1,112,896]{2,1,0:T(8,128)(2,1)S(1)}, bf16[1,112,896]{2,1,0:T(8,128)(2,1)}, u32[]{:S(2)}, u32[]{:S(2)}) collective-permute-start(bf16[1,112,896]{2,1,0:T(8,128)(2,1)S(1)} %copy-done.2), channel_id=1, source_target_pairs={{0,8},{8,16},{16,24},{24,32},{32,40},{40,48},{48,56},{56,64},{64,7... | collective-permute-start | bytes 602120 | tf_op jit(solution)/shard_map/ppermute | solution.py:10
  161.8 4.9 %copy-start.1 = (bf16[32,112,896]{2,1,0:T(8,128)(2,1)S(1)}, bf16[32,112,896]{2,1,0:T(8,128)(2,1)}, u32[]{:S(2)}) copy-start(bf16[32,112,896]{2,1,0:T(8,128)(2,1)} %reshape.62) | copy-start | bytes 19267588
  166.7 22.4 %copy-start.4 = (f32[8]{0:T(128)S(1)}, f32[8]{0:T(128)}, u32[]{:S(2)}) copy-start(f32[8]{0:T(128)} %param.11) | copy-start | bytes 100
  186.7 5.3 %collective-permute-start.1 = (f32[14,896]{1,0:T(8,128)S(1)}, f32[14,896]{1,0:T(8,128)S(1)}, u32[]{:S(2)}, u32[]{:S(2)}) collective-permute-start(f32[14,896]{1,0:T(8,128)S(1)} %slice.22), channel_id=1, source_target_pairs={{0,1},{1,2},{2,3},{3,4},{4,5},{5,6},{6,7},{8,9},{9,10},{10,11},{11... | collective-permute-start | bytes 150536
where the time goes:
time: 196 us; the launch traced here: 194 us
  local copies, waits for them, and re-layouts  75 us (38%)
  waiting for transfers between devices  49.4 us (25%)
  starting transfers between devices  25 us (13%)
  blocking collectives  18.7 us (10%)
  matrix products  17.2 us (9%)
  other arithmetic  7.51 us (4%)
    ppermute x1, waiting for transfers between devices, shifted(): return lax.ppermute(value, axis, pairs)  48.6 us
    reshape x2, local copies, waits for them, and re-layouts, shards(): half_sum = half_sum.reshape(aux_local, virtuals, pair_count * virtuals)  25.5 us
    convert_element_type x2, local copies, waits for them, and re-layouts, shards(): half_sum = jnp.einsum('xd,ldb->lxb', trial_rows, right_block, preferred_e...  20.8 us
    all_to_all x1, starting transfers between devices, shards(): lax.all_to_all(ordered, 'ka', split_axis=0, concat_axis=3, tiled=True)[0]  20 us
    unnamed x1, blocking collectives  18.7 us
    dot_general x2, matrix products, shards(): jnp.einsum('xd,ldb->lxb', trial_rows, right_block, preferred_element_type...  11.4 us
    another operation x2, local copies, waits for them, and re-layouts, shards(): right_block = factors[transfer].reshape(aux_local, virtuals, virtuals)  8.03 us
    slice x3, local copies, waits for them, and re-layouts, shards(): factors = [arrived[transfer] for transfer in range(transfers)]  7.05 us
  transfers between devices with their start and end apart: 3, of which 2 were waited for; matrix products, arithmetic and copies ran while one was open for 6% of the time, Pallas kernels for 0%

commit v1 on v0

--- a/solution.py
+++ b/solution.py
@@ -1,6 +1,10 @@
+import functools
+
 import jax
 import jax.numpy as jnp
 from jax import lax
+from jax.experimental import pallas as pl
+from jax.experimental.pallas import tpu as pltpu
 from jax.sharding import PartitionSpec as P
 
 
@@ -10,9 +14,64 @@
     return lax.ppermute(value, axis, pairs)
 
 
-def trial_block(trial_vector, transfer):
-    arrived = shifted(trial_vector, "ka", transfer)
-    return arrived[0]
+def ladder_kernel(ct_ref, tt_ref, b_ref, out_ref, *, chunk, nv, pairs, lanes):
+    q = pl.program_id(0)
+    j = pl.program_id(1)
+
+    @pl.when((q == 0) & (j == 0))
+    def _():
+        out_ref[...] = jnp.zeros_like(out_ref)
+
+    half = jnp.dot(ct_ref[0], tt_ref[0], preferred_element_type=jnp.float32)
+    half = half.astype(jnp.bfloat16)
+    acc = out_ref[...]
+    for l in range(chunk):
+        rows = half[l * nv:(l + 1) * nv]
+        stacked = jnp.concatenate(
+            [rows[:, p * lanes:p * lanes + nv] for p in range(pairs)], axis=0
+        )
+        acc = acc + lax.dot_general(
+            stacked, b_ref[0, l], (((1,), (1,)), ((), ())),
+            preferred_element_type=jnp.float32,
+        )
+    out_ref[...] = acc
+
+
+def ladder_transposed(ct, tt, bq, chunk=8):
+    transfers, rows, nv = ct.shape
+    aux = bq.shape[1]
+
+    pairs = tt.shape[2] // 128
+    lanes = 128
+    steps = aux // chunk
+    kernel = functools.partial(ladder_kernel, chunk=chunk, nv=nv, pairs=pairs, lanes=lanes)
+    flops = 2 * transfers * aux * nv * nv * (pairs * lanes + pairs * nv)
+    return pl.pallas_call(
+        kernel,
+        out_shape=jax.ShapeDtypeStruct((pairs * nv, nv), jnp.float32),
+        grid=(transfers, steps),
+        in_specs=[
+            pl.BlockSpec((1, chunk * nv, nv), lambda q, j: (q, j, 0)),
+            pl.BlockSpec((1, nv, pairs * lanes), lambda q, j: (q, 0, 0)),
+            pl.BlockSpec((1, chunk, nv, nv), lambda q, j: (q, j, 0, 0)),
+        ],
+        out_specs=pl.BlockSpec((pairs * nv, nv), lambda q, j: (0, 0)),
+        compiler_params=pltpu.CompilerParams(
+            dimension_semantics=("arbitrary", "arbitrary"),
+            vmem_limit_bytes=48 * 1024 * 1024,
+        ),
+        cost_estimate=pl.CostEstimate(
+            flops=flops, transcendentals=0,
+            bytes_accessed=2 * (ct.size + tt.size + bq.size) + 4 * pairs * nv * nv,
+        ),
+    )(ct, tt, bq)
+
+
+def trial_transposed(block, virtuals, pair_count):
+    t = block.reshape(virtuals, pair_count, virtuals)
+    t = jnp.transpose(t, (2, 1, 0))
+    t = jnp.pad(t, ((0, 0), (0, 0), (0, 128 - virtuals)))
+    return t.reshape(virtuals, pair_count * 128)
 
 
 def shards(trial_vector, left_factor, right_factor, kb_table, vir_energy, pair_energy):
@@ -21,23 +80,18 @@
     transfers = left_factor.shape[1]
     aux_local = left_factor.shape[2]
     pair_count = trial_vector.shape[2] // virtuals
-    ordered = jnp.take(right_factor, kb_table, axis=0)
+    ordered = right_factor.at[kb_table].get(mode="promise_in_bounds")
     arrived = lax.all_to_all(ordered, "ka", split_axis=0, concat_axis=3, tiled=True)[0]
-    factors = [arrived[transfer] for transfer in range(transfers)]
+    right = arrived.reshape(transfers, aux_local, virtuals, virtuals)
+    ct = jnp.swapaxes(right, 2, 3).reshape(transfers, aux_local * virtuals, virtuals)
     own_block = trial_vector[0]
-    ladder_sum = jnp.zeros((virtuals, pair_count * virtuals), jnp.float32)
-    for transfer in range(transfers):
-        source_block = own_block if transfer == 0 else trial_block(trial_vector, transfer)
-        trial_rows = source_block.reshape(virtuals * pair_count, virtuals)
-        right_block = factors[transfer].reshape(aux_local, virtuals, virtuals)
-        half_sum = jnp.einsum(
-            "xd,ldb->lxb", trial_rows, right_block, preferred_element_type=jnp.float32
-        ).astype(jnp.bfloat16)
-        half_sum = half_sum.reshape(aux_local, virtuals, pair_count * virtuals)
-        left_block = left_factor[0, transfer].reshape(aux_local, virtuals, virtuals)
-        ladder_sum = ladder_sum + jnp.einsum(
-            "lac,lcy->ay", left_block, half_sum, preferred_element_type=jnp.float32
-        )
+    blocks = [own_block] + [
+        shifted(trial_vector, "ka", t)[0] for t in range(1, transfers)
+    ]
+    tt = jnp.stack([trial_transposed(b, virtuals, pair_count) for b in blocks])
+    bq = left_factor[0].reshape(transfers, aux_local, virtuals, virtuals)
+    ladder_t = ladder_transposed(ct, tt, bq)
+    ladder_sum = ladder_t.T
     ladder = lax.psum_scatter(ladder_sum, "vert", scatter_dimension=0, tiled=True)
     slab_width = ladder.shape[0]
     offset = lax.axis_index("vert") * slab_width

time: 196 us -> 207 us (1.056)
  waiting for transfers between devices: 49.4 us -> 120 us
  local copies, waits for them, and re-layouts: 75 us -> 28.6 us
  blocking collectives: 18.7 us -> 0 us
  matrix products: 17.2 us -> 0 us
  Pallas kernels: 0 us -> 15.5 us
  between operations: 0.8 us -> 14.2 us
  other arithmetic: 7.51 us -> 3.64 us
  starting transfers between devices: 25 us -> 22.8 us
    unnamed x1 -> x2, waiting for transfers between devices: 0.83 us -> 69.6 us
    reshape x2 -> x0, local copies, waits for them, and re-layouts: 25.5 us -> none  [shards(): half_sum = half_sum.reshape(aux_local, virtuals, pair_count * virtuals)]
    convert_element_type x2 -> x0, local copies, waits for them, and re-layouts: 20.8 us -> none  [shards(): half_sum = jnp.einsum('xd,ldb->lxb', trial_rows, right_block, preferred_e...]
    unnamed x1 -> x0, blocking collectives: 18.7 us -> none
    dot_general x4 -> x0, matrix products: 17.2 us -> none  [the longest x2 11.4 us: shards(): jnp.einsum('xd,ldb->lxb', trial_rows, right_block, preferred_element_type...]
    pallas_call x0 -> x1, Pallas kernels: none -> 15.5 us  [ladder_transposed(): pl.pallas_call(kernel, out_shape=jax.ShapeDtypeStruct((pairs * nv, nv), j...]
    slice x4 -> x0, local copies, waits for them, and re-layouts: 9.42 us -> none  [the longest x3 7.05 us: shards(): factors = [arrived[transfer] for transfer in range(transfers)]]
    select_n x2 -> x0, other arithmetic: 4.44 us -> none  [shards(): ordered = jnp.take(right_factor, kb_table, axis=0)]
  transfers between devices with their start and end apart: 3 -> 3, of which waited for: 2 -> 2; matrix products, arithmetic and copies ran while one was open for 6% -> 5% of each run, Pallas kernels for 0% -> 0%
where the time goes in v1:
time: 207 us; the launch traced here: 205 us
  waiting for transfers between devices  120 us (58%)
  local copies, waits for them, and re-layouts  28.6 us (14%)
  starting transfers between devices  22.8 us (11%)
  Pallas kernels  15.5 us (7%)
  between operations  14.2 us (7%)
  other arithmetic  3.64 us (2%)
    unnamed x2, waiting for transfers between devices  69.6 us
    ppermute x1, waiting for transfers between devices, shifted(): return lax.ppermute(value, axis, pairs)  50.8 us
    all_to_all x1, starting transfers between devices, shards(): lax.all_to_all(ordered, 'ka', split_axis=0, concat_axis=3, tiled=True)[0]  20 us
    pallas_call x1, Pallas kernels, ladder_transposed(): pl.pallas_call(kernel, out_shape=jax.ShapeDtypeStruct((pairs * nv, nv), j...  15.5 us
    another operation x1, local copies, waits for them, and re-layouts, shards(): right = arrived.reshape(transfers, aux_local, virtuals, virtuals)  6.18 us
    another operation x1, local copies, waits for them, and re-layouts, shards(): bq = left_factor[0].reshape(transfers, aux_local, virtuals, virtuals)  5.53 us
    unnamed x14, local copies, waits for them, and re-layouts  4.64 us
  transfers between devices with their start and end apart: 3, of which 2 were waited for; matrix products, arithmetic and copies ran while one was open for 5% of the time, Pallas kernels for 0%

profile of v1, /device:TPU:1, one launch (start us, length us, event | category | flops | bytes accessed | tf_op | source)
XLA Modules:
  0.0 205.3 jit_solution(2041256936863842458)
XLA Ops:
  6.5 1.4 select_reduce_fusion.2
  8.0 0.2 copy-done
  8.1 2.0 gather_fusion
  10.1 20.0 %all-to-all-start = ((bf16[64,2,32,196]{3,2,1,0:T(8,128)(2,1)}), bf16[64,2,32,196]{3,2,1,0:T(8,128)(2,1)}, u32[]{:S(2)}, u32[]{:S(2)}) async-start(bf16[64,2,32,196]{3,2,1,0:T(8,128)(2,1)} %gather_fusion), calls=%async_computation | async-start | bytes 4194304 | tf_op jit(solution)/shard_map/all_to_all | solution.py:84
  30.1 0.0 all-reduce.5.cloned.1.call-start
  30.2 2.8 %collective-permute-start = (bf16[1,112,896]{2,1,0:T(8,128)(2,1)S(1)}, bf16[1,112,896]{2,1,0:T(8,128)(2,1)S(1)}, u32[]{:S(2)}, u32[]{:S(2)}) collective-permute-start(bf16[1,112,896]{2,1,0:T(8,128)(2,1)S(1)} %copy-done.3), channel_id=1, source_target_pairs={{0,8},{8,16},{16,24},{24,32},{32,40},{40,48},{48,56},{56,64},{64,7... | collective-permute-start | bytes 602120 | tf_op jit(solution)/shard_map/ppermute | solution.py:14
  33.0 0.3 reshape_squeeze.13
  33.3 0.2 copy.19
  33.6 0.1 stack_reshape.6
  33.7 5.5 %reshape_squeeze.15.b_ref = bf16[2,32,112,112]{3,2,1,0:T(8,128)(2,1)} reshape(bf16[1,2,32,12544]{3,2,1,0:T(8,128)(2,1)} %param.7) | data formatting | bytes 3211264 | tf_op jit(solution)/shard_map/reshape;squeeze | solution.py:92
  39.3 0.2 copy.25
  39.5 0.1 sub.22
  39.5 0.1 sub.23
  39.6 50.8 %collective-permute-done = bf16[1,112,896]{2,1,0:T(8,128)(2,1)S(1)} collective-permute-done((bf16[1,112,896]{2,1,0:T(8,128)(2,1)S(1)}, bf16[1,112,896]{2,1,0:T(8,128)(2,1)S(1)}, u32[]{:S(2)}, u32[]{:S(2)}) %collective-permute-start) | collective-permute-done | bytes 200736 | tf_op jit(solution)/shard_map/ppermute | solution.py:14
  90.4 0.3 reshape_squeeze.14
  90.7 0.2 copy.20
  91.0 0.1 stack_reshape.7
  91.2 4.1 %copy.17 = bf16[1,2,32,64,196]{4,3,2,1,0:T(8,128)(2,1)} copy(bf16[1,2,32,64,196]{4,2,1,3,0:T(8,128)(2,1)} %bitcast.3) | data formatting | bytes 3211264 | tf_op jit(solution)/shard_map/all_to_all | solution.py:84
  95.3 6.2 %reshape_squeeze.12 = bf16[2,32,112,112]{3,2,1,0:T(8,128)(2,1)} reshape(bf16[1,2,32,64,196]{4,3,2,1,0:T(8,128)(2,1)} %copy.17) | data formatting | bytes 3211264 | tf_op jit(solution)/shard_map/reshape;squeeze | solution.py:85
  101.4 3.9 %copy.18 = bf16[2,32,112,112]{3,2,1,0:T(8,128)(2,1)} copy(bf16[2,32,112,112]{2,3,1,0:T(8,128)(2,1)} %bitcast.24) | data formatting | bytes 3211264 | tf_op jit(solution)/shard_map/transpose | solution.py:86
  105.3 1.5 copy-done.1
  106.8 1.5 copy-done.2
  108.3 15.5 %shard_map.64 = f32[896,112]{1,0:T(8,128)} custom-call(bf16[2,3584,112]{2,1,0:T(8,128)(2,1)S(1)} %bitcast.23, bf16[2,112,1024]{2,1,0:T(8,128)(2,1)S(1)} %pad_maximum_fusion.tt_ref, bf16[2,32,112,112]{3,2,1,0:T(8,128)(2,1)S(1)} %copy-done.2), custom_call_target="tpu_custom_call" | custom-call | flops 3082813440 | bytes 4071424 | tf_op jit(solution)/shard_map/pallas_call | solution.py:49
  123.9 0.0 all-reduce.5.cloned.1.call-update
  123.9 0.7 iota_compare_fusion
  124.6 0.1 select_reduce_fusion.1
  124.7 0.1 dynamic_slice.6
  124.7 1.3 dynamic-slice.1
  126.7 0.1 broadcast_add_fusion
  126.7 69.6 %all-reduce.5.cloned.1.call-done = f32[112,896]{0,1:T(8,128)} async-done(((f32[112,896]{0,1:T(8,128)}), f32[112,896]{0,1:T(8,128)}) %all-reduce.5.cloned.1.call-update) | async-done | bytes 401424
  196.3 1.3 fusion.1
  197.7 0.8 copy.22
  (16 shorter events, 0.2 us)
Async XLA Ops:
  6.5 1.6 copy-start
  10.1 20.0 %copy-start.3 = (bf16[1,112,896]{2,1,0:T(8,128)(2,1)S(1)}, bf16[1,112,896]{2,1,0:T(8,128)(2,1)}, u32[]{:S(2)}) copy-start(bf16[1,112,896]{2,1,0:T(8,128)(2,1)} %param.6) | copy-start | bytes 602116
  10.1 81.0 %all-to-all-start = ((bf16[64,2,32,196]{3,2,1,0:T(8,128)(2,1)}), bf16[64,2,32,196]{3,2,1,0:T(8,128)(2,1)}, u32[]{:S(2)}, u32[]{:S(2)}) async-start(bf16[64,2,32,196]{3,2,1,0:T(8,128)(2,1)} %gather_fusion), calls=%async_computation | async-start | bytes 4194304 | tf_op jit(solution)/shard_map/all_to_all | solution.py:84
  30.1 166.2 %all-reduce.5.cloned.1.call-start = ((), (), s32[]{:S(2)}) async-start(), calls=%async_computation.1 | async-start | bytes 917504
  30.2 60.3 %collective-permute-start = (bf16[1,112,896]{2,1,0:T(8,128)(2,1)S(1)}, bf16[1,112,896]{2,1,0:T(8,128)(2,1)S(1)}, u32[]{:S(2)}, u32[]{:S(2)}) collective-permute-start(bf16[1,112,896]{2,1,0:T(8,128)(2,1)S(1)} %copy-done.3), channel_id=1, source_target_pairs={{0,8},{8,16},{16,24},{24,32},{32,40},{40,48},{48,56},{56,64},{64,7... | collective-permute-start | bytes 602120 | tf_op jit(solution)/shard_map/ppermute | solution.py:14
  33.6 5.9 %copy-start.5 = (f32[8]{0:T(128)S(1)}, f32[8]{0:T(128)}, u32[]{:S(2)}) copy-start(f32[8]{0:T(128)} %param.11) | copy-start | bytes 100
  105.3 1.5 copy-start.1
  106.8 1.5 copy-start.2
  108.3 16.2 %copy-start.4 = (f32[64,112]{1,0:T(8,128)S(1)}, f32[64,112]{1,0:T(8,128)}, u32[]{:S(2)}) copy-start(f32[64,112]{1,0:T(8,128)} %param.10) | copy-start | bytes 86020
Sparse Core Ops, SparseCore 0:
  124.0 72.2 all-reduce.4

commit v2 on v1

--- a/solution.py
+++ b/solution.py
@@ -14,15 +14,14 @@
     return lax.ppermute(value, axis, pairs)
 
 
-def ladder_kernel(ct_ref, tt_ref, b_ref, out_ref, *, chunk, nv, pairs, lanes):
-    q = pl.program_id(0)
-    j = pl.program_id(1)
+def ladder_kernel(ct_ref, tt_ref, b_ref, acc_ref, out_ref, *, chunk, nv, pairs, lanes):
+    j = pl.program_id(0)
 
-    @pl.when((q == 0) & (j == 0))
+    @pl.when(j == 0)
     def _():
-        out_ref[...] = jnp.zeros_like(out_ref)
+        out_ref[...] = acc_ref[...]
 
-    half = jnp.dot(ct_ref[0], tt_ref[0], preferred_element_type=jnp.float32)
+    half = jnp.dot(ct_ref[...], tt_ref[...], preferred_element_type=jnp.float32)
     half = half.astype(jnp.bfloat16)
     acc = out_ref[...]
     for l in range(chunk):
@@ -31,40 +30,41 @@
             [rows[:, p * lanes:p * lanes + nv] for p in range(pairs)], axis=0
         )
         acc = acc + lax.dot_general(
-            stacked, b_ref[0, l], (((1,), (1,)), ((), ())),
+            stacked, b_ref[l], (((1,), (1,)), ((), ())),
             preferred_element_type=jnp.float32,
         )
     out_ref[...] = acc
 
 
-def ladder_transposed(ct, tt, bq, chunk=8):
-    transfers, rows, nv = ct.shape
-    aux = bq.shape[1]
-
-    pairs = tt.shape[2] // 128
+def ladder_transposed(ct, tt, bq, acc, chunk=8):
+    rows, nv = ct.shape
+    aux = bq.shape[0]
     lanes = 128
+    pairs = tt.shape[1] // lanes
     steps = aux // chunk
     kernel = functools.partial(ladder_kernel, chunk=chunk, nv=nv, pairs=pairs, lanes=lanes)
-    flops = 2 * transfers * aux * nv * nv * (pairs * lanes + pairs * nv)
+    flops = 2 * aux * nv * nv * (pairs * lanes + pairs * nv)
     return pl.pallas_call(
         kernel,
         out_shape=jax.ShapeDtypeStruct((pairs * nv, nv), jnp.float32),
-        grid=(transfers, steps),
+        grid=(steps,),
         in_specs=[
-            pl.BlockSpec((1, chunk * nv, nv), lambda q, j: (q, j, 0)),
-            pl.BlockSpec((1, nv, pairs * lanes), lambda q, j: (q, 0, 0)),
-            pl.BlockSpec((1, chunk, nv, nv), lambda q, j: (q, j, 0, 0)),
+            pl.BlockSpec((chunk * nv, nv), lambda j: (j, 0)),
+            pl.BlockSpec((nv, pairs * lanes), lambda j: (0, 0)),
+            pl.BlockSpec((chunk, nv, nv), lambda j: (j, 0, 0)),
+            pl.BlockSpec((pairs * nv, nv), lambda j: (0, 0)),
         ],
-        out_specs=pl.BlockSpec((pairs * nv, nv), lambda q, j: (0, 0)),
+        out_specs=pl.BlockSpec((pairs * nv, nv), lambda j: (0, 0)),
+        input_output_aliases={3: 0},
         compiler_params=pltpu.CompilerParams(
-            dimension_semantics=("arbitrary", "arbitrary"),
+            dimension_semantics=("arbitrary",),
             vmem_limit_bytes=48 * 1024 * 1024,
         ),
         cost_estimate=pl.CostEstimate(
             flops=flops, transcendentals=0,
-            bytes_accessed=2 * (ct.size + tt.size + bq.size) + 4 * pairs * nv * nv,
+            bytes_accessed=2 * (ct.size + tt.size + bq.size) + 8 * pairs * nv * nv,
         ),
-    )(ct, tt, bq)
+    )(ct, tt, bq, acc)
 
 
 def trial_transposed(block, virtuals, pair_count):
@@ -81,19 +81,27 @@
     aux_local = left_factor.shape[2]
     pair_count = trial_vector.shape[2] // virtuals
     ordered = right_factor.at[kb_table].get(mode="promise_in_bounds")
-    arrived = lax.all_to_all(ordered, "ka", split_axis=0, concat_axis=3, tiled=True)[0]
-    right = arrived.reshape(transfers, aux_local, virtuals, virtuals)
-    ct = jnp.swapaxes(right, 2, 3).reshape(transfers, aux_local * virtuals, virtuals)
     own_block = trial_vector[0]
-    blocks = [own_block] + [
-        shifted(trial_vector, "ka", t)[0] for t in range(1, transfers)
-    ]
-    tt = jnp.stack([trial_transposed(b, virtuals, pair_count) for b in blocks])
     bq = left_factor[0].reshape(transfers, aux_local, virtuals, virtuals)
-    ladder_t = ladder_transposed(ct, tt, bq)
+    ladder_t = jnp.zeros((pair_count * virtuals, virtuals), jnp.float32)
+    previous = None
+    for transfer in range(transfers):
+        piece = ordered[:, transfer]
+        if previous is not None:
+            piece, previous = lax.optimization_barrier((piece, previous))
+        arrived = lax.all_to_all(piece, "ka", split_axis=0, concat_axis=2, tiled=True)[0]
+        previous = arrived
+        right = arrived.reshape(aux_local, virtuals, virtuals)
+        ct = jnp.swapaxes(right, 1, 2).reshape(aux_local * virtuals, virtuals)
+        block = own_block if transfer == 0 else shifted(trial_vector, "ka", transfer)[0]
+        tt = trial_transposed(block, virtuals, pair_count)
+        ladder_t = ladder_transposed(ct, tt, bq[transfer], ladder_t)
     ladder_sum = ladder_t.T
-    ladder = lax.psum_scatter(ladder_sum, "vert", scatter_dimension=0, tiled=True)
-    slab_width = ladder.shape[0]
+    vert = lax.axis_size("vert")
+    slab_width = virtuals // vert
+    ladder = lax.all_to_all(
+        ladder_sum.reshape(vert, slab_width, -1), "vert", 0, 0, tiled=True
+    ).sum(0)
     offset = lax.axis_index("vert") * slab_width
     labels = jnp.arange(kpoints, dtype=jnp.int32)
     owner_index = lax.axis_index("ka")

time: 207 us -> 151 us (0.73)
  waiting for transfers between devices: 120 us -> 38.3 us
  starting transfers between devices: 22.8 us -> 50.8 us
  between operations: 14.2 us -> 0.18 us
  local copies, waits for them, and re-layouts: 28.6 us -> 42.4 us
    unnamed x2 -> x0, waiting for transfers between devices: 69.6 us -> none
    ppermute x1, waiting for transfers between devices: 50.8 us -> 0.01 us  [shifted(): return lax.ppermute(value, axis, pairs)]
    all_to_all x1 -> x3, waiting for transfers between devices: 0.01 us -> 38.3 us  [the longest x2 26.4 us: shards(): lax.all_to_all(piece, 'ka', split_axis=0, concat_axis=2, tiled=True)[0]]
    all_to_all x1 -> x3, starting transfers between devices: 20 us -> 47.9 us  [the longest x2 28.7 us: shards(): lax.all_to_all(piece, 'ka', split_axis=0, concat_axis=2, tiled=True)[0]]
    squeeze x0 -> x3, local copies, waits for them, and re-layouts: none -> 10.1 us  [the longest x2 7.08 us: shards(): ladder_t = ladder_transposed(ct, tt, bq[transfer], ladder_t)]
    another operation x4, local copies, waits for them, and re-layouts: 1 us -> 5.18 us  [trial_transposed(): t = block.reshape(virtuals, pair_count, virtuals)]
    another operation x4 -> x2, local copies, waits for them, and re-layouts: 11.9 us -> 8.03 us  [shards(): right = arrived.reshape(aux_local, virtuals, virtuals)]
    slice x0 -> x1, local copies, waits for them, and re-layouts: none -> 2.71 us  [shards(): ladder_t = ladder_transposed(ct, tt, bq[transfer], ladder_t)]
  transfers between devices with their start and end apart: 3 -> 4, of which waited for: 2 -> 2; matrix products, arithmetic and copies ran while one was open for 5% -> 17% of each run, Pallas kernels for 0% -> 0%
where the time goes in v2:
time: 151 us; the launch traced here: 150 us
  starting transfers between devices  50.8 us (34%)
  local copies, waits for them, and re-layouts  42.4 us (28%)
  waiting for transfers between devices  38.3 us (25%)
  Pallas kernels  14.8 us (10%)
  other arithmetic  3.72 us (2%)
    all_to_all x2, starting transfers between devices, shards(): lax.all_to_all(piece, 'ka', split_axis=0, concat_axis=2, tiled=True)[0]  28.7 us
    all_to_all x2, waiting for transfers between devices, shards(): lax.all_to_all(piece, 'ka', split_axis=0, concat_axis=2, tiled=True)[0]  26.4 us
    all_to_all x1, starting transfers between devices, shards(): lax.all_to_all(ladder_sum.reshape(vert, slab_width, -1), 'vert', 0, 0, ti...  19.2 us
    pallas_call x2, Pallas kernels, ladder_transposed(): pl.pallas_call(kernel, out_shape=jax.ShapeDtypeStruct((pairs * nv, nv), j...  14.8 us
    all_to_all x1, waiting for transfers between devices, shards(): lax.all_to_all(ladder_sum.reshape(vert, slab_width, -1), 'vert', 0, 0, ti...  11.9 us
    another operation x2, local copies, waits for them, and re-layouts, shards(): right = arrived.reshape(aux_local, virtuals, virtuals)  8.03 us
    squeeze x2, local copies, waits for them, and re-layouts, shards(): ladder_t = ladder_transposed(ct, tt, bq[transfer], ladder_t)  7.08 us
    another operation x4, local copies, waits for them, and re-layouts, trial_transposed(): t = block.reshape(virtuals, pair_count, virtuals)  5.18 us
  transfers between devices with their start and end apart: 4, of which 2 were waited for; matrix products, arithmetic and copies ran while one was open for 17% of the time, Pallas kernels for 0%

profile of v2, /device:TPU:1, one launch (start us, length us, event | category | flops | bytes accessed | tf_op | source)
XLA Modules:
  0.0 150.2 jit_solution(6226282681025674327)
XLA Ops:
  0.0 1.4 select_reduce_fusion.2
  1.6 2.0 %gather_fusion = bf16[64,2,32,196]{3,2,1,0:T(8,128)(2,1)} fusion(bf16[64,2,32,196]{3,2,1,0:T(8,128)(2,1)S(1)} %copy-done, s32[1024]{0:T(1024)S(1)} %pad_clamp_fusion), kind=kCustom, calls=%fused_computation | custom fusion | bytes 3211520 | tf_op jit(solution)/shard_map/gather | solution.py:83
  3.6 3.0 %slice_bitcast_fusion = (bf16[64,32,196]{2,1,0:T(8,128)(2,1)}, bf16[64,32,196]{2,1,0:T(8,128)(2,1)}) fusion(bf16[64,2,32,196]{3,2,1,0:T(8,128)(2,1)} %gather_fusion), kind=kLoop, calls=%fused_computation.1 | loop fusion | bytes 3211264 | tf_op jit(solution)/shard_map/squeeze | solution.py:89
  6.7 19.6 %all-to-all-start.1 = ((bf16[64,32,196]{2,1,0:T(8,128)(2,1)}), bf16[64,32,196]{2,1,0:T(8,128)(2,1)S(1)}, u32[]{:S(2)}, u32[]{:S(2)}) async-start(bf16[64,32,196]{2,1,0:T(8,128)(2,1)} %get-tuple-element.7), calls=%async_computation.1 | async-start | bytes 2097152 | tf_op jit(solution)/shard_map/all_to_all | solution.py:92
  26.3 2.9 %collective-permute-start = (bf16[1,112,896]{2,1,0:T(8,128)(2,1)}, bf16[1,112,896]{2,1,0:T(8,128)(2,1)}, u32[]{:S(2)}, u32[]{:S(2)}) collective-permute-start(bf16[1,112,896]{2,1,0:T(8,128)(2,1)} %param.6), channel_id=1, source_target_pairs={{0,8},{8,16},{16,24},{24,32},{32,40},{40,48},{48,56},{56,64},{64,7... | collective-permute-start | bytes 602120 | tf_op jit(solution)/shard_map/ppermute | solution.py:14
  29.2 26.4 %all-to-all-done.1 = bf16[64,32,196]{2,1,0:T(8,128)(2,1)S(1)} async-done(((bf16[64,32,196]{2,1,0:T(8,128)(2,1)}), bf16[64,32,196]{2,1,0:T(8,128)(2,1)S(1)}, u32[]{:S(2)}, u32[]{:S(2)}) %all-to-all-start.1) | async-done | bytes 802848 | tf_op jit(solution)/shard_map/all_to_all | solution.py:92
  55.5 9.1 %all-to-all-start = ((bf16[64,32,196]{2,1,0:T(8,128)(2,1)}), bf16[64,32,196]{2,1,0:T(8,128)(2,1)}, u32[]{:S(2)}, u32[]{:S(2)}) async-start(bf16[64,32,196]{2,1,0:T(8,128)(2,1)} %get-tuple-element.8), calls=%async_computation | async-start | bytes 2097152 | tf_op jit(solution)/shard_map/all_to_all | solution.py:92
  64.7 2.7 %fusion.1 = (bf16[1,1,32,12544]{3,2,1,0:T(8,128)(2,1)}, bf16[1,1,32,12544]{3,2,1,0:T(8,128)(2,1)}) fusion(bf16[1,2,32,12544]{3,2,1,0:T(8,128)(2,1)} %param.7), kind=kLoop, calls=%fused_computation.15 | loop fusion | bytes 3211264 | tf_op jit(solution)/shard_map/slice | solution.py:98
  67.4 1.2 reshape_squeeze.16
  68.6 3.5 %squeeze.17.b_ref = bf16[32,112,112]{2,1,0:T(8,128)(2,1)} reshape(bf16[1,1,32,12544]{3,2,1,0:T(8,128)(2,1)} %get-tuple-element.9) | data formatting | bytes 1605632 | tf_op jit(solution)/shard_map/squeeze | solution.py:98
  72.1 0.9 copy.23
  73.0 1.0 pad.8
  74.0 0.7 copy.33
  74.8 3.5 %squeeze.15.b_ref = bf16[32,112,112]{2,1,0:T(8,128)(2,1)} reshape(bf16[1,1,32,12544]{3,2,1,0:T(8,128)(2,1)} %get-tuple-element.10) | data formatting | bytes 1605632 | tf_op jit(solution)/shard_map/squeeze | solution.py:98
  78.3 1.9 %reshape_squeeze.14 = bf16[112,8,112]{2,1,0:T(8,128)(2,1)} reshape(bf16[1,112,896]{2,1,0:T(8,128)(2,1)} %collective-permute-done) | data formatting | bytes 401408 | tf_op jit(solution)/shard_map/reshape;squeeze | solution.py:71
  80.2 1.2 copy.20
  81.4 0.7 copy.34
  82.1 1.6 %copy.21 = bf16[1,32,64,196]{3,2,1,0:T(8,128)(2,1)} copy(bf16[1,32,64,196]{3,1,2,0:T(8,128)(2,1)S(1)} %bitcast.42) | data formatting | bytes 1605632 | tf_op jit(solution)/shard_map/all_to_all | solution.py:92
  83.8 4.0 %reshape_squeeze.15 = bf16[32,112,112]{2,1,0:T(8,128)(2,1)} reshape(bf16[1,32,64,196]{3,2,1,0:T(8,128)(2,1)} %copy.21) | data formatting | bytes 1605632 | tf_op jit(solution)/shard_map/reshape;squeeze | solution.py:94
  87.8 1.5 %copy.22 = bf16[32,112,112]{2,1,0:T(8,128)(2,1)S(1)} copy(bf16[32,112,112]{1,2,0:T(8,128)(2,1)} %bitcast.43) | data formatting | bytes 1605632 | tf_op jit(solution)/shard_map/transpose | solution.py:95
  89.3 2.8 %copy.18 = bf16[1,32,64,196]{3,2,1,0:T(8,128)(2,1)} copy(bf16[1,32,64,196]{3,1,2,0:T(8,128)(2,1)} %bitcast.2) | data formatting | bytes 1605632 | tf_op jit(solution)/shard_map/all_to_all | solution.py:92
  92.1 4.0 %reshape_squeeze.13 = bf16[32,112,112]{2,1,0:T(8,128)(2,1)} reshape(bf16[1,32,64,196]{3,2,1,0:T(8,128)(2,1)} %copy.18) | data formatting | bytes 1605632 | tf_op jit(solution)/shard_map/reshape;squeeze | solution.py:94
  96.2 2.2 %copy.19 = bf16[32,112,112]{2,1,0:T(8,128)(2,1)} copy(bf16[32,112,112]{1,2,0:T(8,128)(2,1)} %bitcast.44) | data formatting | bytes 1605632 | tf_op jit(solution)/shard_map/transpose | solution.py:95
  98.4 1.2 copy-done.2
  99.5 0.9 copy-done.4
  100.5 7.4 %shard_map.64.acc_ref = f32[896,112]{1,0:T(8,128)S(1)} custom-call(bf16[3584,112]{1,0:T(8,128)(2,1)S(1)} %bitcast.38, bf16[112,1024]{1,0:T(8,128)(2,1)S(1)} %bitcast.40, bf16[32,112,112]{2,1,0:T(8,128)(2,1)S(1)} %copy-done.2, f32[896,112]{1,0:T(8,128)S(1)} %broadcast_in_dim.33.clone.acc_ref), custom_call_target="tpu_custom_call", output_to_operand_aliasing={{}: (3, {})} | custom-call | flops 1541406720 | bytes 2637824 | tf_op jit(solution)/shard_map/pallas_call | solution.py:47
  107.9 7.4 %shard_map.65 = f32[896,112]{1,0:T(8,128)S(1)} custom-call(bf16[3584,112]{1,0:T(8,128)(2,1)S(1)} %bitcast.39, bf16[112,1024]{1,0:T(8,128)(2,1)S(1)} %bitcast.41, bf16[32,112,112]{2,1,0:T(8,128)(2,1)S(1)} %copy-done.3, f32[896,112]{1,0:T(8,128)S(1)} %shard_map.64.acc_ref), custom_call_target="tpu_custom_call", output_to_operand_aliasing={{}: (3, {})} | custom-call | flops 1541406720 | bytes 2637824 | tf_op jit(solution)/shard_map/pallas_call | solution.py:47
  115.6 0.8 reshape.105
  116.4 19.2 %all-to-all-start.2 = ((f32[8,14,896]{2,1,0:T(8,128)}), f32[8,14,896]{2,1,0:T(8,128)S(1)}, u32[]{:S(2)}, u32[]{:S(2)}) async-start(f32[8,14,896]{2,1,0:T(8,128)} %reshape.105), calls=%async_computation.2 | async-start | bytes 917504 | tf_op jit(solution)/shard_map/all_to_all | solution.py:102
  135.6 0.6 iota_compare_fusion
  136.8 11.9 %all-to-all-done.2 = f32[8,14,896]{2,1,0:T(8,128)S(1)} async-done(((f32[8,14,896]{2,1,0:T(8,128)}), f32[8,14,896]{2,1,0:T(8,128)S(1)}, u32[]{:S(2)}, u32[]{:S(2)}) %all-to-all-start.2) | async-done | bytes 401440 | tf_op jit(solution)/shard_map/all_to_all | solution.py:102
  148.7 1.4 fusion
  (28 shorter events, 1.0 us)
Async XLA Ops:
  0.0 1.6 %copy-start = (bf16[64,2,32,196]{3,2,1,0:T(8,128)(2,1)S(1)}, bf16[64,2,32,196]{3,2,1,0:T(8,128)(2,1)}, u32[]{:S(2)}) copy-start(bf16[64,2,32,196]{3,2,1,0:T(8,128)(2,1)} %param.8) | copy-start | bytes 4816900
  6.7 48.9 %all-to-all-start.1 = ((bf16[64,32,196]{2,1,0:T(8,128)(2,1)}), bf16[64,32,196]{2,1,0:T(8,128)(2,1)S(1)}, u32[]{:S(2)}, u32[]{:S(2)}) async-start(bf16[64,32,196]{2,1,0:T(8,128)(2,1)} %get-tuple-element.7), calls=%async_computation.1 | async-start | bytes 2097152 | tf_op jit(solution)/shard_map/all_to_all | solution.py:92
  26.3 52.0 %collective-permute-start = (bf16[1,112,896]{2,1,0:T(8,128)(2,1)}, bf16[1,112,896]{2,1,0:T(8,128)(2,1)}, u32[]{:S(2)}, u32[]{:S(2)}) collective-permute-start(bf16[1,112,896]{2,1,0:T(8,128)(2,1)} %param.6), channel_id=1, source_target_pairs={{0,8},{8,16},{16,24},{24,32},{32,40},{40,48},{48,56},{56,64},{64,7... | collective-permute-start | bytes 602120 | tf_op jit(solution)/shard_map/ppermute | solution.py:14
  55.5 33.7 %all-to-all-start = ((bf16[64,32,196]{2,1,0:T(8,128)(2,1)}), bf16[64,32,196]{2,1,0:T(8,128)(2,1)}, u32[]{:S(2)}, u32[]{:S(2)}) async-start(bf16[64,32,196]{2,1,0:T(8,128)(2,1)} %get-tuple-element.8), calls=%async_computation | async-start | bytes 2097152 | tf_op jit(solution)/shard_map/all_to_all | solution.py:92
  98.4 1.2 copy-start.2
  99.5 0.9 copy-start.4
  100.5 7.4 %copy-start.1 = (bf16[32,112,112]{2,1,0:T(8,128)(2,1)S(1)}, bf16[32,112,112]{2,1,0:T(8,128)(2,1)}, u32[]{:S(2)}) copy-start(bf16[32,112,112]{2,1,0:T(8,128)(2,1)} %copy.19) | copy-start | bytes 2408452
  100.5 7.4 %copy-start.3 = (bf16[32,112,112]{2,1,0:T(8,128)(2,1)S(1)}, bf16[32,112,112]{2,1,0:T(8,128)(2,1)}, u32[]{:S(2)}) copy-start(bf16[32,112,112]{2,1,0:T(8,128)(2,1)} %squeeze.15.b_ref) | copy-start | bytes 2408452
  100.5 7.4 %copy-start.5 = (bf16[14,8,8,128]{3,1,2,0:T(8,128)(2,1)S(1)}, bf16[14,8,8,128]{3,1,2,0:T(8,128)(2,1)}, u32[]{:S(2)}) copy-start(bf16[14,8,8,128]{3,1,2,0:T(8,128)(2,1)} %copy.34) | copy-start | bytes 688132
  115.4 20.9 %copy-start.6 = (f32[64,112]{1,0:T(8,128)S(1)}, f32[64,112]{1,0:T(8,128)}, u32[]{:S(2)}) copy-start(f32[64,112]{1,0:T(8,128)} %param.10) | copy-start | bytes 86020
  115.4 21.3 %copy-start.7 = (f32[8]{0:T(128)S(1)}, f32[8]{0:T(128)}, u32[]{:S(2)}) copy-start(f32[8]{0:T(128)} %param.11) | copy-start | bytes 100
  116.4 32.3 %all-to-all-start.2 = ((f32[8,14,896]{2,1,0:T(8,128)}), f32[8,14,896]{2,1,0:T(8,128)S(1)}, u32[]{:S(2)}, u32[]{:S(2)}) async-start(f32[8,14,896]{2,1,0:T(8,128)} %reshape.105), calls=%async_computation.2 | async-start | bytes 917504 | tf_op jit(solution)/shard_map/all_to_all | solution.py:102

commit v3 on v2

--- a/solution.py
+++ b/solution.py
@@ -81,27 +81,25 @@
     aux_local = left_factor.shape[2]
     pair_count = trial_vector.shape[2] // virtuals
     ordered = right_factor.at[kb_table].get(mode="promise_in_bounds")
+    flat = ordered.size // kpoints
+    send = ordered.reshape(kpoints, flat // 128, 128)
+    received = lax.all_to_all(send, "ka", split_axis=0, concat_axis=0, tiled=True)
+    arrived = received.reshape(kpoints, transfers, aux_local, -1)
+    arrived = jnp.transpose(arrived, (1, 2, 0, 3)).reshape(transfers, aux_local, virtuals, virtuals)
+    ct_all = jnp.swapaxes(arrived, 2, 3).reshape(transfers, aux_local * virtuals, virtuals)
     own_block = trial_vector[0]
     bq = left_factor[0].reshape(transfers, aux_local, virtuals, virtuals)
     ladder_t = jnp.zeros((pair_count * virtuals, virtuals), jnp.float32)
-    previous = None
     for transfer in range(transfers):
-        piece = ordered[:, transfer]
-        if previous is not None:
-            piece, previous = lax.optimization_barrier((piece, previous))
-        arrived = lax.all_to_all(piece, "ka", split_axis=0, concat_axis=2, tiled=True)[0]
-        previous = arrived
-        right = arrived.reshape(aux_local, virtuals, virtuals)
-        ct = jnp.swapaxes(right, 1, 2).reshape(aux_local * virtuals, virtuals)
         block = own_block if transfer == 0 else shifted(trial_vector, "ka", transfer)[0]
         tt = trial_transposed(block, virtuals, pair_count)
-        ladder_t = ladder_transposed(ct, tt, bq[transfer], ladder_t)
+        ladder_t = ladder_transposed(ct_all[transfer], tt, bq[transfer], ladder_t)
     ladder_sum = ladder_t.T
     vert = lax.axis_size("vert")
     slab_width = virtuals // vert
-    ladder = lax.all_to_all(
-        ladder_sum.reshape(vert, slab_width, -1), "vert", 0, 0, tiled=True
-    ).sum(0)
+    ladder = lax.psum_scatter(
+        ladder_sum.reshape(vert, slab_width, -1), "vert", scatter_dimension=0, tiled=True
+    )[0]
     offset = lax.axis_index("vert") * slab_width
     labels = jnp.arange(kpoints, dtype=jnp.int32)
     owner_index = lax.axis_index("ka")

time: 151 us -> 179 us (1.19); the launches traced: 150 us -> 176 us
  waiting for transfers between devices: 38.3 us -> 70.2 us
  starting transfers between devices: 50.8 us -> 22.7 us
  between operations: 0.18 us -> 13.6 us
  local copies, waits for them, and re-layouts: 42.4 us -> 51 us
    all_to_all x3 -> x1, waiting for transfers between devices: 38.3 us -> 0.01 us  [shards(): lax.all_to_all(send, 'ka', split_axis=0, concat_axis=0, tiled=True)]
    ppermute x1, waiting for transfers between devices: 0.01 us -> 37.3 us  [shifted(): return lax.ppermute(value, axis, pairs)]
    reduce_scatter x0 -> x1, waiting for transfers between devices: none -> 32.9 us  [shards(): lax.psum_scatter(ladder_sum.reshape(vert, slab_width, -1), 'vert', scatte...]
    all_to_all x3 -> x1, starting transfers between devices: 47.9 us -> 19.8 us  [shards(): lax.all_to_all(send, 'ka', split_axis=0, concat_axis=0, tiled=True)]
    reshape x0 -> x3, local copies, waits for them, and re-layouts: none -> 21.5 us  [the longest x1 8.41 us: shards(): arrived = received.reshape(kpoints, transfers, aux_local, -1)]
    another operation x2 -> x0, local copies, waits for them, and re-layouts: 8.03 us -> none  [shards(): right = arrived.reshape(aux_local, virtuals, virtuals)]
    slice x1 -> x4, local copies, waits for them, and re-layouts: 2.71 us -> 7.65 us  [shards(): ladder_t = ladder_transposed(ct_all[transfer], tt, bq[transfer], ladder_t)]
    all_to_all x2 -> x0, local copies, waits for them, and re-layouts: 4.45 us -> none  [shards(): lax.all_to_all(piece, 'ka', split_axis=0, concat_axis=2, tiled=True)[0]]
  transfers between devices with their start and end apart: 4 -> 3, of which waited for: 2 -> 2; matrix products, arithmetic and copies ran while one was open for 17% -> 8% of each run, Pallas kernels for 0% -> 0%
where the time goes in v3:
time: 179 us; the launch traced here: 176 us
  waiting for transfers between devices  70.2 us (39%)
  local copies, waits for them, and re-layouts  51 us (28%)
  starting transfers between devices  22.7 us (13%)
  Pallas kernels  14.8 us (8%)
  between operations  13.6 us (8%)
  other arithmetic  3.72 us (2%)
    ppermute x1, waiting for transfers between devices, shifted(): return lax.ppermute(value, axis, pairs)  37.3 us
    reduce_scatter x1, waiting for transfers between devices, shards(): lax.psum_scatter(ladder_sum.reshape(vert, slab_width, -1), 'vert', scatte...  32.9 us
    all_to_all x1, starting transfers between devices, shards(): lax.all_to_all(send, 'ka', split_axis=0, concat_axis=0, tiled=True)  19.8 us
    pallas_call x2, Pallas kernels, ladder_transposed(): pl.pallas_call(kernel, out_shape=jax.ShapeDtypeStruct((pairs * nv, nv), j...  14.8 us
    reshape x1, local copies, waits for them, and re-layouts, shards(): arrived = received.reshape(kpoints, transfers, aux_local, -1)  8.41 us
    slice x4, local copies, waits for them, and re-layouts, shards(): ladder_t = ladder_transposed(ct_all[transfer], tt, bq[transfer], ladder_t)  7.65 us
    reshape x1, local copies, waits for them, and re-layouts, shards(): send = ordered.reshape(kpoints, flat // 128, 128)  6.96 us
    squeeze x2, local copies, waits for them, and re-layouts, shards(): ladder_t = ladder_transposed(ct_all[transfer], tt, bq[transfer], ladder_t)  6.45 us
  transfers between devices with their start and end apart: 3, of which 2 were waited for; matrix products, arithmetic and copies ran while one was open for 8% of the time, Pallas kernels for 0%

profile of v3, /device:TPU:1, one launch (start us, length us, event | category | flops | bytes accessed | tf_op | source)
XLA Modules:
  0.0 176.0 jit_solution(11324723547262572125)
XLA Ops:
  6.5 1.4 select_reduce_fusion.2
  8.0 0.2 copy-done
  8.1 2.0 %gather_fusion = bf16[64,2,32,196]{3,2,1,0:T(8,128)(2,1)} fusion(bf16[64,2,32,196]{3,2,1,0:T(8,128)(2,1)S(1)} %copy-done, s32[1024]{0:T(1024)S(1)} %pad_clamp_fusion), kind=kCustom, calls=%fused_computation | custom fusion | bytes 3211520 | tf_op jit(solution)/shard_map/gather | solution.py:83
  10.2 7.0 %reshape.105 = bf16[64,98,128]{2,1,0:T(8,128)(2,1)} reshape(bf16[64,2,32,196]{3,2,1,0:T(8,128)(2,1)} %gather_fusion) | data formatting | bytes 3211264 | tf_op jit(solution)/shard_map/reshape | solution.py:85
  17.1 19.8 %all-to-all-start = ((bf16[64,98,128]{2,1,0:T(8,128)(2,1)}), bf16[64,98,128]{2,1,0:T(8,128)(2,1)}, u32[]{:S(2)}, u32[]{:S(2)}) async-start(bf16[64,98,128]{2,1,0:T(8,128)(2,1)} %reshape.105), calls=%async_computation | async-start | bytes 3407872 | tf_op jit(solution)/shard_map/all_to_all | solution.py:86
  37.0 2.9 %collective-permute-start = (bf16[1,112,896]{2,1,0:T(8,128)(2,1)}, bf16[1,112,896]{2,1,0:T(8,128)(2,1)}, u32[]{:S(2)}, u32[]{:S(2)}) collective-permute-start(bf16[1,112,896]{2,1,0:T(8,128)(2,1)} %param.6), channel_id=1, source_target_pairs={{0,8},{8,16},{16,24},{24,32},{32,40},{40,48},{48,56},{56,64},{64,7... | collective-permute-start | bytes 602120 | tf_op jit(solution)/shard_map/ppermute | solution.py:14
  39.8 2.4 %fusion.1 = (bf16[1,1,32,12544]{3,2,1,0:T(8,128)(2,1)}, bf16[1,1,32,12544]{3,2,1,0:T(8,128)(2,1)S(1)}) fusion(bf16[1,2,32,12544]{3,2,1,0:T(8,128)(2,1)} %param.7), kind=kLoop, calls=%fused_computation.13 | loop fusion | bytes 3211264 | tf_op jit(solution)/shard_map/slice | solution.py:96
  42.2 1.2 reshape_squeeze.8
  43.4 3.7 %squeeze.17.b_ref = bf16[32,112,112]{2,1,0:T(8,128)(2,1)} reshape(bf16[1,1,32,12544]{3,2,1,0:T(8,128)(2,1)} %get-tuple-element.9) | data formatting | bytes 1605632 | tf_op jit(solution)/shard_map/squeeze | solution.py:96
  47.1 0.2 copy.28
  47.4 0.7 copy.37
  48.2 2.7 %squeeze.15.b_ref = bf16[32,112,112]{2,1,0:T(8,128)(2,1)} reshape(bf16[1,1,32,12544]{3,2,1,0:T(8,128)(2,1)S(1)} %get-tuple-element.10) | data formatting | bytes 1605632 | tf_op jit(solution)/shard_map/squeeze | solution.py:96
  50.9 37.3 %collective-permute-done = bf16[1,112,896]{2,1,0:T(8,128)(2,1)} collective-permute-done((bf16[1,112,896]{2,1,0:T(8,128)(2,1)}, bf16[1,112,896]{2,1,0:T(8,128)(2,1)}, u32[]{:S(2)}, u32[]{:S(2)}) %collective-permute-start) | collective-permute-done | bytes 200736 | tf_op jit(solution)/shard_map/ppermute | solution.py:14
  88.2 1.2 reshape_squeeze.7
  89.4 0.2 copy.26
  89.7 0.7 copy.38
  90.4 8.4 %reshape.106 = bf16[64,2,32,196]{3,2,1,0:T(8,128)(2,1)} reshape(bf16[64,98,128]{2,1,0:T(8,128)(2,1)} %all-to-all-done) | data formatting | bytes 3211264 | tf_op jit(solution)/shard_map/reshape | solution.py:87
  98.8 4.1 %copy.24 = bf16[2,32,64,196]{3,2,1,0:T(8,128)(2,1)} copy(bf16[2,32,64,196]{3,1,0,2:T(8,128)(2,1)} %bitcast.28) | data formatting | bytes 3211264 | tf_op jit(solution)/shard_map/transpose | solution.py:88
  102.9 6.2 %reshape.107 = bf16[2,32,112,112]{3,2,1,0:T(8,128)(2,1)} reshape(bf16[2,32,64,196]{3,2,1,0:T(8,128)(2,1)} %copy.24) | data formatting | bytes 3211264 | tf_op jit(solution)/shard_map/reshape | solution.py:88
  109.1 2.5 %fusion = (bf16[1,32,112,112]{2,3,1,0:T(8,128)(2,1)S(1)}, bf16[1,32,112,112]{2,3,1,0:T(8,128)(2,1)}) fusion(bf16[2,32,112,112]{2,3,1,0:T(8,128)(2,1)} %bitcast.29), kind=kLoop, calls=%fused_computation.12 | loop fusion | bytes 3211264 | tf_op jit(solution)/shard_map/slice | solution.py:96
  111.6 1.2 copy.27
  112.8 1.5 copy.25
  114.4 1.2 copy-done.1
  115.6 1.2 copy-done.2
  116.8 0.9 copy-done.4
  117.7 7.4 %shard_map.64.acc_ref = f32[896,112]{1,0:T(8,128)S(1)} custom-call(bf16[3584,112]{1,0:T(8,128)(2,1)S(1)} %bitcast.25, bf16[112,1024]{1,0:T(8,128)(2,1)S(1)} %bitcast.26, bf16[32,112,112]{2,1,0:T(8,128)(2,1)S(1)} %copy-done.2, f32[896,112]{1,0:T(8,128)S(1)} %broadcast_in_dim.33.clone.acc_ref), custom_call_target="tpu_custom_call", output_to_operand_aliasing={{}: (3, {})} | custom-call | flops 1541406720 | bytes 2637824 | tf_op jit(solution)/shard_map/pallas_call | solution.py:47
  125.1 7.4 %shard_map.65 = f32[896,112]{1,0:T(8,128)S(1)} custom-call(bf16[3584,112]{1,0:T(8,128)(2,1)S(1)} %bitcast.24, bf16[112,1024]{1,0:T(8,128)(2,1)S(1)} %bitcast.27, bf16[32,112,112]{2,1,0:T(8,128)(2,1)S(1)} %copy-done.3, f32[896,112]{1,0:T(8,128)S(1)} %shard_map.64.acc_ref), custom_call_target="tpu_custom_call", output_to_operand_aliasing={{}: (3, {})} | custom-call | flops 1541406720 | bytes 2637824 | tf_op jit(solution)/shard_map/pallas_call | solution.py:47
  132.6 0.2 copy.30
  132.8 0.8 reshape.110
  133.6 0.7 iota_compare_fusion
  134.8 32.9 %reduce-scatter.2.cloned.1.call-done = f32[1,14,896]{2,1,0:T(8,128)} async-done(((f32[8,14,896]{2,1,0:T(8,128)}), f32[1,14,896]{2,1,0:T(8,128)}) %reduce-scatter.2.cloned.1.call-update) | async-done | bytes 50192 | tf_op jit(solution)/shard_map/reduce_scatter | solution.py:100
  167.7 1.4 add_convert_fusion
  (26 shorter events, 0.7 us)
Async XLA Ops:
  6.5 1.6 copy-start
  17.1 73.3 %all-to-all-start = ((bf16[64,98,128]{2,1,0:T(8,128)(2,1)}), bf16[64,98,128]{2,1,0:T(8,128)(2,1)}, u32[]{:S(2)}, u32[]{:S(2)}) async-start(bf16[64,98,128]{2,1,0:T(8,128)(2,1)} %reshape.105), calls=%async_computation | async-start | bytes 3407872 | tf_op jit(solution)/shard_map/all_to_all | solution.py:86
  36.9 130.8 %reduce-scatter.2.cloned.1.call-start = ((), (), s32[]{:S(2)}) async-start(), calls=%async_computation.2 | async-start | bytes 516096 | tf_op jit(solution)/shard_map/reduce_scatter | solution.py:100
  37.0 51.2 %collective-permute-start = (bf16[1,112,896]{2,1,0:T(8,128)(2,1)}, bf16[1,112,896]{2,1,0:T(8,128)(2,1)}, u32[]{:S(2)}, u32[]{:S(2)}) collective-permute-start(bf16[1,112,896]{2,1,0:T(8,128)(2,1)} %param.6), channel_id=1, source_target_pairs={{0,8},{8,16},{16,24},{24,32},{32,40},{40,48},{48,56},{56,64},{64,7... | collective-permute-start | bytes 602120 | tf_op jit(solution)/shard_map/ppermute | solution.py:14
  114.4 1.2 copy-start.1
  115.6 1.2 copy-start.2
  116.8 0.9 copy-start.4
  117.7 7.4 %copy-start.3 = (bf16[32,112,112]{2,1,0:T(8,128)(2,1)S(1)}, bf16[32,112,112]{2,1,0:T(8,128)(2,1)}, u32[]{:S(2)}) copy-start(bf16[32,112,112]{2,1,0:T(8,128)(2,1)} %squeeze.15.b_ref) | copy-start | bytes 2408452
  117.7 7.4 %copy-start.5 = (bf16[14,8,8,128]{3,1,2,0:T(8,128)(2,1)S(1)}, bf16[14,8,8,128]{3,1,2,0:T(8,128)(2,1)}, u32[]{:S(2)}) copy-start(bf16[14,8,8,128]{3,1,2,0:T(8,128)(2,1)} %copy.38) | copy-start | bytes 688132
  132.6 1.7 copy-start.6
  132.6 2.1 %copy-start.7 = (f32[8]{0:T(128)S(1)}, f32[8]{0:T(128)}, u32[]{:S(2)}) copy-start(f32[8]{0:T(128)} %param.11) | copy-start | bytes 100
Sparse Core Ops, SparseCore 0:
  133.8 33.9 reduce-scatter.1

commit v4 on v2

--- a/solution.py
+++ b/solution.py
@@ -80,18 +80,19 @@
     transfers = left_factor.shape[1]
     aux_local = left_factor.shape[2]
     pair_count = trial_vector.shape[2] // virtuals
-    ordered = right_factor.at[kb_table].get(mode="promise_in_bounds")
     own_block = trial_vector[0]
     bq = left_factor[0].reshape(transfers, aux_local, virtuals, virtuals)
+    arrivals = []
+    for transfer in range(transfers):
+        piece = right_factor[:, transfer].at[kb_table].get(mode="promise_in_bounds")
+        if arrivals:
+            piece, arrivals[-1], bq = lax.optimization_barrier((piece, arrivals[-1], bq))
+        arrivals.append(
+            lax.all_to_all(piece, "ka", split_axis=0, concat_axis=2, tiled=True)[0]
+        )
     ladder_t = jnp.zeros((pair_count * virtuals, virtuals), jnp.float32)
-    previous = None
     for transfer in range(transfers):
-        piece = ordered[:, transfer]
-        if previous is not None:
-            piece, previous = lax.optimization_barrier((piece, previous))
-        arrived = lax.all_to_all(piece, "ka", split_axis=0, concat_axis=2, tiled=True)[0]
-        previous = arrived
-        right = arrived.reshape(aux_local, virtuals, virtuals)
+        right = arrivals[transfer].reshape(aux_local, virtuals, virtuals)
         ct = jnp.swapaxes(right, 1, 2).reshape(aux_local * virtuals, virtuals)
         block = own_block if transfer == 0 else shifted(trial_vector, "ka", transfer)[0]
         tt = trial_transposed(block, virtuals, pair_count)

time: 151 us -> 150 us (level)
  waiting for transfers between devices: 38.3 us -> 66.6 us
  local copies, waits for them, and re-layouts: 42.4 us -> 25.4 us
  starting transfers between devices: 50.8 us -> 39.8 us
    ppermute x1, waiting for transfers between devices: 0.01 us -> 32.5 us  [shifted(): return lax.ppermute(value, axis, pairs)]
    all_to_all x1, starting transfers between devices: 19.2 us -> 8.1 us  [shards(): lax.all_to_all(ladder_sum.reshape(vert, slab_width, -1), 'vert', 0, 0, ti...]
    squeeze x2 -> x1, local copies, waits for them, and re-layouts: 7.08 us -> 1.58 us  [shards(): ladder_t = ladder_transposed(ct, tt, bq[transfer], ladder_t)]
    all_to_all x2, waiting for transfers between devices: 26.4 us -> 22.2 us  [shards(): lax.all_to_all(piece, 'ka', split_axis=0, concat_axis=2, tiled=True)[0]]
    another operation x4, local copies, waits for them, and re-layouts: 5.18 us -> 1 us  [trial_transposed(): t = block.reshape(virtuals, pair_count, virtuals)]
    unnamed x18 -> x8, local copies, waits for them, and re-layouts: 3.76 us -> 0.09 us
    slice x1 -> x0, local copies, waits for them, and re-layouts: 2.71 us -> none  [shards(): ladder_t = ladder_transposed(ct, tt, bq[transfer], ladder_t)]
    all_to_all x2, local copies, waits for them, and re-layouts: 4.45 us -> 2.39 us  [shards(): lax.all_to_all(piece, 'ka', split_axis=0, concat_axis=2, tiled=True)[0]]
  transfers between devices with their start and end apart: 4 -> 4, of which waited for: 2 -> 3; matrix products, arithmetic and copies ran while one was open for 17% -> 9% of each run, Pallas kernels for 0% -> 5%
where the time goes in v4:
time: 150 us
  waiting for transfers between devices  66.6 us (44%)
  starting transfers between devices  39.8 us (27%)
  local copies, waits for them, and re-layouts  25.4 us (17%)
  Pallas kernels  14.9 us (10%)
  other arithmetic  2.79 us (2%)
    ppermute x1, waiting for transfers between devices, shifted(): return lax.ppermute(value, axis, pairs)  32.5 us
    all_to_all x2, starting transfers between devices, shards(): lax.all_to_all(piece, 'ka', split_axis=0, concat_axis=2, tiled=True)[0]  28.7 us
    all_to_all x2, waiting for transfers between devices, shards(): lax.all_to_all(piece, 'ka', split_axis=0, concat_axis=2, tiled=True)[0]  22.2 us
    pallas_call x2, Pallas kernels, ladder_transposed(): pl.pallas_call(kernel, out_shape=jax.ShapeDtypeStruct((pairs * nv, nv), j...  14.9 us
    all_to_all x1, waiting for transfers between devices, shards(): lax.all_to_all(ladder_sum.reshape(vert, slab_width, -1), 'vert', 0, 0, ti...  11.9 us
    all_to_all x1, starting transfers between devices, shards(): lax.all_to_all(ladder_sum.reshape(vert, slab_width, -1), 'vert', 0, 0, ti...  8.1 us
    another operation x1, local copies, waits for them, and re-layouts, shards(): bq = left_factor[0].reshape(transfers, aux_local, virtuals, virtuals)  5.53 us
    gather x2, local copies, waits for them, and re-layouts, shards(): piece = right_factor[:, transfer].at[kb_table].get(mode='promise_in_bounds')  3.18 us
  transfers between devices with their start and end apart: 4, of which 3 were waited for; matrix products, arithmetic and copies ran while one was open for 9% of the time, Pallas kernels for 5%

profile of v4, /device:TPU:1, one launch (start us, length us, event | category | flops | bytes accessed | tf_op | source)
XLA Modules:
  0.0 149.7 jit_solution(5959268910652083093)
XLA Ops:
  0.0 1.3 select_reduce_fusion.2
  1.3 1.7 %slice_bitcast_fusion = (bf16[64,32,196]{2,1,0:T(8,128)(2,1)S(1)}, bf16[64,32,196]{2,1,0:T(8,128)(2,1)S(1)}) fusion(bf16[64,2,32,196]{3,2,1,0:T(8,128)(2,1)} %param.8), kind=kLoop, calls=%fused_computation.2 | loop fusion | bytes 3211264 | tf_op jit(solution)/shard_map/squeeze | solution.py:87
  3.0 1.6 %gather_fusion.1 = bf16[64,32,196]{2,1,0:T(8,128)(2,1)} fusion(bf16[64,32,196]{2,1,0:T(8,128)(2,1)S(1)} %get-tuple-element.13, s32[1024]{0:T(1024)S(1)} %pad_clamp_fusion), kind=kCustom, calls=%fused_computation.1 | custom fusion | bytes 1605888 | tf_op jit(solution)/shard_map/gather | solution.py:87
  4.6 19.6 %all-to-all-start = ((bf16[64,32,196]{2,1,0:T(8,128)(2,1)}), bf16[64,32,196]{2,1,0:T(8,128)(2,1)S(1)}, u32[]{:S(2)}, u32[]{:S(2)}) async-start(bf16[64,32,196]{2,1,0:T(8,128)(2,1)} %gather_fusion.1), calls=%async_computation | async-start | bytes 2097152 | tf_op jit(solution)/shard_map/all_to_all | solution.py:91
  24.2 1.6 %gather_fusion = bf16[64,32,196]{2,1,0:T(8,128)(2,1)} fusion(bf16[64,32,196]{2,1,0:T(8,128)(2,1)S(1)} %get-tuple-element.14, s32[1024]{0:T(1024)S(1)} %pad_clamp_fusion), kind=kCustom, calls=%fused_computation | custom fusion | bytes 1605888 | tf_op jit(solution)/shard_map/gather | solution.py:87
  25.8 5.5 %reshape_squeeze.12 = bf16[2,32,112,112]{3,2,1,0:T(8,128)(2,1)} reshape(bf16[1,2,32,12544]{3,2,1,0:T(8,128)(2,1)} %param.7) | data formatting | bytes 3211264 | tf_op jit(solution)/shard_map/reshape;squeeze | solution.py:84
  31.3 22.1 %all-to-all-done = bf16[64,32,196]{2,1,0:T(8,128)(2,1)S(1)} async-done(((bf16[64,32,196]{2,1,0:T(8,128)(2,1)}), bf16[64,32,196]{2,1,0:T(8,128)(2,1)S(1)}, u32[]{:S(2)}, u32[]{:S(2)}) %all-to-all-start) | async-done | bytes 802848 | tf_op jit(solution)/shard_map/all_to_all | solution.py:91
  53.5 0.6 copy.18
  54.1 1.4 squeeze.18
  55.5 9.2 %all-to-all-start.1 = ((bf16[64,32,196]{2,1,0:T(8,128)(2,1)}), bf16[64,32,196]{2,1,0:T(8,128)(2,1)}, u32[]{:S(2)}, u32[]{:S(2)}) async-start(bf16[64,32,196]{2,1,0:T(8,128)(2,1)} %gather_fusion), calls=%async_computation.1 | async-start | bytes 2097152 | tf_op jit(solution)/shard_map/all_to_all | solution.py:91
  64.7 3.0 %collective-permute-start = (bf16[1,112,896]{2,1,0:T(8,128)(2,1)S(1)}, bf16[1,112,896]{2,1,0:T(8,128)(2,1)S(1)}, u32[]{:S(2)}, u32[]{:S(2)}) collective-permute-start(bf16[1,112,896]{2,1,0:T(8,128)(2,1)S(1)} %copy-done), channel_id=1, source_target_pairs={{0,8},{8,16},{16,24},{24,32},{32,40},{40,48},{48,56},{56,64},{64,7... | collective-permute-start | bytes 602120 | tf_op jit(solution)/shard_map/ppermute | solution.py:14
  67.7 0.3 reshape_squeeze.15
  68.0 0.2 copy.23
  68.3 32.5 %collective-permute-done = bf16[1,112,896]{2,1,0:T(8,128)(2,1)S(1)} collective-permute-done((bf16[1,112,896]{2,1,0:T(8,128)(2,1)S(1)}, bf16[1,112,896]{2,1,0:T(8,128)(2,1)S(1)}, u32[]{:S(2)}, u32[]{:S(2)}) %collective-permute-start) | collective-permute-done | bytes 200736 | tf_op jit(solution)/shard_map/ppermute | solution.py:14
  100.9 0.3 reshape_squeeze.14
  101.1 0.2 copy.21
  101.5 1.8 %reshape.101 = bf16[32,112,112]{2,1,0:T(8,128)(2,1)S(1)} reshape(bf16[32,12544]{1,0:T(8,128)(2,1)S(1)} %squeeze.18) | data formatting | bytes 1605632 | tf_op jit(solution)/shard_map/reshape | solution.py:95
  103.3 0.6 copy.22
  103.9 1.6 %slice_bitcast_fusion.2 = (bf16[32,112,112]{2,1,0:T(8,128)(2,1)S(1)}, bf16[32,112,112]{2,1,0:T(8,128)(2,1)S(1)}) fusion(bf16[2,32,112,112]{3,2,1,0:T(8,128)(2,1)} %reshape_squeeze.12), kind=kLoop, calls=%fused_computation.4 | loop fusion | bytes 3211264 | tf_op jit(solution)/shard_map/squeeze | solution.py:99
  105.5 7.4 %shard_map.64.acc_ref = f32[896,112]{1,0:T(8,128)S(1)} custom-call(bf16[3584,112]{1,0:T(8,128)(2,1)S(1)} %bitcast.40, bf16[112,1024]{1,0:T(8,128)(2,1)S(1)} %bitcast.43, bf16[32,112,112]{2,1,0:T(8,128)(2,1)S(1)} %get-tuple-element.15.b_ref, f32[896,112]{1,0:T(8,128)S(1)} %broadcast_in_dim.34.clone.acc_ref), custom_call_target="tpu_custom_call", output_to_operand_aliasing={{}: (3, {})} | custom-call | flops 1541406720 | bytes 2637824 | tf_op jit(solution)/shard_map/pallas_call | solution.py:47
  112.9 1.8 %copy.19 = bf16[1,32,64,196]{3,2,1,0:T(8,128)(2,1)S(1)} copy(bf16[1,32,64,196]{3,1,2,0:T(8,128)(2,1)} %bitcast.5) | data formatting | bytes 1605632 | tf_op jit(solution)/shard_map/all_to_all | solution.py:91
  114.7 3.1 %reshape_squeeze.13 = bf16[32,112,112]{2,1,0:T(8,128)(2,1)} reshape(bf16[1,32,64,196]{3,2,1,0:T(8,128)(2,1)S(1)} %copy.19) | data formatting | bytes 1605632 | tf_op jit(solution)/shard_map/reshape;squeeze | solution.py:95
  117.9 1.5 %copy.20 = bf16[32,112,112]{2,1,0:T(8,128)(2,1)S(1)} copy(bf16[32,112,112]{1,2,0:T(8,128)(2,1)} %bitcast.46) | data formatting | bytes 1605632 | tf_op jit(solution)/shard_map/transpose | solution.py:96
  119.4 7.4 %shard_map.65 = f32[896,112]{1,0:T(8,128)S(1)} custom-call(bf16[3584,112]{1,0:T(8,128)(2,1)S(1)} %bitcast.41, bf16[112,1024]{1,0:T(8,128)(2,1)S(1)} %bitcast.42, bf16[32,112,112]{2,1,0:T(8,128)(2,1)S(1)} %get-tuple-element.16.b_ref, f32[896,112]{1,0:T(8,128)S(1)} %shard_map.64.acc_ref), custom_call_target="tpu_custom_call", output_to_operand_aliasing={{}: (3, {})} | custom-call | flops 1541406720 | bytes 2637824 | tf_op jit(solution)/shard_map/pallas_call | solution.py:47
  126.8 0.2 copy.25
  127.0 0.8 reshape.104
  127.9 8.1 %all-to-all-start.2 = ((f32[8,14,896]{2,1,0:T(8,128)}), f32[8,14,896]{2,1,0:T(8,128)S(1)}, u32[]{:S(2)}, u32[]{:S(2)}) async-start(f32[8,14,896]{2,1,0:T(8,128)} %reshape.104), calls=%async_computation.2 | async-start | bytes 917504 | tf_op jit(solution)/shard_map/all_to_all | solution.py:103
  136.0 0.6 iota_compare_fusion
  136.6 0.1 select_reduce_fusion.1
  136.9 0.1 sub.28
  137.1 11.9 %all-to-all-done.2 = f32[8,14,896]{2,1,0:T(8,128)S(1)} async-done(((f32[8,14,896]{2,1,0:T(8,128)}), f32[8,14,896]{2,1,0:T(8,128)S(1)}, u32[]{:S(2)}, u32[]{:S(2)}) %all-to-all-start.2) | async-done | bytes 401440 | tf_op jit(solution)/shard_map/all_to_all | solution.py:103
  149.1 0.6 fusion
  (20 shorter events, 0.6 us)
Async XLA Ops:
  4.6 48.9 %all-to-all-start = ((bf16[64,32,196]{2,1,0:T(8,128)(2,1)}), bf16[64,32,196]{2,1,0:T(8,128)(2,1)S(1)}, u32[]{:S(2)}, u32[]{:S(2)}) async-start(bf16[64,32,196]{2,1,0:T(8,128)(2,1)} %gather_fusion.1), calls=%async_computation | async-start | bytes 2097152 | tf_op jit(solution)/shard_map/all_to_all | solution.py:91
  54.1 10.6 %copy-start = (bf16[1,112,896]{2,1,0:T(8,128)(2,1)S(1)}, bf16[1,112,896]{2,1,0:T(8,128)(2,1)}, u32[]{:S(2)}) copy-start(bf16[1,112,896]{2,1,0:T(8,128)(2,1)} %param.6) | copy-start | bytes 602116
  55.5 57.4 %all-to-all-start.1 = ((bf16[64,32,196]{2,1,0:T(8,128)(2,1)}), bf16[64,32,196]{2,1,0:T(8,128)(2,1)}, u32[]{:S(2)}, u32[]{:S(2)}) async-start(bf16[64,32,196]{2,1,0:T(8,128)(2,1)} %gather_fusion), calls=%async_computation.1 | async-start | bytes 2097152 | tf_op jit(solution)/shard_map/all_to_all | solution.py:91
  64.7 36.2 %collective-permute-start = (bf16[1,112,896]{2,1,0:T(8,128)(2,1)S(1)}, bf16[1,112,896]{2,1,0:T(8,128)(2,1)S(1)}, u32[]{:S(2)}, u32[]{:S(2)}) collective-permute-start(bf16[1,112,896]{2,1,0:T(8,128)(2,1)S(1)} %copy-done), channel_id=1, source_target_pairs={{0,8},{8,16},{16,24},{24,32},{32,40},{40,48},{48,56},{56,64},{64,7... | collective-permute-start | bytes 602120 | tf_op jit(solution)/shard_map/ppermute | solution.py:14
  126.8 9.8 %copy-start.1 = (f32[64,112]{1,0:T(8,128)S(1)}, f32[64,112]{1,0:T(8,128)}, u32[]{:S(2)}) copy-start(f32[64,112]{1,0:T(8,128)} %param.10) | copy-start | bytes 86020
  126.8 10.2 %copy-start.2 = (f32[8]{0:T(128)S(1)}, f32[8]{0:T(128)}, u32[]{:S(2)}) copy-start(f32[8]{0:T(128)} %param.11) | copy-start | bytes 100
  127.9 21.2 %all-to-all-start.2 = ((f32[8,14,896]{2,1,0:T(8,128)}), f32[8,14,896]{2,1,0:T(8,128)S(1)}, u32[]{:S(2)}, u32[]{:S(2)}) async-start(f32[8,14,896]{2,1,0:T(8,128)} %reshape.104), calls=%async_computation.2 | async-start | bytes 917504 | tf_op jit(solution)/shard_map/all_to_all | solution.py:103

commit v5 on v4

--- a/solution.py
+++ b/solution.py
@@ -82,11 +82,16 @@
     pair_count = trial_vector.shape[2] // virtuals
     own_block = trial_vector[0]
     bq = left_factor[0].reshape(transfers, aux_local, virtuals, virtuals)
+    blocks = [own_block] + [
+        shifted(trial_vector, "ka", transfer)[0] for transfer in range(1, transfers)
+    ]
     arrivals = []
     for transfer in range(transfers):
         piece = right_factor[:, transfer].at[kb_table].get(mode="promise_in_bounds")
         if arrivals:
-            piece, arrivals[-1], bq = lax.optimization_barrier((piece, arrivals[-1], bq))
+            piece, arrivals[-1], bq, blocks = lax.optimization_barrier(
+                (piece, arrivals[-1], bq, blocks)
+            )
         arrivals.append(
             lax.all_to_all(piece, "ka", split_axis=0, concat_axis=2, tiled=True)[0]
         )
@@ -94,8 +99,7 @@
     for transfer in range(transfers):
         right = arrivals[transfer].reshape(aux_local, virtuals, virtuals)
         ct = jnp.swapaxes(right, 1, 2).reshape(aux_local * virtuals, virtuals)
-        block = own_block if transfer == 0 else shifted(trial_vector, "ka", transfer)[0]
-        tt = trial_transposed(block, virtuals, pair_count)
+        tt = trial_transposed(blocks[transfer], virtuals, pair_count)
         ladder_t = ladder_transposed(ct, tt, bq[transfer], ladder_t)
     ladder_sum = ladder_t.T
     vert = lax.axis_size("vert")
@@ -110,7 +114,7 @@
     energy_rows = jnp.sum(jnp.where((labels == owner_index)[:, None], vir_energy, 0.0), axis=0)
     energy_other = jnp.sum(jnp.where((labels == momentum_b)[:, None], vir_energy, 0.0), axis=0)
     energy_a = lax.dynamic_slice_in_dim(energy_rows, offset, slab_width, 0)
-    own_rows = lax.dynamic_slice_in_dim(own_block, offset, slab_width, 0).astype(jnp.float32)
+    own_rows = lax.dynamic_slice_in_dim(blocks[0], offset, slab_width, 0).astype(jnp.float32)
     own_rows = own_rows.reshape(slab_width, pair_count, virtuals)
     shift_energy = (
         energy_a[:, None, None] + energy_other[None, None, :] - pair_energy[None, :, None]

time: 150 us -> 138 us (0.920)
  waiting for transfers between devices: 66.6 us -> 51.3 us
  starting transfers between devices: 39.8 us -> 42.6 us
    ppermute x1, waiting for transfers between devices: 32.5 us -> 6.31 us  [shifted(): return lax.ppermute(value, axis, pairs)]
    all_to_all x2, waiting for transfers between devices: 22.2 us -> 33.1 us  [shards(): lax.all_to_all(piece, 'ka', split_axis=0, concat_axis=2, tiled=True)[0]]
    all_to_all x1, starting transfers between devices: 8.1 us -> 12.1 us  [shards(): lax.all_to_all(ladder_sum.reshape(vert, slab_width, -1), 'vert', 0, 0, ti...]
  transfers between devices with their start and end apart: 4 -> 4, of which waited for: 3 -> 4; matrix products, arithmetic and copies ran while one was open for 9% -> 11% of each run, Pallas kernels for 5% -> 5%
where the time goes in v5:
time: 138 us; the launch traced here: 137 us
  waiting for transfers between devices  51.3 us (37%)
  starting transfers between devices  42.6 us (31%)
  local copies, waits for them, and re-layouts  25.4 us (18%)
  Pallas kernels  14.9 us (11%)
  other arithmetic  2.92 us (2%)
    all_to_all x2, waiting for transfers between devices, shards(): lax.all_to_all(piece, 'ka', split_axis=0, concat_axis=2, tiled=True)[0]  33.1 us
    all_to_all x2, starting transfers between devices, shards(): lax.all_to_all(piece, 'ka', split_axis=0, concat_axis=2, tiled=True)[0]  27.6 us
    pallas_call x2, Pallas kernels, ladder_transposed(): pl.pallas_call(kernel, out_shape=jax.ShapeDtypeStruct((pairs * nv, nv), j...  14.9 us
    all_to_all x1, starting transfers between devices, shards(): lax.all_to_all(ladder_sum.reshape(vert, slab_width, -1), 'vert', 0, 0, ti...  12.1 us
    all_to_all x1, waiting for transfers between devices, shards(): lax.all_to_all(ladder_sum.reshape(vert, slab_width, -1), 'vert', 0, 0, ti...  11.9 us
    ppermute x1, waiting for transfers between devices, shifted(): return lax.ppermute(value, axis, pairs)  6.31 us
    another operation x1, local copies, waits for them, and re-layouts, shards(): bq = left_factor[0].reshape(transfers, aux_local, virtuals, virtuals)  5.52 us
    gather x2, local copies, waits for them, and re-layouts, shards(): piece = right_factor[:, transfer].at[kb_table].get(mode='promise_in_bounds')  3.18 us
  transfers between devices with their start and end apart: 4, of which 4 were waited for; matrix products, arithmetic and copies ran while one was open for 11% of the time, Pallas kernels for 5%

profile of v5, /device:TPU:1, one launch (start us, length us, event | category | flops | bytes accessed | tf_op | source)
XLA Modules:
  0.0 137.3 jit_solution(2052625472343779424)
XLA Ops:
  0.0 1.7 %slice_bitcast_fusion = (bf16[64,32,196]{2,1,0:T(8,128)(2,1)S(1)}, bf16[64,32,196]{2,1,0:T(8,128)(2,1)S(1)}) fusion(bf16[64,2,32,196]{3,2,1,0:T(8,128)(2,1)} %param.8), kind=kLoop, calls=%fused_computation.2 | loop fusion | bytes 3211264 | tf_op jit(solution)/shard_map/squeeze | solution.py:90
  1.8 0.6 select_reduce_fusion.2
  2.4 1.6 %gather_fusion.1 = bf16[64,32,196]{2,1,0:T(8,128)(2,1)} fusion(bf16[64,32,196]{2,1,0:T(8,128)(2,1)S(1)} %get-tuple-element.17, s32[1024]{0:T(1024)S(1)} %pad_clamp_fusion), kind=kCustom, calls=%fused_computation.1 | custom fusion | bytes 1605888 | tf_op jit(solution)/shard_map/gather | solution.py:90
  4.0 19.6 %all-to-all-start = ((bf16[64,32,196]{2,1,0:T(8,128)(2,1)}), bf16[64,32,196]{2,1,0:T(8,128)(2,1)S(1)}, u32[]{:S(2)}, u32[]{:S(2)}) async-start(bf16[64,32,196]{2,1,0:T(8,128)(2,1)} %gather_fusion.1), calls=%async_computation | async-start | bytes 2097152 | tf_op jit(solution)/shard_map/all_to_all | solution.py:96
  23.6 2.9 %collective-permute-start = (bf16[1,112,896]{2,1,0:T(8,128)(2,1)S(1)}, bf16[1,112,896]{2,1,0:T(8,128)(2,1)S(1)}, u32[]{:S(2)}, u32[]{:S(2)}) collective-permute-start(bf16[1,112,896]{2,1,0:T(8,128)(2,1)S(1)} %copy-done), channel_id=1, source_target_pairs={{0,8},{8,16},{16,24},{24,32},{32,40},{40,48},{48,56},{56,64},{64,7... | collective-permute-start | bytes 602120 | tf_op jit(solution)/shard_map/ppermute | solution.py:14
  26.5 1.6 %gather_fusion = bf16[64,32,196]{2,1,0:T(8,128)(2,1)} fusion(bf16[64,32,196]{2,1,0:T(8,128)(2,1)S(1)} %get-tuple-element.18, s32[1024]{0:T(1024)S(1)} %pad_clamp_fusion), kind=kCustom, calls=%fused_computation | custom fusion | bytes 1605888 | tf_op jit(solution)/shard_map/gather | solution.py:90
  28.1 5.5 %reshape_squeeze.6 = bf16[2,32,112,112]{3,2,1,0:T(8,128)(2,1)} reshape(bf16[1,2,32,12544]{3,2,1,0:T(8,128)(2,1)} %param.7) | data formatting | bytes 3211264 | tf_op jit(solution)/shard_map/reshape;squeeze | solution.py:84
  33.6 19.2 %all-to-all-done = bf16[64,32,196]{2,1,0:T(8,128)(2,1)S(1)} async-done(((bf16[64,32,196]{2,1,0:T(8,128)(2,1)}), bf16[64,32,196]{2,1,0:T(8,128)(2,1)S(1)}, u32[]{:S(2)}, u32[]{:S(2)}) %all-to-all-start) | async-done | bytes 802848 | tf_op jit(solution)/shard_map/all_to_all | solution.py:96
  52.8 0.6 copy.18
  53.4 1.4 %squeeze.23 = bf16[32,12544]{1,0:T(8,128)(2,1)S(1)} reshape(bf16[1,32,64,196]{3,2,1,0:T(8,128)(2,1)S(1)} %copy.18) | data formatting | bytes 1605632 | tf_op jit(solution)/shard_map/squeeze | solution.py:96
  54.9 6.3 %collective-permute-done = bf16[1,112,896]{2,1,0:T(8,128)(2,1)S(1)} collective-permute-done((bf16[1,112,896]{2,1,0:T(8,128)(2,1)S(1)}, bf16[1,112,896]{2,1,0:T(8,128)(2,1)S(1)}, u32[]{:S(2)}, u32[]{:S(2)}) %collective-permute-start) | collective-permute-done | bytes 200736 | tf_op jit(solution)/shard_map/ppermute | solution.py:14
  61.2 8.0 %all-to-all-start.1 = ((bf16[64,32,196]{2,1,0:T(8,128)(2,1)}), bf16[64,32,196]{2,1,0:T(8,128)(2,1)}, u32[]{:S(2)}, u32[]{:S(2)}) async-start(bf16[64,32,196]{2,1,0:T(8,128)(2,1)} %gather_fusion), calls=%async_computation.1 | async-start | bytes 2097152 | tf_op jit(solution)/shard_map/all_to_all | solution.py:96
  69.2 0.3 reshape.68
  69.5 0.2 copy.21
  69.8 1.8 %reshape.70 = bf16[32,112,112]{2,1,0:T(8,128)(2,1)S(1)} reshape(bf16[32,12544]{1,0:T(8,128)(2,1)S(1)} %squeeze.23) | data formatting | bytes 1605632 | tf_op jit(solution)/shard_map/reshape | solution.py:100
  71.6 0.6 copy.22
  72.2 0.3 reshape.72
  72.5 0.2 copy.23
  72.8 1.6 %slice_bitcast_fusion.2 = (bf16[32,112,112]{2,1,0:T(8,128)(2,1)S(1)}, bf16[32,112,112]{2,1,0:T(8,128)(2,1)S(1)}) fusion(bf16[2,32,112,112]{3,2,1,0:T(8,128)(2,1)} %reshape_squeeze.6), kind=kLoop, calls=%fused_computation.4 | loop fusion | bytes 3211264 | tf_op jit(solution)/shard_map/squeeze | solution.py:103
  74.4 7.4 %shard_map.64.acc_ref = f32[896,112]{1,0:T(8,128)S(1)} custom-call(bf16[3584,112]{1,0:T(8,128)(2,1)S(1)} %bitcast.40, bf16[112,1024]{1,0:T(8,128)(2,1)S(1)} %bitcast.43, bf16[32,112,112]{2,1,0:T(8,128)(2,1)S(1)} %get-tuple-element.19.b_ref, f32[896,112]{1,0:T(8,128)S(1)} %broadcast_in_dim.36.clone.acc_ref), custom_call_target="tpu_custom_call", output_to_operand_aliasing={{}: (3, {})} | custom-call | flops 1541406720 | bytes 2637824 | tf_op jit(solution)/shard_map/pallas_call | solution.py:47
  81.9 13.8 %all-to-all-done.1 = bf16[64,32,196]{2,1,0:T(8,128)(2,1)} async-done(((bf16[64,32,196]{2,1,0:T(8,128)(2,1)}), bf16[64,32,196]{2,1,0:T(8,128)(2,1)}, u32[]{:S(2)}, u32[]{:S(2)}) %all-to-all-start.1) | async-done | bytes 802848 | tf_op jit(solution)/shard_map/all_to_all | solution.py:96
  95.7 1.8 %copy.19 = bf16[1,32,64,196]{3,2,1,0:T(8,128)(2,1)S(1)} copy(bf16[1,32,64,196]{3,1,2,0:T(8,128)(2,1)} %bitcast.7) | data formatting | bytes 1605632 | tf_op jit(solution)/shard_map/all_to_all | solution.py:96
  97.5 3.1 %reshape_squeeze.7 = bf16[32,112,112]{2,1,0:T(8,128)(2,1)} reshape(bf16[1,32,64,196]{3,2,1,0:T(8,128)(2,1)S(1)} %copy.19) | data formatting | bytes 1605632 | tf_op jit(solution)/shard_map/reshape;squeeze | solution.py:100
  100.7 1.5 %copy.20 = bf16[32,112,112]{2,1,0:T(8,128)(2,1)S(1)} copy(bf16[32,112,112]{1,2,0:T(8,128)(2,1)} %bitcast.46) | data formatting | bytes 1605632 | tf_op jit(solution)/shard_map/transpose | solution.py:101
  102.2 7.4 %shard_map.65 = f32[896,112]{1,0:T(8,128)S(1)} custom-call(bf16[3584,112]{1,0:T(8,128)(2,1)S(1)} %bitcast.41, bf16[112,1024]{1,0:T(8,128)(2,1)S(1)} %bitcast.42, bf16[32,112,112]{2,1,0:T(8,128)(2,1)S(1)} %get-tuple-element.20.b_ref, f32[896,112]{1,0:T(8,128)S(1)} %shard_map.64.acc_ref), custom_call_target="tpu_custom_call", output_to_operand_aliasing={{}: (3, {})} | custom-call | flops 1541406720 | bytes 2637824 | tf_op jit(solution)/shard_map/pallas_call | solution.py:47
  109.6 0.2 copy.25
  109.8 0.8 reshape.74
  110.7 12.1 %all-to-all-start.2 = ((f32[8,14,896]{2,1,0:T(8,128)}), f32[8,14,896]{2,1,0:T(8,128)S(1)}, u32[]{:S(2)}, u32[]{:S(2)}) async-start(f32[8,14,896]{2,1,0:T(8,128)} %reshape.74), calls=%async_computation.2 | async-start | bytes 917504 | tf_op jit(solution)/shard_map/all_to_all | solution.py:107
  122.8 0.6 iota_compare_fusion
  123.5 0.1 select_reduce_fusion.1
  124.0 11.9 %all-to-all-done.2 = f32[8,14,896]{2,1,0:T(8,128)S(1)} async-done(((f32[8,14,896]{2,1,0:T(8,128)}), f32[8,14,896]{2,1,0:T(8,128)S(1)}, u32[]{:S(2)}, u32[]{:S(2)}) %all-to-all-start.2) | async-done | bytes 401440 | tf_op jit(solution)/shard_map/all_to_all | solution.py:107
  135.9 1.4 %fusion = bf16[1,14,896]{2,1,0:T(8,128)(2,1)} fusion(f32[14,896]{1,0:T(8,128)S(1)} %reduce_sum.36, f32[14,896]{1,0:T(8,128)S(1)} %sub.21, bf16[112,896]{1,0:T(8,128)(2,1)} %bitcast.51, s32[]{:T(128)S(6)} %select_n.21, f32[896]{0:T(1024)S(1)} %sub.23), kind=kLoop, calls=%fused_computation.11 | loop fusion | flops 62720 | bytes 154116 | tf_op jit(solution)/shard_map/broadcast_in_dim | solution.py:123
  (24 shorter events, 0.7 us)
Async XLA Ops:
  0.0 1.7 %copy-start.4 = (s32[64]{0:T(128)S(1)}, s32[64]{0:T(128)}, u32[]{:S(2)}) copy-start(s32[64]{0:T(128)} %param.9) | copy-start | bytes 772
  2.4 21.2 %copy-start = (bf16[1,112,896]{2,1,0:T(8,128)(2,1)S(1)}, bf16[1,112,896]{2,1,0:T(8,128)(2,1)}, u32[]{:S(2)}) copy-start(bf16[1,112,896]{2,1,0:T(8,128)(2,1)} %param.6) | copy-start | bytes 602116
  4.0 48.9 %all-to-all-start = ((bf16[64,32,196]{2,1,0:T(8,128)(2,1)}), bf16[64,32,196]{2,1,0:T(8,128)(2,1)S(1)}, u32[]{:S(2)}, u32[]{:S(2)}) async-start(bf16[64,32,196]{2,1,0:T(8,128)(2,1)} %gather_fusion.1), calls=%async_computation | async-start | bytes 2097152 | tf_op jit(solution)/shard_map/all_to_all | solution.py:96
  23.6 37.6 %collective-permute-start = (bf16[1,112,896]{2,1,0:T(8,128)(2,1)S(1)}, bf16[1,112,896]{2,1,0:T(8,128)(2,1)S(1)}, u32[]{:S(2)}, u32[]{:S(2)}) collective-permute-start(bf16[1,112,896]{2,1,0:T(8,128)(2,1)S(1)} %copy-done), channel_id=1, source_target_pairs={{0,8},{8,16},{16,24},{24,32},{32,40},{40,48},{48,56},{56,64},{64,7... | collective-permute-start | bytes 602120 | tf_op jit(solution)/shard_map/ppermute | solution.py:14
  61.2 34.5 %all-to-all-start.1 = ((bf16[64,32,196]{2,1,0:T(8,128)(2,1)}), bf16[64,32,196]{2,1,0:T(8,128)(2,1)}, u32[]{:S(2)}, u32[]{:S(2)}) async-start(bf16[64,32,196]{2,1,0:T(8,128)(2,1)} %gather_fusion), calls=%async_computation.1 | async-start | bytes 2097152 | tf_op jit(solution)/shard_map/all_to_all | solution.py:96
  69.8 2.4 %copy-start.1 = (bf16[1,112,896]{2,1,0:T(8,128)(2,1)S(1)}, bf16[1,112,896]{2,1,0:T(8,128)(2,1)}, u32[]{:S(2)}) copy-start(bf16[1,112,896]{2,1,0:T(8,128)(2,1)} %param.6) | copy-start | bytes 602116
  109.6 13.8 %copy-start.2 = (f32[64,112]{1,0:T(8,128)S(1)}, f32[64,112]{1,0:T(8,128)}, u32[]{:S(2)}) copy-start(f32[64,112]{1,0:T(8,128)} %param.10) | copy-start | bytes 86020
  109.6 14.2 %copy-start.3 = (f32[8]{0:T(128)S(1)}, f32[8]{0:T(128)}, u32[]{:S(2)}) copy-start(f32[8]{0:T(128)} %param.11) | copy-start | bytes 100
  110.7 25.2 %all-to-all-start.2 = ((f32[8,14,896]{2,1,0:T(8,128)}), f32[8,14,896]{2,1,0:T(8,128)S(1)}, u32[]{:S(2)}, u32[]{:S(2)}) async-start(f32[8,14,896]{2,1,0:T(8,128)} %reshape.74), calls=%async_computation.2 | async-start | bytes 917504 | tf_op jit(solution)/shard_map/all_to_all | solution.py:107

commit v6 on v4

--- a/solution.py
+++ b/solution.py
@@ -91,10 +91,15 @@
             lax.all_to_all(piece, "ka", split_axis=0, concat_axis=2, tiled=True)[0]
         )
     ladder_t = jnp.zeros((pair_count * virtuals, virtuals), jnp.float32)
+    trial_now = trial_vector
     for transfer in range(transfers):
         right = arrivals[transfer].reshape(aux_local, virtuals, virtuals)
         ct = jnp.swapaxes(right, 1, 2).reshape(aux_local * virtuals, virtuals)
-        block = own_block if transfer == 0 else shifted(trial_vector, "ka", transfer)[0]
+        if transfer == 0:
+            block = own_block
+        else:
+            trial_now, ladder_t = lax.optimization_barrier((trial_now, ladder_t))
+            block = shifted(trial_now, "ka", transfer)[0]
         tt = trial_transposed(block, virtuals, pair_count)
         ladder_t = ladder_transposed(ct, tt, bq[transfer], ladder_t)
     ladder_sum = ladder_t.T

time: 150 us -> 139 us (0.927)
  waiting for transfers between devices: 66.6 us -> 55.1 us
    ppermute x1, waiting for transfers between devices: 32.5 us -> 21 us  [shifted(): return lax.ppermute(value, axis, pairs)]
  transfers between devices with their start and end apart: 4 -> 4, of which waited for: 3 -> 3; matrix products, arithmetic and copies ran while one was open for 9% -> 10% of each run, Pallas kernels for 5% -> 5%
where the time goes in v6:
time: 139 us; the launch traced here: 138 us
  waiting for transfers between devices  55.1 us (40%)
  starting transfers between devices  40 us (29%)
  local copies, waits for them, and re-layouts  25.4 us (18%)
  Pallas kernels  14.9 us (11%)
  other arithmetic  2.79 us (2%)
    all_to_all x2, starting transfers between devices, shards(): lax.all_to_all(piece, 'ka', split_axis=0, concat_axis=2, tiled=True)[0]  28.7 us
    all_to_all x2, waiting for transfers between devices, shards(): lax.all_to_all(piece, 'ka', split_axis=0, concat_axis=2, tiled=True)[0]  22.2 us
    ppermute x1, waiting for transfers between devices, shifted(): return lax.ppermute(value, axis, pairs)  21 us
    pallas_call x2, Pallas kernels, ladder_transposed(): pl.pallas_call(kernel, out_shape=jax.ShapeDtypeStruct((pairs * nv, nv), j...  14.9 us
    all_to_all x1, waiting for transfers between devices, shards(): lax.all_to_all(ladder_sum.reshape(vert, slab_width, -1), 'vert', 0, 0, ti...  11.9 us
    all_to_all x1, starting transfers between devices, shards(): lax.all_to_all(ladder_sum.reshape(vert, slab_width, -1), 'vert', 0, 0, ti...  8.24 us
    another operation x1, local copies, waits for them, and re-layouts, shards(): bq = left_factor[0].reshape(transfers, aux_local, virtuals, virtuals)  5.52 us
    gather x2, local copies, waits for them, and re-layouts, shards(): piece = right_factor[:, transfer].at[kb_table].get(mode='promise_in_bounds')  3.17 us
  transfers between devices with their start and end apart: 4, of which 3 were waited for; matrix products, arithmetic and copies ran while one was open for 10% of the time, Pallas kernels for 5%

profile of v6, /device:TPU:1, one launch (start us, length us, event | category | flops | bytes accessed | tf_op | source)
XLA Modules:
  0.0 138.4 jit_solution(7044467847806217267)
XLA Ops:
  0.0 1.3 select_reduce_fusion.2
  1.3 1.7 %slice_bitcast_fusion = (bf16[64,32,196]{2,1,0:T(8,128)(2,1)S(1)}, bf16[64,32,196]{2,1,0:T(8,128)(2,1)S(1)}) fusion(bf16[64,2,32,196]{3,2,1,0:T(8,128)(2,1)} %param.8), kind=kLoop, calls=%fused_computation.2 | loop fusion | bytes 3211264 | tf_op jit(solution)/shard_map/squeeze | solution.py:87
  3.0 1.6 %gather_fusion.1 = bf16[64,32,196]{2,1,0:T(8,128)(2,1)} fusion(bf16[64,32,196]{2,1,0:T(8,128)(2,1)S(1)} %get-tuple-element.17, s32[1024]{0:T(1024)S(1)} %pad_clamp_fusion), kind=kCustom, calls=%fused_computation.1 | custom fusion | bytes 1605888 | tf_op jit(solution)/shard_map/gather | solution.py:87
  4.6 19.6 %all-to-all-start = ((bf16[64,32,196]{2,1,0:T(8,128)(2,1)}), bf16[64,32,196]{2,1,0:T(8,128)(2,1)S(1)}, u32[]{:S(2)}, u32[]{:S(2)}) async-start(bf16[64,32,196]{2,1,0:T(8,128)(2,1)} %gather_fusion.1), calls=%async_computation | async-start | bytes 2097152 | tf_op jit(solution)/shard_map/all_to_all | solution.py:91
  24.2 1.6 %gather_fusion = bf16[64,32,196]{2,1,0:T(8,128)(2,1)} fusion(bf16[64,32,196]{2,1,0:T(8,128)(2,1)S(1)} %get-tuple-element.18, s32[1024]{0:T(1024)S(1)} %pad_clamp_fusion), kind=kCustom, calls=%fused_computation | custom fusion | bytes 1605888 | tf_op jit(solution)/shard_map/gather | solution.py:87
  25.8 5.5 %reshape_squeeze.12 = bf16[2,32,112,112]{3,2,1,0:T(8,128)(2,1)} reshape(bf16[1,2,32,12544]{3,2,1,0:T(8,128)(2,1)} %param.7) | data formatting | bytes 3211264 | tf_op jit(solution)/shard_map/reshape;squeeze | solution.py:84
  31.3 22.2 %all-to-all-done = bf16[64,32,196]{2,1,0:T(8,128)(2,1)S(1)} async-done(((bf16[64,32,196]{2,1,0:T(8,128)(2,1)}), bf16[64,32,196]{2,1,0:T(8,128)(2,1)S(1)}, u32[]{:S(2)}, u32[]{:S(2)}) %all-to-all-start) | async-done | bytes 802848 | tf_op jit(solution)/shard_map/all_to_all | solution.py:91
  53.5 0.6 copy.18
  54.1 1.4 %squeeze.18 = bf16[32,12544]{1,0:T(8,128)(2,1)S(1)} reshape(bf16[1,32,64,196]{3,2,1,0:T(8,128)(2,1)S(1)} %copy.18) | data formatting | bytes 1605632 | tf_op jit(solution)/shard_map/squeeze | solution.py:91
  55.5 9.2 %all-to-all-start.1 = ((bf16[64,32,196]{2,1,0:T(8,128)(2,1)}), bf16[64,32,196]{2,1,0:T(8,128)(2,1)}, u32[]{:S(2)}, u32[]{:S(2)}) async-start(bf16[64,32,196]{2,1,0:T(8,128)(2,1)} %gather_fusion), calls=%async_computation.1 | async-start | bytes 2097152 | tf_op jit(solution)/shard_map/all_to_all | solution.py:91
  64.7 0.3 reshape_squeeze.14
  65.0 0.2 copy.22
  65.3 1.8 %reshape.100 = bf16[32,112,112]{2,1,0:T(8,128)(2,1)S(1)} reshape(bf16[32,12544]{1,0:T(8,128)(2,1)S(1)} %squeeze.18) | data formatting | bytes 1605632 | tf_op jit(solution)/shard_map/reshape | solution.py:96
  67.1 0.6 copy.21
  67.7 1.6 %slice_bitcast_fusion.2 = (bf16[32,112,112]{2,1,0:T(8,128)(2,1)S(1)}, bf16[32,112,112]{2,1,0:T(8,128)(2,1)S(1)}) fusion(bf16[2,32,112,112]{3,2,1,0:T(8,128)(2,1)} %reshape_squeeze.12), kind=kLoop, calls=%fused_computation.4 | loop fusion | bytes 3211264 | tf_op jit(solution)/shard_map/squeeze | solution.py:104
  69.3 7.4 %shard_map.64.acc_ref = f32[896,112]{1,0:T(8,128)S(1)} custom-call(bf16[3584,112]{1,0:T(8,128)(2,1)S(1)} %bitcast.40, bf16[112,1024]{1,0:T(8,128)(2,1)S(1)} %bitcast.43, bf16[32,112,112]{2,1,0:T(8,128)(2,1)S(1)} %get-tuple-element.20.b_ref, f32[896,112]{1,0:T(8,128)S(1)} %broadcast_in_dim.34.clone.acc_ref), custom_call_target="tpu_custom_call", output_to_operand_aliasing={{}: (3, {})} | custom-call | flops 1541406720 | bytes 2637824 | tf_op jit(solution)/shard_map/pallas_call | solution.py:47
  76.7 3.0 %collective-permute-start = (bf16[1,112,896]{2,1,0:T(8,128)(2,1)S(1)}, bf16[1,112,896]{2,1,0:T(8,128)(2,1)S(1)}, u32[]{:S(2)}, u32[]{:S(2)}) collective-permute-start(bf16[1,112,896]{2,1,0:T(8,128)(2,1)S(1)} %copy-done.1), channel_id=1, source_target_pairs={{0,8},{8,16},{16,24},{24,32},{32,40},{40,48},{48,56},{56,64},{64,7... | collective-permute-start | bytes 602120 | tf_op jit(solution)/shard_map/ppermute | solution.py:14
  79.8 21.0 %collective-permute-done = bf16[1,112,896]{2,1,0:T(8,128)(2,1)S(1)} collective-permute-done((bf16[1,112,896]{2,1,0:T(8,128)(2,1)S(1)}, bf16[1,112,896]{2,1,0:T(8,128)(2,1)S(1)}, u32[]{:S(2)}, u32[]{:S(2)}) %collective-permute-start) | collective-permute-done | bytes 200736 | tf_op jit(solution)/shard_map/ppermute | solution.py:14
  100.8 0.3 reshape_squeeze.15
  101.1 0.2 copy.24
  101.4 1.8 %copy.19 = bf16[1,32,64,196]{3,2,1,0:T(8,128)(2,1)S(1)} copy(bf16[1,32,64,196]{3,1,2,0:T(8,128)(2,1)} %bitcast.5) | data formatting | bytes 1605632 | tf_op jit(solution)/shard_map/all_to_all | solution.py:91
  103.2 3.1 %reshape_squeeze.13 = bf16[32,112,112]{2,1,0:T(8,128)(2,1)} reshape(bf16[1,32,64,196]{3,2,1,0:T(8,128)(2,1)S(1)} %copy.19) | data formatting | bytes 1605632 | tf_op jit(solution)/shard_map/reshape;squeeze | solution.py:96
  106.4 1.5 %copy.20 = bf16[32,112,112]{2,1,0:T(8,128)(2,1)S(1)} copy(bf16[32,112,112]{1,2,0:T(8,128)(2,1)} %bitcast.46) | data formatting | bytes 1605632 | tf_op jit(solution)/shard_map/transpose | solution.py:97
  107.9 7.4 %shard_map.65 = f32[896,112]{1,0:T(8,128)S(1)} custom-call(bf16[3584,112]{1,0:T(8,128)(2,1)S(1)} %bitcast.41, bf16[112,1024]{1,0:T(8,128)(2,1)S(1)} %bitcast.42, bf16[32,112,112]{2,1,0:T(8,128)(2,1)S(1)} %get-tuple-element.19.b_ref, f32[896,112]{1,0:T(8,128)S(1)} %shard_map.64.acc_ref), custom_call_target="tpu_custom_call", output_to_operand_aliasing={{}: (3, {})} | custom-call | flops 1541406720 | bytes 2637824 | tf_op jit(solution)/shard_map/pallas_call | solution.py:47
  115.4 0.2 copy.25
  115.6 0.8 reshape.104
  116.4 8.2 %all-to-all-start.2 = ((f32[8,14,896]{2,1,0:T(8,128)}), f32[8,14,896]{2,1,0:T(8,128)S(1)}, u32[]{:S(2)}, u32[]{:S(2)}) async-start(f32[8,14,896]{2,1,0:T(8,128)} %reshape.104), calls=%async_computation.2 | async-start | bytes 917504 | tf_op jit(solution)/shard_map/all_to_all | solution.py:108
  124.6 0.6 iota_compare_fusion
  125.3 0.1 select_reduce_fusion.1
  125.6 0.1 sub.28
  125.8 11.9 %all-to-all-done.2 = f32[8,14,896]{2,1,0:T(8,128)S(1)} async-done(((f32[8,14,896]{2,1,0:T(8,128)}), f32[8,14,896]{2,1,0:T(8,128)S(1)}, u32[]{:S(2)}, u32[]{:S(2)}) %all-to-all-start.2) | async-done | bytes 401440 | tf_op jit(solution)/shard_map/all_to_all | solution.py:108
  137.8 0.6 fusion
  (22 shorter events, 0.6 us)
Async XLA Ops:
  4.6 48.9 %all-to-all-start = ((bf16[64,32,196]{2,1,0:T(8,128)(2,1)}), bf16[64,32,196]{2,1,0:T(8,128)(2,1)S(1)}, u32[]{:S(2)}, u32[]{:S(2)}) async-start(bf16[64,32,196]{2,1,0:T(8,128)(2,1)} %gather_fusion.1), calls=%async_computation | async-start | bytes 2097152 | tf_op jit(solution)/shard_map/all_to_all | solution.py:91
  54.0 10.6 %copy-start = (bf16[1,112,896]{2,1,0:T(8,128)(2,1)S(1)}, bf16[1,112,896]{2,1,0:T(8,128)(2,1)}, u32[]{:S(2)}) copy-start(bf16[1,112,896]{2,1,0:T(8,128)(2,1)} %param.6) | copy-start | bytes 602116
  55.5 45.9 %all-to-all-start.1 = ((bf16[64,32,196]{2,1,0:T(8,128)(2,1)}), bf16[64,32,196]{2,1,0:T(8,128)(2,1)}, u32[]{:S(2)}, u32[]{:S(2)}) async-start(bf16[64,32,196]{2,1,0:T(8,128)(2,1)} %gather_fusion), calls=%async_computation.1 | async-start | bytes 2097152 | tf_op jit(solution)/shard_map/all_to_all | solution.py:91
  69.3 7.4 %copy-start.1 = (bf16[1,112,896]{2,1,0:T(8,128)(2,1)S(1)}, bf16[1,112,896]{2,1,0:T(8,128)(2,1)}, u32[]{:S(2)}) copy-start(bf16[1,112,896]{2,1,0:T(8,128)(2,1)} %param.6) | copy-start | bytes 602116
  76.7 24.1 %collective-permute-start = (bf16[1,112,896]{2,1,0:T(8,128)(2,1)S(1)}, bf16[1,112,896]{2,1,0:T(8,128)(2,1)S(1)}, u32[]{:S(2)}, u32[]{:S(2)}) collective-permute-start(bf16[1,112,896]{2,1,0:T(8,128)(2,1)S(1)} %copy-done.1), channel_id=1, source_target_pairs={{0,8},{8,16},{16,24},{24,32},{32,40},{40,48},{48,56},{56,64},{64,7... | collective-permute-start | bytes 602120 | tf_op jit(solution)/shard_map/ppermute | solution.py:14
  115.3 10.0 %copy-start.2 = (f32[64,112]{1,0:T(8,128)S(1)}, f32[64,112]{1,0:T(8,128)}, u32[]{:S(2)}) copy-start(f32[64,112]{1,0:T(8,128)} %param.10) | copy-start | bytes 86020
  115.4 10.3 %copy-start.3 = (f32[8]{0:T(128)S(1)}, f32[8]{0:T(128)}, u32[]{:S(2)}) copy-start(f32[8]{0:T(128)} %param.11) | copy-start | bytes 100
  116.4 21.3 %all-to-all-start.2 = ((f32[8,14,896]{2,1,0:T(8,128)}), f32[8,14,896]{2,1,0:T(8,128)S(1)}, u32[]{:S(2)}, u32[]{:S(2)}) async-start(f32[8,14,896]{2,1,0:T(8,128)} %reshape.104), calls=%async_computation.2 | async-start | bytes 917504 | tf_op jit(solution)/shard_map/all_to_all | solution.py:108

commit v7 on v5

--- a/solution.py
+++ b/solution.py
@@ -85,9 +85,18 @@
     blocks = [own_block] + [
         shifted(trial_vector, "ka", transfer)[0] for transfer in range(1, transfers)
     ]
+    tail = aux_local // 2
+    last = transfers - 1
+    groups = [
+        [(t, 0, aux_local) for t in range(last)] + [(last, 0, aux_local - tail)],
+        [(last, aux_local - tail, tail)],
+    ]
     arrivals = []
-    for transfer in range(transfers):
-        piece = right_factor[:, transfer].at[kb_table].get(mode="promise_in_bounds")
+    for group in groups:
+        piece = jnp.concatenate(
+            [right_factor[:, t, start:start + count] for t, start, count in group], axis=1
+        )
+        piece = piece.at[kb_table].get(mode="promise_in_bounds")
         if arrivals:
             piece, arrivals[-1], bq, blocks = lax.optimization_barrier(
                 (piece, arrivals[-1], bq, blocks)
@@ -96,11 +105,18 @@
             lax.all_to_all(piece, "ka", split_axis=0, concat_axis=2, tiled=True)[0]
         )
     ladder_t = jnp.zeros((pair_count * virtuals, virtuals), jnp.float32)
-    for transfer in range(transfers):
-        right = arrivals[transfer].reshape(aux_local, virtuals, virtuals)
-        ct = jnp.swapaxes(right, 1, 2).reshape(aux_local * virtuals, virtuals)
-        tt = trial_transposed(blocks[transfer], virtuals, pair_count)
-        ladder_t = ladder_transposed(ct, tt, bq[transfer], ladder_t)
+    tts = [trial_transposed(b, virtuals, pair_count) for b in blocks]
+    for group, arrived in zip(groups, arrivals):
+        slabs = sum(count for _, _, count in group)
+        right = arrived.reshape(slabs, virtuals, virtuals)
+        ct = jnp.swapaxes(right, 1, 2).reshape(slabs * virtuals, virtuals)
+        at = 0
+        for t, start, count in group:
+            ladder_t = ladder_transposed(
+                ct[at * virtuals:(at + count) * virtuals], tts[t],
+                bq[t, start:start + count], ladder_t,
+            )
+            at += count
     ladder_sum = ladder_t.T
     vert = lax.axis_size("vert")
     slab_width = virtuals // vert
@@ -114,7 +130,7 @@
     energy_rows = jnp.sum(jnp.where((labels == owner_index)[:, None], vir_energy, 0.0), axis=0)
     energy_other = jnp.sum(jnp.where((labels == momentum_b)[:, None], vir_energy, 0.0), axis=0)
     energy_a = lax.dynamic_slice_in_dim(energy_rows, offset, slab_width, 0)
-    own_rows = lax.dynamic_slice_in_dim(blocks[0], offset, slab_width, 0).astype(jnp.float32)
+    own_rows = lax.dynamic_slice_in_dim(own_block, offset, slab_width, 0).astype(jnp.float32)
     own_rows = own_rows.reshape(slab_width, pair_count, virtuals)
     shift_energy = (
         energy_a[:, None, None] + energy_other[None, None, :] - pair_energy[None, :, None]

time: 138 us -> 136 us (0.986)
  waiting for transfers between devices: 51.3 us -> 47.4 us
    all_to_all x1, starting transfers between devices: 12.1 us -> 6.68 us  [shards(): lax.all_to_all(ladder_sum.reshape(vert, slab_width, -1), 'vert', 0, 0, ti...]
    all_to_all x2, starting transfers between devices: 27.6 us -> 32 us  [shards(): lax.all_to_all(piece, 'ka', split_axis=0, concat_axis=2, tiled=True)[0]]
    all_to_all x2, waiting for transfers between devices: 33.1 us -> 30.2 us  [shards(): lax.all_to_all(piece, 'ka', split_axis=0, concat_axis=2, tiled=True)[0]]
    another operation x1, local copies, waits for them, and re-layouts: 3.14 us -> 1.06 us  [shards(): right = arrived.reshape(slabs, virtuals, virtuals)]
    reshape x1, local copies, waits for them, and re-layouts: 1.78 us -> 3.77 us  [shards(): right = arrived.reshape(slabs, virtuals, virtuals)]
    transpose x2 -> x1, local copies, waits for them, and re-layouts: 2.09 us -> 0.24 us  [shards(): ct = jnp.swapaxes(right, 1, 2).reshape(slabs * virtuals, virtuals)]
    all_to_all x2, local copies, waits for them, and re-layouts: 2.39 us -> 0.68 us  [shards(): lax.all_to_all(piece, 'ka', split_axis=0, concat_axis=2, tiled=True)[0]]
    squeeze x1, local copies, waits for them, and re-layouts: 1.43 us -> 2.92 us  [shards(): lax.all_to_all(piece, 'ka', split_axis=0, concat_axis=2, tiled=True)[0]]
  transfers between devices with their start and end apart: 4 -> 4, of which waited for: 4 -> 3; matrix products, arithmetic and copies ran while one was open for 11% -> 14% of each run, Pallas kernels for 5% -> 8%
where the time goes in v7:
time: 136 us; the launch traced here: 135 us
  waiting for transfers between devices  47.4 us (35%)
  starting transfers between devices  41.6 us (31%)
  local copies, waits for them, and re-layouts  26.6 us (20%)
  Pallas kernels  14.9 us (11%)
  other arithmetic  4.3 us (3%)
    all_to_all x2, starting transfers between devices, shards(): lax.all_to_all(piece, 'ka', split_axis=0, concat_axis=2, tiled=True)[0]  32 us
    all_to_all x2, waiting for transfers between devices, shards(): lax.all_to_all(piece, 'ka', split_axis=0, concat_axis=2, tiled=True)[0]  30.2 us
    pallas_call x3, Pallas kernels, ladder_transposed(): pl.pallas_call(kernel, out_shape=jax.ShapeDtypeStruct((pairs * nv, nv), j...  14.9 us
    all_to_all x1, waiting for transfers between devices, shards(): lax.all_to_all(ladder_sum.reshape(vert, slab_width, -1), 'vert', 0, 0, ti...  11.9 us
    all_to_all x1, starting transfers between devices, shards(): lax.all_to_all(ladder_sum.reshape(vert, slab_width, -1), 'vert', 0, 0, ti...  6.68 us
    another operation x1, local copies, waits for them, and re-layouts, shards(): bq = left_factor[0].reshape(transfers, aux_local, virtuals, virtuals)  5.5 us
    ppermute x1, waiting for transfers between devices, shifted(): return lax.ppermute(value, axis, pairs)  5.22 us
    reshape x1, local copies, waits for them, and re-layouts, shards(): right = arrived.reshape(slabs, virtuals, virtuals)  3.77 us
  transfers between devices with their start and end apart: 4, of which 3 were waited for; matrix products, arithmetic and copies ran while one was open for 14% of the time, Pallas kernels for 8%

profile of v7, /device:TPU:1, one launch (start us, length us, event | category | flops | bytes accessed | tf_op | source)
XLA Modules:
  0.0 135.1 jit_solution(2753711126196843496)
XLA Ops:
  0.0 2.2 %slice_bitcast_fusion.2 = (bf16[64,16,196]{2,1,0:T(8,128)(2,1)}, bf16[64,16,196]{2,1,0:T(8,128)(2,1)S(1)}) fusion(bf16[64,2,32,196]{3,2,1,0:T(8,128)(2,1)} %param.8), kind=kLoop, calls=%fused_computation.5 | loop fusion | bytes 1605632 | tf_op jit(solution)/shard_map/squeeze | solution.py:97
  2.3 0.6 copy-done.7
  2.9 0.6 select_reduce_fusion.2
  3.5 1.4 %pad_maximum_fusion = bf16[64,48,196]{2,1,0:T(8,128)(2,1)S(1)} fusion(bf16[64,16,196]{2,1,0:T(8,128)(2,1)} %get-tuple-element.17, bf16[64,32,196]{2,1,0:T(8,128)(2,1)S(1)} %slice_bitcast_fusion), kind=kLoop, calls=%fused_computation.2 | loop fusion | flops 2408448 | bytes 2408448 | tf_op jit(solution)/shard_map/concatenate | solution.py:96
  4.9 1.8 %gather_fusion.1 = bf16[64,48,196]{2,1,0:T(8,128)(2,1)} fusion(bf16[64,48,196]{2,1,0:T(8,128)(2,1)S(1)} %pad_maximum_fusion, s32[1024]{0:T(1024)S(1)} %pad_clamp_fusion), kind=kCustom, calls=%fused_computation.1 | custom fusion | bytes 2408704 | tf_op jit(solution)/shard_map/gather | solution.py:99
  6.7 19.7 %all-to-all-start = ((bf16[64,48,196]{2,1,0:T(8,128)(2,1)}), bf16[64,48,196]{2,1,0:T(8,128)(2,1)S(1)}, u32[]{:S(2)}, u32[]{:S(2)}) async-start(bf16[64,48,196]{2,1,0:T(8,128)(2,1)} %gather_fusion.1), calls=%async_computation | async-start | bytes 3145728 | tf_op jit(solution)/shard_map/all_to_all | solution.py:105
  26.4 2.9 %collective-permute-start = (bf16[1,112,896]{2,1,0:T(8,128)(2,1)S(1)}, bf16[1,112,896]{2,1,0:T(8,128)(2,1)S(1)}, u32[]{:S(2)}, u32[]{:S(2)}) collective-permute-start(bf16[1,112,896]{2,1,0:T(8,128)(2,1)S(1)} %copy-done.2), channel_id=1, source_target_pairs={{0,8},{8,16},{16,24},{24,32},{32,40},{40,48},{48,56},{56,64},{64,7... | collective-permute-start | bytes 602120 | tf_op jit(solution)/shard_map/ppermute | solution.py:14
  29.3 1.4 %gather_fusion = bf16[64,16,196]{2,1,0:T(8,128)(2,1)} fusion(bf16[64,16,196]{2,1,0:T(8,128)(2,1)S(1)} %get-tuple-element.18, s32[1024]{0:T(1024)S(1)} %pad_clamp_fusion), kind=kCustom, calls=%fused_computation | custom fusion | bytes 803072 | tf_op jit(solution)/shard_map/gather | solution.py:99
  30.7 5.5 %reshape_squeeze.6 = bf16[2,32,112,112]{3,2,1,0:T(8,128)(2,1)} reshape(bf16[1,2,32,12544]{3,2,1,0:T(8,128)(2,1)} %param.7) | data formatting | bytes 3211264 | tf_op jit(solution)/shard_map/reshape;squeeze | solution.py:84
  36.2 30.2 %all-to-all-done = bf16[64,48,196]{2,1,0:T(8,128)(2,1)S(1)} async-done(((bf16[64,48,196]{2,1,0:T(8,128)(2,1)}), bf16[64,48,196]{2,1,0:T(8,128)(2,1)S(1)}, u32[]{:S(2)}, u32[]{:S(2)}) %all-to-all-start) | async-done | bytes 1204256 | tf_op jit(solution)/shard_map/all_to_all | solution.py:105
  66.4 0.5 copy.20
  67.0 2.9 %squeeze.30 = bf16[48,12544]{1,0:T(8,128)(2,1)} reshape(bf16[1,48,64,196]{3,2,1,0:T(8,128)(2,1)S(1)} %copy.20) | data formatting | bytes 2408448 | tf_op jit(solution)/shard_map/squeeze | solution.py:105
  69.9 5.2 %collective-permute-done = bf16[1,112,896]{2,1,0:T(8,128)(2,1)S(1)} collective-permute-done((bf16[1,112,896]{2,1,0:T(8,128)(2,1)S(1)}, bf16[1,112,896]{2,1,0:T(8,128)(2,1)S(1)}, u32[]{:S(2)}, u32[]{:S(2)}) %collective-permute-start) | collective-permute-done | bytes 200736 | tf_op jit(solution)/shard_map/ppermute | solution.py:14
  75.1 0.7 copy-done.4
  75.8 12.3 %all-to-all-start.1 = ((bf16[64,16,196]{2,1,0:T(8,128)(2,1)}), bf16[64,16,196]{2,1,0:T(8,128)(2,1)S(1)}, u32[]{:S(2)}, u32[]{:S(2)}) async-start(bf16[64,16,196]{2,1,0:T(8,128)(2,1)} %gather_fusion), calls=%async_computation.1 | async-start | bytes 1048576 | tf_op jit(solution)/shard_map/all_to_all | solution.py:105
  88.1 3.8 %reshape.108 = bf16[48,112,112]{2,1,0:T(8,128)(2,1)S(1)} reshape(bf16[48,12544]{1,0:T(8,128)(2,1)} %squeeze.30) | data formatting | bytes 2408448 | tf_op jit(solution)/shard_map/reshape | solution.py:111
  91.9 1.2 reshape.106
  93.2 0.2 copy.23
  93.5 0.2 copy.24
  93.7 0.6 copy.25
  94.4 0.3 reshape.109
  95.0 1.2 slice_bitcast_fusion.1.b_ref
  96.3 7.4 %shard_map.64.acc_ref = f32[896,112]{1,0:T(8,128)S(1)} custom-call(bf16[3584,112]{1,0:T(8,128)(2,1)S(1)} %bitcast.47, bf16[112,1024]{1,0:T(8,128)(2,1)S(1)} %bitcast.52, bf16[32,112,112]{2,1,0:T(8,128)(2,1)S(1)} %slice_bitcast_fusion.1.b_ref, f32[896,112]{1,0:T(8,128)S(1)} %broadcast_in_dim.34.clone.acc_ref), custom_call_target="tpu_custom_call", output_to_operand_aliasing={{}: (3, {})} | custom-call | flops 1541406720 | bytes 2637824 | tf_op jit(solution)/shard_map/pallas_call | solution.py:47
  103.8 3.8 %shard_map.65.acc_ref = f32[896,112]{1,0:T(8,128)S(1)} custom-call(bf16[1792,112]{1,0:T(8,128)(2,1)S(1)} %bitcast.48, bf16[112,1024]{1,0:T(8,128)(2,1)S(1)} %bitcast.50, bf16[16,112,112]{2,1,0:T(8,128)(2,1)S(1)} %get-tuple-element.19.b_ref, f32[896,112]{1,0:T(8,128)S(1)} %shard_map.64.acc_ref), custom_call_target="tpu_custom_call", output_to_operand_aliasing={{}: (3, {})} | custom-call | flops 770703360 | bytes 1835008 | tf_op jit(solution)/shard_map/pallas_call | solution.py:47
  107.7 1.1 reshape_squeeze.7
  108.8 0.2 copy.22
  109.0 3.8 %shard_map.66 = f32[896,112]{1,0:T(8,128)S(1)} custom-call(bf16[1792,112]{1,0:T(8,128)(2,1)S(1)} %bitcast.49, bf16[112,1024]{1,0:T(8,128)(2,1)S(1)} %bitcast.51, bf16[16,112,112]{2,1,0:T(8,128)(2,1)S(1)} %get-tuple-element.20.b_ref, f32[896,112]{1,0:T(8,128)S(1)} %shard_map.65.acc_ref), custom_call_target="tpu_custom_call", output_to_operand_aliasing={{}: (3, {})} | custom-call | flops 770703360 | bytes 1835008 | tf_op jit(solution)/shard_map/pallas_call | solution.py:47
  113.0 0.8 reshape.111
  113.8 6.7 %all-to-all-start.2 = ((f32[8,14,896]{2,1,0:T(8,128)}), f32[8,14,896]{2,1,0:T(8,128)S(1)}, u32[]{:S(2)}, u32[]{:S(2)}) async-start(f32[8,14,896]{2,1,0:T(8,128)} %reshape.111), calls=%async_computation.2 | async-start | bytes 917504 | tf_op jit(solution)/shard_map/all_to_all | solution.py:123
  120.5 0.6 iota_compare_fusion
  121.7 11.9 %all-to-all-done.2 = f32[8,14,896]{2,1,0:T(8,128)S(1)} async-done(((f32[8,14,896]{2,1,0:T(8,128)}), f32[8,14,896]{2,1,0:T(8,128)S(1)}, u32[]{:S(2)}, u32[]{:S(2)}) %all-to-all-start.2) | async-done | bytes 401440 | tf_op jit(solution)/shard_map/all_to_all | solution.py:123
  133.6 1.4 %fusion = bf16[1,14,896]{2,1,0:T(8,128)(2,1)} fusion(f32[14,896]{1,0:T(8,128)S(1)} %reduce_sum.38, f32[1,14,896]{2,1,0:T(8,128)S(1)} %sub.28, bf16[1,112,896]{2,1,0:T(8,128)(2,1)} %param.6, s32[]{:T(128)S(6)} %select_n.21, f32[896]{0:T(1024)S(1)} %sub.30), kind=kLoop, calls=%fused_computation.12 | loop fusion | flops 62720 | bytes 154116 | tf_op jit(solution)/shard_map/convert_element_type | solution.py:139
  (37 shorter events, 1.6 us)
Async XLA Ops:
  0.0 2.2 %copy-start.1 = (bf16[64,2,32,196]{3,2,1,0:T(8,128)(2,1)S(1)}, bf16[64,2,32,196]{3,2,1,0:T(8,128)(2,1)}, u32[]{:S(2)}) copy-start(bf16[64,2,32,196]{3,2,1,0:T(8,128)(2,1)} %param.8) | copy-start | bytes 4816900
  2.2 0.7 copy-start.7
  6.7 19.7 %copy-start.2 = (bf16[1,112,896]{2,1,0:T(8,128)(2,1)S(1)}, bf16[1,112,896]{2,1,0:T(8,128)(2,1)}, u32[]{:S(2)}) copy-start(bf16[1,112,896]{2,1,0:T(8,128)(2,1)} %param.6) | copy-start | bytes 602116
  6.7 59.8 %all-to-all-start = ((bf16[64,48,196]{2,1,0:T(8,128)(2,1)}), bf16[64,48,196]{2,1,0:T(8,128)(2,1)S(1)}, u32[]{:S(2)}, u32[]{:S(2)}) async-start(bf16[64,48,196]{2,1,0:T(8,128)(2,1)} %gather_fusion.1), calls=%async_computation | async-start | bytes 3145728 | tf_op jit(solution)/shard_map/all_to_all | solution.py:105
  26.4 48.7 %collective-permute-start = (bf16[1,112,896]{2,1,0:T(8,128)(2,1)S(1)}, bf16[1,112,896]{2,1,0:T(8,128)(2,1)S(1)}, u32[]{:S(2)}, u32[]{:S(2)}) collective-permute-start(bf16[1,112,896]{2,1,0:T(8,128)(2,1)S(1)} %copy-done.2), channel_id=1, source_target_pairs={{0,8},{8,16},{16,24},{24,32},{32,40},{40,48},{48,56},{56,64},{64,7... | collective-permute-start | bytes 602120 | tf_op jit(solution)/shard_map/ppermute | solution.py:14
  75.1 0.7 copy-start.4
  75.8 31.8 %all-to-all-start.1 = ((bf16[64,16,196]{2,1,0:T(8,128)(2,1)}), bf16[64,16,196]{2,1,0:T(8,128)(2,1)S(1)}, u32[]{:S(2)}, u32[]{:S(2)}) async-start(bf16[64,16,196]{2,1,0:T(8,128)(2,1)} %gather_fusion), calls=%async_computation.1 | async-start | bytes 1048576 | tf_op jit(solution)/shard_map/all_to_all | solution.py:105
  93.4 0.9 copy-start.3
  96.3 7.4 %copy-start = (bf16[2,32,112,112]{3,2,1,0:T(8,128)(2,1)S(1)}, bf16[2,32,112,112]{3,2,1,0:T(8,128)(2,1)}, u32[]{:S(2)}) copy-start(bf16[2,32,112,112]{3,2,1,0:T(8,128)(2,1)} %reshape_squeeze.6) | copy-start | bytes 4816900
  112.8 8.4 %copy-start.5 = (f32[64,112]{1,0:T(8,128)S(1)}, f32[64,112]{1,0:T(8,128)}, u32[]{:S(2)}) copy-start(f32[64,112]{1,0:T(8,128)} %param.10) | copy-start | bytes 86020
  112.8 8.7 %copy-start.6 = (f32[8]{0:T(128)S(1)}, f32[8]{0:T(128)}, u32[]{:S(2)}) copy-start(f32[8]{0:T(128)} %param.11) | copy-start | bytes 100
  113.8 19.8 %all-to-all-start.2 = ((f32[8,14,896]{2,1,0:T(8,128)}), f32[8,14,896]{2,1,0:T(8,128)S(1)}, u32[]{:S(2)}, u32[]{:S(2)}) async-start(f32[8,14,896]{2,1,0:T(8,128)} %reshape.111), calls=%async_computation.2 | async-start | bytes 917504 | tf_op jit(solution)/shard_map/all_to_all | solution.py:123

commit v8 on v7

--- a/solution.py
+++ b/solution.py
@@ -120,9 +120,12 @@
     ladder_sum = ladder_t.T
     vert = lax.axis_size("vert")
     slab_width = virtuals // vert
-    ladder = lax.all_to_all(
-        ladder_sum.reshape(vert, slab_width, -1), "vert", 0, 0, tiled=True
-    ).sum(0)
+    slabs = ladder_sum.reshape(vert, slab_width, -1)
+    me = lax.axis_index("vert")
+    ladder = lax.dynamic_index_in_dim(slabs, me, 0, keepdims=False)
+    for step in range(1, vert):
+        outgoing = lax.dynamic_index_in_dim(slabs, (me + step) % vert, 0, keepdims=False)
+        ladder = ladder + shifted(outgoing, "vert", step)
     offset = lax.axis_index("vert") * slab_width
     labels = jnp.arange(kpoints, dtype=jnp.int32)
     owner_index = lax.axis_index("ka")

time: 136 us -> 141 us (1.037)
  starting transfers between devices: 41.6 us -> 58.5 us
  waiting for transfers between devices: 47.4 us -> 36.4 us
  local copies, waits for them, and re-layouts: 26.6 us -> 24.2 us
    ppermute x1 -> x8, starting transfers between devices: 2.92 us -> 26.5 us  [shifted(): return lax.ppermute(value, axis, pairs)]
    all_to_all x1 -> x0, waiting for transfers between devices: 11.9 us -> none  [shards(): lax.all_to_all(ladder_sum.reshape(vert, slab_width, -1), 'vert', 0, 0, ti...]
    all_to_all x1 -> x0, starting transfers between devices: 6.68 us -> none  [shards(): lax.all_to_all(ladder_sum.reshape(vert, slab_width, -1), 'vert', 0, 0, ti...]
    broadcast_in_dim x0 -> x1, other arithmetic: none -> 1.44 us  [shards(): return combined.astype(jnp.bfloat16)[None]]
    convert_element_type x1 -> x0, other arithmetic: 1.43 us -> none  [shards(): return combined.astype(jnp.bfloat16)[None]]
    ppermute x1 -> x8, waiting for transfers between devices: 5.22 us -> 6.21 us  [shifted(): return lax.ppermute(value, axis, pairs)]
  transfers between devices with their start and end apart: 4 -> 10, of which waited for: 3 -> 4; matrix products, arithmetic and copies ran while one was open for 14% -> 13% of each run, Pallas kernels for 8% -> 8%
where the time goes in v8:
time: 141 us; the launch traced here: 139 us
  starting transfers between devices  58.5 us (41%)
  waiting for transfers between devices  36.4 us (26%)
  local copies, waits for them, and re-layouts  24.2 us (17%)
  Pallas kernels  14.9 us (11%)
  other arithmetic  4.28 us (3%)
    all_to_all x2, starting transfers between devices, shards(): lax.all_to_all(piece, 'ka', split_axis=0, concat_axis=2, tiled=True)[0]  32 us
    all_to_all x2, waiting for transfers between devices, shards(): lax.all_to_all(piece, 'ka', split_axis=0, concat_axis=2, tiled=True)[0]  30.2 us
    ppermute x8, starting transfers between devices, shifted(): return lax.ppermute(value, axis, pairs)  26.5 us
    pallas_call x3, Pallas kernels, ladder_transposed(): pl.pallas_call(kernel, out_shape=jax.ShapeDtypeStruct((pairs * nv, nv), j...  14.9 us
    ppermute x8, waiting for transfers between devices, shifted(): return lax.ppermute(value, axis, pairs)  6.21 us
    another operation x1, local copies, waits for them, and re-layouts, shards(): bq = left_factor[0].reshape(transfers, aux_local, virtuals, virtuals)  5.51 us
    gather x2, local copies, waits for them, and re-layouts, shards(): piece = piece.at[kb_table].get(mode='promise_in_bounds')  3.2 us
    squeeze x1, local copies, waits for them, and re-layouts, shards(): lax.all_to_all(piece, 'ka', split_axis=0, concat_axis=2, tiled=True)[0]  2.91 us
  transfers between devices with their start and end apart: 10, of which 4 were waited for; matrix products, arithmetic and copies ran while one was open for 13% of the time, Pallas kernels for 8%

profile of v8, /device:TPU:1, one launch (start us, length us, event | category | flops | bytes accessed | tf_op | source)
XLA Modules:
  0.0 138.9 jit_solution(1546003911471232509)
XLA Ops:
  0.0 2.2 %slice_bitcast_fusion.2 = (bf16[64,16,196]{2,1,0:T(8,128)(2,1)}, bf16[64,16,196]{2,1,0:T(8,128)(2,1)S(1)}) fusion(bf16[64,2,32,196]{3,2,1,0:T(8,128)(2,1)} %param.8), kind=kLoop, calls=%fused_computation.5 | loop fusion | bytes 1605632 | tf_op jit(solution)/shard_map/squeeze | solution.py:97
  2.3 0.6 copy-done.7
  2.9 0.6 compare_select_fusion
  3.5 1.4 pad_maximum_fusion
  4.9 1.8 %gather_fusion.1 = bf16[64,48,196]{2,1,0:T(8,128)(2,1)} fusion(bf16[64,48,196]{2,1,0:T(8,128)(2,1)S(1)} %pad_maximum_fusion, s32[1024]{0:T(1024)S(1)} %pad_clamp_fusion), kind=kCustom, calls=%fused_computation.1 | custom fusion | bytes 2408704 | tf_op jit(solution)/shard_map/gather | solution.py:99
  6.7 19.7 %all-to-all-start = ((bf16[64,48,196]{2,1,0:T(8,128)(2,1)}), bf16[64,48,196]{2,1,0:T(8,128)(2,1)S(1)}, u32[]{:S(2)}, u32[]{:S(2)}) async-start(bf16[64,48,196]{2,1,0:T(8,128)(2,1)} %gather_fusion.1), calls=%async_computation | async-start | bytes 3145728 | tf_op jit(solution)/shard_map/all_to_all | solution.py:105
  26.4 2.9 %collective-permute-start = (bf16[1,112,896]{2,1,0:T(8,128)(2,1)S(1)}, bf16[1,112,896]{2,1,0:T(8,128)(2,1)}, u32[]{:S(2)}, u32[]{:S(2)}) collective-permute-start(bf16[1,112,896]{2,1,0:T(8,128)(2,1)S(1)} %copy-done.3), channel_id=1, source_target_pairs={{0,8},{8,16},{16,24},{24,32},{32,40},{40,48},{48,56},{56,64},{64,7... | collective-permute-start | bytes 602120 | tf_op jit(solution)/shard_map/ppermute | solution.py:14
  29.3 1.4 %gather_fusion = bf16[64,16,196]{2,1,0:T(8,128)(2,1)} fusion(bf16[64,16,196]{2,1,0:T(8,128)(2,1)S(1)} %get-tuple-element.18, s32[1024]{0:T(1024)S(1)} %pad_clamp_fusion), kind=kCustom, calls=%fused_computation | custom fusion | bytes 803072 | tf_op jit(solution)/shard_map/gather | solution.py:99
  30.7 5.5 %reshape_squeeze.6 = bf16[2,32,112,112]{3,2,1,0:T(8,128)(2,1)} reshape(bf16[1,2,32,12544]{3,2,1,0:T(8,128)(2,1)} %param.7) | data formatting | bytes 3211264 | tf_op jit(solution)/shard_map/reshape;squeeze | solution.py:84
  36.3 30.2 %all-to-all-done = bf16[64,48,196]{2,1,0:T(8,128)(2,1)S(1)} async-done(((bf16[64,48,196]{2,1,0:T(8,128)(2,1)}), bf16[64,48,196]{2,1,0:T(8,128)(2,1)S(1)}, u32[]{:S(2)}, u32[]{:S(2)}) %all-to-all-start) | async-done | bytes 1204256 | tf_op jit(solution)/shard_map/all_to_all | solution.py:105
  66.5 0.5 copy.28
  67.0 2.9 %squeeze.55 = bf16[48,12544]{1,0:T(8,128)(2,1)} reshape(bf16[1,48,64,196]{3,2,1,0:T(8,128)(2,1)S(1)} %copy.28) | data formatting | bytes 2408448 | tf_op jit(solution)/shard_map/squeeze | solution.py:105
  69.9 5.3 %collective-permute-done = bf16[1,112,896]{2,1,0:T(8,128)(2,1)} collective-permute-done((bf16[1,112,896]{2,1,0:T(8,128)(2,1)S(1)}, bf16[1,112,896]{2,1,0:T(8,128)(2,1)}, u32[]{:S(2)}, u32[]{:S(2)}) %collective-permute-start) | collective-permute-done | bytes 200736 | tf_op jit(solution)/shard_map/ppermute | solution.py:14
  75.2 12.3 %all-to-all-start.1 = ((bf16[64,16,196]{2,1,0:T(8,128)(2,1)}), bf16[64,16,196]{2,1,0:T(8,128)(2,1)S(1)}, u32[]{:S(2)}, u32[]{:S(2)}) async-start(bf16[64,16,196]{2,1,0:T(8,128)(2,1)} %gather_fusion), calls=%async_computation.1 | async-start | bytes 1048576 | tf_op jit(solution)/shard_map/all_to_all | solution.py:105
  87.5 0.7 iota_compare_fusion
  88.3 2.7 %reshape.75 = bf16[48,112,112]{2,1,0:T(8,128)(2,1)S(1)} reshape(bf16[48,12544]{1,0:T(8,128)(2,1)S(1)} %copy-done.1) | data formatting | bytes 2408448 | tf_op jit(solution)/shard_map/reshape | solution.py:111
  91.2 1.2 reshape.73
  92.9 0.6 copy.33
  94.2 1.2 slice_bitcast_fusion.1.b_ref
  95.5 7.4 %shard_map.64.acc_ref = f32[896,112]{1,0:T(8,128)S(1)} custom-call(bf16[3584,112]{1,0:T(8,128)(2,1)S(1)} %bitcast.82, bf16[112,1024]{1,0:T(8,128)(2,1)S(1)} %bitcast.87, bf16[32,112,112]{2,1,0:T(8,128)(2,1)S(1)} %slice_bitcast_fusion.1.b_ref, f32[896,112]{1,0:T(8,128)S(1)} %broadcast_in_dim.36.clone.acc_ref), custom_call_target="tpu_custom_call", output_to_operand_aliasing={{}: (3, {})} | custom-call | flops 1541406720 | bytes 2637824 | tf_op jit(solution)/shard_map/pallas_call | solution.py:47
  103.0 3.8 %shard_map.65.acc_ref = f32[896,112]{1,0:T(8,128)S(1)} custom-call(bf16[1792,112]{1,0:T(8,128)(2,1)S(1)} %bitcast.83, bf16[112,1024]{1,0:T(8,128)(2,1)S(1)} %bitcast.85, bf16[16,112,112]{2,1,0:T(8,128)(2,1)S(1)} %get-tuple-element.19.b_ref, f32[896,112]{1,0:T(8,128)S(1)} %shard_map.64.acc_ref), custom_call_target="tpu_custom_call", output_to_operand_aliasing={{}: (3, {})} | custom-call | flops 770703360 | bytes 1835008 | tf_op jit(solution)/shard_map/pallas_call | solution.py:47
  106.9 1.1 reshape_squeeze.7
  108.3 3.8 %shard_map.66 = f32[896,112]{1,0:T(8,128)S(1)} custom-call(bf16[1792,112]{1,0:T(8,128)(2,1)S(1)} %bitcast.84, bf16[112,1024]{1,0:T(8,128)(2,1)S(1)} %bitcast.86, bf16[16,112,112]{2,1,0:T(8,128)(2,1)S(1)} %get-tuple-element.20.b_ref, f32[896,112]{1,0:T(8,128)S(1)} %shard_map.65.acc_ref), custom_call_target="tpu_custom_call", output_to_operand_aliasing={{}: (3, {})} | custom-call | flops 770703360 | bytes 1835008 | tf_op jit(solution)/shard_map/pallas_call | solution.py:47
  112.3 4.7 %collective-permute-start.7 = (f32[14,896]{1,0:T(8,128)S(1)}, f32[14,896]{1,0:T(8,128)S(1)}, u32[]{:S(2)}, u32[]{:S(2)}) collective-permute-start(f32[14,896]{1,0:T(8,128)S(1)} %get-tuple-element.22), channel_id=1, source_target_pairs={{0,7},{1,0},{2,1},{3,2},{4,3},{5,4},{6,5},{7,6},{8,15},{9,8},{10,9... | collective-permute-start | bytes 150536 | tf_op jit(solution)/shard_map/ppermute | solution.py:14
  117.0 4.5 %collective-permute-start.6 = (f32[14,896]{1,0:T(8,128)S(1)}, f32[14,896]{1,0:T(8,128)S(1)}, u32[]{:S(2)}, u32[]{:S(2)}) collective-permute-start(f32[14,896]{1,0:T(8,128)S(1)} %get-tuple-element.23), channel_id=1, source_target_pairs={{0,6},{1,7},{2,0},{3,1},{4,2},{5,3},{6,4},{7,5},{8,14},{9,15},{10,... | collective-permute-start | bytes 150536 | tf_op jit(solution)/shard_map/ppermute | solution.py:14
  121.8 1.9 %collective-permute-start.5 = (f32[14,896]{1,0:T(8,128)S(1)}, f32[14,896]{1,0:T(8,128)S(1)}, u32[]{:S(2)}, u32[]{:S(2)}) collective-permute-start(f32[14,896]{1,0:T(8,128)S(1)} %get-tuple-element.24), channel_id=1, source_target_pairs={{0,5},{1,6},{2,7},{3,0},{4,1},{5,2},{6,3},{7,4},{8,13},{9,14},{10,... | collective-permute-start | bytes 150536 | tf_op jit(solution)/shard_map/ppermute | solution.py:14
  123.7 2.3 %collective-permute-start.4 = (f32[14,896]{1,0:T(8,128)S(1)}, f32[14,896]{1,0:T(8,128)S(1)}, u32[]{:S(2)}, u32[]{:S(2)}) collective-permute-start(f32[14,896]{1,0:T(8,128)S(1)} %get-tuple-element.25), channel_id=1, source_target_pairs={{0,4},{1,5},{2,6},{3,7},{4,0},{5,1},{6,2},{7,3},{8,12},{9,13},{10,... | collective-permute-start | bytes 150536 | tf_op jit(solution)/shard_map/ppermute | solution.py:14
  126.0 4.4 %collective-permute-start.3 = (f32[14,896]{1,0:T(8,128)S(1)}, f32[14,896]{1,0:T(8,128)S(1)}, u32[]{:S(2)}, u32[]{:S(2)}) collective-permute-start(f32[14,896]{1,0:T(8,128)S(1)} %get-tuple-element.26), channel_id=1, source_target_pairs={{0,3},{1,4},{2,5},{3,6},{4,7},{5,0},{6,1},{7,2},{8,11},{9,12},{10,... | collective-permute-start | bytes 150536 | tf_op jit(solution)/shard_map/ppermute | solution.py:14
  130.3 2.3 %collective-permute-start.2 = (f32[14,896]{1,0:T(8,128)S(1)}, f32[14,896]{1,0:T(8,128)S(1)}, u32[]{:S(2)}, u32[]{:S(2)}) collective-permute-start(f32[14,896]{1,0:T(8,128)S(1)} %get-tuple-element.27), channel_id=1, source_target_pairs={{0,2},{1,3},{2,4},{3,5},{4,6},{5,7},{6,0},{7,1},{8,10},{9,11},{10,... | collective-permute-start | bytes 150536 | tf_op jit(solution)/shard_map/ppermute | solution.py:14
  132.7 3.5 %collective-permute-start.1 = (f32[14,896]{1,0:T(8,128)S(1)}, f32[14,896]{1,0:T(8,128)S(1)}, u32[]{:S(2)}, u32[]{:S(2)}) collective-permute-start(f32[14,896]{1,0:T(8,128)S(1)} %get-tuple-element.21), channel_id=1, source_target_pairs={{0,1},{1,2},{2,3},{3,4},{4,5},{5,6},{6,7},{7,0},{8,9},{9,10},{10,1... | collective-permute-start | bytes 150536 | tf_op jit(solution)/shard_map/ppermute | solution.py:14
  136.6 0.5 collective-permute-done.2
  137.4 1.4 %fusion.8 = bf16[1,14,896]{2,1,0:T(8,128)(2,1)} fusion(bf16[1,112,896]{2,1,0:T(8,128)(2,1)} %param.6, s32[]{:T(128)S(6)} %select_n.92, f32[14,896]{1,0:T(8,128)S(1)} %sub.21, f32[896]{0:T(1024)S(1)} %sub.23, f32[14,896]{1,0:T(8,128)S(1)} %collective-permute-done.7, f32[14,896]{1,0:T(8,128)S(1)} %collective-permute-done.6, ...), kind=kLoop, calls=%fused_computation.30 | loop fusion | flops 150528 | bytes 505352 | tf_op jit(solution)/shard_map/broadcast_in_dim | solution.py:142
  (49 shorter events, 3.1 us)
Async XLA Ops:
  0.0 2.2 %copy-start.2 = (bf16[64,2,32,196]{3,2,1,0:T(8,128)(2,1)S(1)}, bf16[64,2,32,196]{3,2,1,0:T(8,128)(2,1)}, u32[]{:S(2)}) copy-start(bf16[64,2,32,196]{3,2,1,0:T(8,128)(2,1)} %param.8) | copy-start | bytes 4816900
  2.2 0.7 copy-start.7
  6.7 19.7 %copy-start.3 = (bf16[1,112,896]{2,1,0:T(8,128)(2,1)S(1)}, bf16[1,112,896]{2,1,0:T(8,128)(2,1)}, u32[]{:S(2)}) copy-start(bf16[1,112,896]{2,1,0:T(8,128)(2,1)} %param.6) | copy-start | bytes 602116
  6.7 59.8 %all-to-all-start = ((bf16[64,48,196]{2,1,0:T(8,128)(2,1)}), bf16[64,48,196]{2,1,0:T(8,128)(2,1)S(1)}, u32[]{:S(2)}, u32[]{:S(2)}) async-start(bf16[64,48,196]{2,1,0:T(8,128)(2,1)} %gather_fusion.1), calls=%async_computation | async-start | bytes 3145728 | tf_op jit(solution)/shard_map/all_to_all | solution.py:105
  26.4 48.8 %collective-permute-start = (bf16[1,112,896]{2,1,0:T(8,128)(2,1)S(1)}, bf16[1,112,896]{2,1,0:T(8,128)(2,1)}, u32[]{:S(2)}, u32[]{:S(2)}) collective-permute-start(bf16[1,112,896]{2,1,0:T(8,128)(2,1)S(1)} %copy-done.3), channel_id=1, source_target_pairs={{0,8},{8,16},{16,24},{24,32},{32,40},{40,48},{48,56},{56,64},{64,7... | collective-permute-start | bytes 602120 | tf_op jit(solution)/shard_map/ppermute | solution.py:14
  69.9 18.4 %copy-start.1 = (bf16[48,12544]{1,0:T(8,128)(2,1)S(1)}, bf16[48,12544]{1,0:T(8,128)(2,1)}, u32[]{:S(2)}) copy-start(bf16[48,12544]{1,0:T(8,128)(2,1)} %squeeze.55) | copy-start | bytes 3612676
  75.2 31.5 %all-to-all-start.1 = ((bf16[64,16,196]{2,1,0:T(8,128)(2,1)}), bf16[64,16,196]{2,1,0:T(8,128)(2,1)S(1)}, u32[]{:S(2)}, u32[]{:S(2)}) async-start(bf16[64,16,196]{2,1,0:T(8,128)(2,1)} %gather_fusion), calls=%async_computation.1 | async-start | bytes 1048576 | tf_op jit(solution)/shard_map/all_to_all | solution.py:105
  92.6 0.9 copy-start.4
  95.5 7.4 %copy-start = (bf16[2,32,112,112]{3,2,1,0:T(8,128)(2,1)S(1)}, bf16[2,32,112,112]{3,2,1,0:T(8,128)(2,1)}, u32[]{:S(2)}) copy-start(bf16[2,32,112,112]{3,2,1,0:T(8,128)(2,1)} %reshape_squeeze.6) | copy-start | bytes 4816900
  112.0 9.6 %copy-start.5 = (f32[64,112]{1,0:T(8,128)S(1)}, f32[64,112]{1,0:T(8,128)}, u32[]{:S(2)}) copy-start(f32[64,112]{1,0:T(8,128)} %param.10) | copy-start | bytes 86020
  112.0 24.3 %copy-start.6 = (f32[8]{0:T(128)S(1)}, f32[8]{0:T(128)}, u32[]{:S(2)}) copy-start(f32[8]{0:T(128)} %param.11) | copy-start | bytes 100
  112.3 18.0 %collective-permute-start.7 = (f32[14,896]{1,0:T(8,128)S(1)}, f32[14,896]{1,0:T(8,128)S(1)}, u32[]{:S(2)}, u32[]{:S(2)}) collective-permute-start(f32[14,896]{1,0:T(8,128)S(1)} %get-tuple-element.22), channel_id=1, source_target_pairs={{0,7},{1,0},{2,1},{3,2},{4,3},{5,4},{6,5},{7,6},{8,15},{9,8},{10,9... | collective-permute-start | bytes 150536 | tf_op jit(solution)/shard_map/ppermute | solution.py:14
  117.0 15.6 %collective-permute-start.6 = (f32[14,896]{1,0:T(8,128)S(1)}, f32[14,896]{1,0:T(8,128)S(1)}, u32[]{:S(2)}, u32[]{:S(2)}) collective-permute-start(f32[14,896]{1,0:T(8,128)S(1)} %get-tuple-element.23), channel_id=1, source_target_pairs={{0,6},{1,7},{2,0},{3,1},{4,2},{5,3},{6,4},{7,5},{8,14},{9,15},{10,... | collective-permute-start | bytes 150536 | tf_op jit(solution)/shard_map/ppermute | solution.py:14
  121.8 14.8 %collective-permute-start.5 = (f32[14,896]{1,0:T(8,128)S(1)}, f32[14,896]{1,0:T(8,128)S(1)}, u32[]{:S(2)}, u32[]{:S(2)}) collective-permute-start(f32[14,896]{1,0:T(8,128)S(1)} %get-tuple-element.24), channel_id=1, source_target_pairs={{0,5},{1,6},{2,7},{3,0},{4,1},{5,2},{6,3},{7,4},{8,13},{9,14},{10,... | collective-permute-start | bytes 150536 | tf_op jit(solution)/shard_map/ppermute | solution.py:14
  123.7 12.9 %collective-permute-start.4 = (f32[14,896]{1,0:T(8,128)S(1)}, f32[14,896]{1,0:T(8,128)S(1)}, u32[]{:S(2)}, u32[]{:S(2)}) collective-permute-start(f32[14,896]{1,0:T(8,128)S(1)} %get-tuple-element.25), channel_id=1, source_target_pairs={{0,4},{1,5},{2,6},{3,7},{4,0},{5,1},{6,2},{7,3},{8,12},{9,13},{10,... | collective-permute-start | bytes 150536 | tf_op jit(solution)/shard_map/ppermute | solution.py:14
  126.0 10.6 %collective-permute-start.3 = (f32[14,896]{1,0:T(8,128)S(1)}, f32[14,896]{1,0:T(8,128)S(1)}, u32[]{:S(2)}, u32[]{:S(2)}) collective-permute-start(f32[14,896]{1,0:T(8,128)S(1)} %get-tuple-element.26), channel_id=1, source_target_pairs={{0,3},{1,4},{2,5},{3,6},{4,7},{5,0},{6,1},{7,2},{8,11},{9,12},{10,... | collective-permute-start | bytes 150536 | tf_op jit(solution)/shard_map/ppermute | solution.py:14
  130.3 6.7 %collective-permute-start.2 = (f32[14,896]{1,0:T(8,128)S(1)}, f32[14,896]{1,0:T(8,128)S(1)}, u32[]{:S(2)}, u32[]{:S(2)}) collective-permute-start(f32[14,896]{1,0:T(8,128)S(1)} %get-tuple-element.27), channel_id=1, source_target_pairs={{0,2},{1,3},{2,4},{3,5},{4,6},{5,7},{6,0},{7,1},{8,10},{9,11},{10,... | collective-permute-start | bytes 150536 | tf_op jit(solution)/shard_map/ppermute | solution.py:14
  132.7 4.8 %collective-permute-start.1 = (f32[14,896]{1,0:T(8,128)S(1)}, f32[14,896]{1,0:T(8,128)S(1)}, u32[]{:S(2)}, u32[]{:S(2)}) collective-permute-start(f32[14,896]{1,0:T(8,128)S(1)} %get-tuple-element.21), channel_id=1, source_target_pairs={{0,1},{1,2},{2,3},{3,4},{4,5},{5,6},{6,7},{7,0},{8,9},{9,10},{10,1... | collective-permute-start | bytes 150536 | tf_op jit(solution)/shard_map/ppermute | solution.py:14

commit v9 on v7

--- a/solution.py
+++ b/solution.py
@@ -24,21 +24,23 @@
     half = jnp.dot(ct_ref[...], tt_ref[...], preferred_element_type=jnp.float32)
     half = half.astype(jnp.bfloat16)
     acc = out_ref[...]
-    for l in range(chunk):
-        rows = half[l * nv:(l + 1) * nv]
-        stacked = jnp.concatenate(
-            [rows[:, p * lanes:p * lanes + nv] for p in range(pairs)], axis=0
-        )
+    for two in range(chunk // 2):
+        stacked = []
+        for l in (2 * two, 2 * two + 1):
+            rows = half[l * nv:(l + 1) * nv]
+            stacked.append(jnp.concatenate(
+                [rows[:, p * lanes:(p + 1) * lanes] for p in range(pairs)], axis=0
+            ))
         acc = acc + lax.dot_general(
-            stacked, b_ref[l], (((1,), (1,)), ((), ())),
+            jnp.concatenate(stacked, axis=1), b_ref[two], (((1,), (1,)), ((), ())),
             preferred_element_type=jnp.float32,
         )
     out_ref[...] = acc
 
 
-def ladder_transposed(ct, tt, bq, acc, chunk=8):
+def ladder_transposed(ct, tt, bpair, acc, chunk=8):
     rows, nv = ct.shape
-    aux = bq.shape[0]
+    aux = 2 * bpair.shape[0]
     lanes = 128
     pairs = tt.shape[1] // lanes
     steps = aux // chunk
@@ -51,7 +53,7 @@
         in_specs=[
             pl.BlockSpec((chunk * nv, nv), lambda j: (j, 0)),
             pl.BlockSpec((nv, pairs * lanes), lambda j: (0, 0)),
-            pl.BlockSpec((chunk, nv, nv), lambda j: (j, 0, 0)),
+            pl.BlockSpec((chunk // 2, nv, 2 * lanes), lambda j: (j, 0, 0)),
             pl.BlockSpec((pairs * nv, nv), lambda j: (0, 0)),
         ],
         out_specs=pl.BlockSpec((pairs * nv, nv), lambda j: (0, 0)),
@@ -62,9 +64,17 @@
         ),
         cost_estimate=pl.CostEstimate(
             flops=flops, transcendentals=0,
-            bytes_accessed=2 * (ct.size + tt.size + bq.size) + 8 * pairs * nv * nv,
+            bytes_accessed=2 * (ct.size + tt.size + bpair.size) + 8 * pairs * nv * nv,
         ),
-    )(ct, tt, bq, acc)
+    )(ct, tt, bpair, acc)
+
+
+def left_pairs(left, virtuals):
+    transfers, aux = left.shape[0], left.shape[1]
+    b = left.reshape(transfers, aux // 2, 2, virtuals, virtuals)
+    b = jnp.pad(b, ((0, 0), (0, 0), (0, 0), (0, 0), (0, 128 - virtuals)))
+    b = jnp.transpose(b, (0, 1, 3, 2, 4))
+    return b.reshape(transfers, aux // 2, virtuals, 256)
 
 
 def trial_transposed(block, virtuals, pair_count):
@@ -81,7 +91,7 @@
     aux_local = left_factor.shape[2]
     pair_count = trial_vector.shape[2] // virtuals
     own_block = trial_vector[0]
-    bq = left_factor[0].reshape(transfers, aux_local, virtuals, virtuals)
+    bq = left_pairs(left_factor[0], virtuals)
     blocks = [own_block] + [
         shifted(trial_vector, "ka", transfer)[0] for transfer in range(1, transfers)
     ]
@@ -114,7 +124,7 @@
         for t, start, count in group:
             ladder_t = ladder_transposed(
                 ct[at * virtuals:(at + count) * virtuals], tts[t],
-                bq[t, start:start + count], ladder_t,
+                bq[t, start // 2:(start + count) // 2], ladder_t,
             )
             at += count
     ladder_sum = ladder_t.T

time: 136 us -> 132 us (0.971)
  Pallas kernels: 14.9 us -> 11.2 us
  waiting for transfers between devices: 47.4 us -> 44.1 us
  local copies, waits for them, and re-layouts: 26.6 us -> 29.2 us
  starting transfers between devices: 41.6 us -> 43 us
    all_to_all x2, waiting for transfers between devices: 30.2 us -> 26 us  [shards(): lax.all_to_all(piece, 'ka', split_axis=0, concat_axis=2, tiled=True)[0]]
    pallas_call x3, Pallas kernels: 14.9 us -> 11.2 us  [ladder_transposed(): pl.pallas_call(kernel, out_shape=jax.ShapeDtypeStruct((pairs * nv, nv), j...]
    all_to_all x1, starting transfers between devices: 6.68 us -> 9.04 us  [shards(): lax.all_to_all(ladder_sum.reshape(vert, slab_width, -1), 'vert', 0, 0, ti...]
    reshape x0 -> x1, local copies, waits for them, and re-layouts: none -> 2.15 us  [left_pairs(): return b.reshape(transfers, aux // 2, virtuals, 256)]
    transpose x0 -> x1, local copies, waits for them, and re-layouts: none -> 1.98 us  [left_pairs(): b = jnp.transpose(b, (0, 1, 3, 2, 4))]
    another operation x1 -> x2, local copies, waits for them, and re-layouts: 5.5 us -> 6.15 us  [left_pairs(): b = left.reshape(transfers, aux // 2, 2, virtuals, virtuals)]
  transfers between devices with their start and end apart: 4 -> 4, of which waited for: 3 -> 4; matrix products, arithmetic and copies ran while one was open for 14% -> 18% of each run, Pallas kernels for 8% -> 6%
where the time goes in v9:
time: 132 us; the launch traced here: 131 us
  waiting for transfers between devices  44.1 us (33%)
  starting transfers between devices  43 us (33%)
  local copies, waits for them, and re-layouts  29.2 us (22%)
  Pallas kernels  11.2 us (8%)
  other arithmetic  3.23 us (2%)
    all_to_all x2, starting transfers between devices, shards(): lax.all_to_all(piece, 'ka', split_axis=0, concat_axis=2, tiled=True)[0]  31.1 us
    all_to_all x2, waiting for transfers between devices, shards(): lax.all_to_all(piece, 'ka', split_axis=0, concat_axis=2, tiled=True)[0]  26 us
    all_to_all x1, waiting for transfers between devices, shards(): lax.all_to_all(ladder_sum.reshape(vert, slab_width, -1), 'vert', 0, 0, ti...  11.9 us
    pallas_call x3, Pallas kernels, ladder_transposed(): pl.pallas_call(kernel, out_shape=jax.ShapeDtypeStruct((pairs * nv, nv), j...  11.2 us
    all_to_all x1, starting transfers between devices, shards(): lax.all_to_all(ladder_sum.reshape(vert, slab_width, -1), 'vert', 0, 0, ti...  9.04 us
    another operation x2, local copies, waits for them, and re-layouts, left_pairs(): b = left.reshape(transfers, aux // 2, 2, virtuals, virtuals)  6.15 us
    ppermute x1, waiting for transfers between devices, shifted(): return lax.ppermute(value, axis, pairs)  6.14 us
    gather x2, local copies, waits for them, and re-layouts, shards(): piece = piece.at[kb_table].get(mode='promise_in_bounds')  3.16 us
  transfers between devices with their start and end apart: 4, of which 4 were waited for; matrix products, arithmetic and copies ran while one was open for 18% of the time, Pallas kernels for 6%

profile of v9, /device:TPU:1, one launch (start us, length us, event | category | flops | bytes accessed | tf_op | source)
XLA Modules:
  0.0 131.1 jit_solution(11904294678819750357)
XLA Ops:
  0.0 2.2 %slice_bitcast_fusion.2 = (bf16[64,16,196]{2,1,0:T(8,128)(2,1)S(1)}, bf16[64,16,196]{2,1,0:T(8,128)(2,1)}) fusion(bf16[64,2,32,196]{3,2,1,0:T(8,128)(2,1)} %param.8), kind=kLoop, calls=%fused_computation.6 | loop fusion | bytes 1605632 | tf_op jit(solution)/shard_map/squeeze | solution.py:107
  2.3 0.6 select_reduce_fusion.2
  3.0 0.3 pad_maximum_fusion
  3.3 1.8 %gather_fusion.1 = bf16[64,48,196]{2,1,0:T(8,128)(2,1)} fusion(bf16[64,48,196]{2,1,0:T(8,128)(2,1)S(1)} %pad_maximum_fusion, s32[1024]{0:T(1024)S(1)} %pad_clamp_fusion), kind=kCustom, calls=%fused_computation.1 | custom fusion | bytes 2408704 | tf_op jit(solution)/shard_map/gather | solution.py:109
  5.1 19.7 %all-to-all-start = ((bf16[64,48,196]{2,1,0:T(8,128)(2,1)}), bf16[64,48,196]{2,1,0:T(8,128)(2,1)S(1)}, u32[]{:S(2)}, u32[]{:S(2)}) async-start(bf16[64,48,196]{2,1,0:T(8,128)(2,1)} %gather_fusion.1), calls=%async_computation | async-start | bytes 3145728 | tf_op jit(solution)/shard_map/all_to_all | solution.py:115
  24.8 2.9 %collective-permute-start = (bf16[1,112,896]{2,1,0:T(8,128)(2,1)}, bf16[1,112,896]{2,1,0:T(8,128)(2,1)}, u32[]{:S(2)}, u32[]{:S(2)}) collective-permute-start(bf16[1,112,896]{2,1,0:T(8,128)(2,1)} %param.6), channel_id=1, source_target_pairs={{0,8},{8,16},{16,24},{24,32},{32,40},{40,48},{48,56},{56,64},{64,7... | collective-permute-start | bytes 602120 | tf_op jit(solution)/shard_map/ppermute | solution.py:14
  27.7 1.4 %gather_fusion = bf16[64,16,196]{2,1,0:T(8,128)(2,1)} fusion(bf16[64,16,196]{2,1,0:T(8,128)(2,1)S(1)} %copy-done.2, s32[1024]{0:T(1024)S(1)} %pad_clamp_fusion), kind=kCustom, calls=%fused_computation | custom fusion | bytes 803072 | tf_op jit(solution)/shard_map/gather | solution.py:109
  29.1 4.7 %reshape_squeeze.6 = bf16[2,16,2,112,112]{4,3,2,1,0:T(8,128)(2,1)S(1)} reshape(bf16[1,2,32,12544]{3,2,1,0:T(8,128)(2,1)} %param.7) | data formatting | bytes 3211264 | tf_op jit(solution)/shard_map/reshape;squeeze | solution.py:74
  33.8 1.4 %copy.23 = bf16[2,16,2,112,112]{4,2,3,1,0:T(2,128)(2,1)S(1)} copy(bf16[2,16,2,112,112]{4,3,2,1,0:T(8,128)(2,1)S(1)} %reshape_squeeze.6) | data formatting | bytes 3211264 | tf_op jit(solution)/shard_map/reshape;squeeze | solution.py:74
  35.3 2.0 %pad_bitcast_fusion = bf16[2,16,112,2,128]{4,3,2,1,0:T(2,128)(2,1)S(1)} fusion(bf16[2,16,2,112,112]{4,2,3,1,0:T(2,128)(2,1)S(1)} %copy.23), kind=kLoop, calls=%fused_computation.2 | loop fusion | bytes 3440640 | tf_op jit(solution)/shard_map/transpose | solution.py:76
  37.3 2.1 %reshape.108 = bf16[2,16,112,256]{3,2,1,0:T(8,128)(2,1)} reshape(bf16[2,16,112,2,128]{4,3,2,1,0:T(2,128)(2,1)S(1)} %pad_bitcast_fusion) | data formatting | bytes 3670016 | tf_op jit(solution)/shard_map/reshape | solution.py:77
  39.4 25.4 %all-to-all-done = bf16[64,48,196]{2,1,0:T(8,128)(2,1)S(1)} async-done(((bf16[64,48,196]{2,1,0:T(8,128)(2,1)}), bf16[64,48,196]{2,1,0:T(8,128)(2,1)S(1)}, u32[]{:S(2)}, u32[]{:S(2)}) %all-to-all-start) | async-done | bytes 1204256 | tf_op jit(solution)/shard_map/all_to_all | solution.py:115
  64.8 0.5 copy.22
  65.4 2.1 %squeeze.30 = bf16[48,12544]{1,0:T(8,128)(2,1)S(1)} reshape(bf16[1,48,64,196]{3,2,1,0:T(8,128)(2,1)S(1)} %copy.22) | data formatting | bytes 2408448 | tf_op jit(solution)/shard_map/squeeze | solution.py:115
  67.5 6.1 %collective-permute-done = bf16[1,112,896]{2,1,0:T(8,128)(2,1)} collective-permute-done((bf16[1,112,896]{2,1,0:T(8,128)(2,1)}, bf16[1,112,896]{2,1,0:T(8,128)(2,1)}, u32[]{:S(2)}, u32[]{:S(2)}) %collective-permute-start) | collective-permute-done | bytes 200736 | tf_op jit(solution)/shard_map/ppermute | solution.py:14
  73.6 11.4 %all-to-all-start.1 = ((bf16[64,16,196]{2,1,0:T(8,128)(2,1)}), bf16[64,16,196]{2,1,0:T(8,128)(2,1)S(1)}, u32[]{:S(2)}, u32[]{:S(2)}) async-start(bf16[64,16,196]{2,1,0:T(8,128)(2,1)} %gather_fusion), calls=%async_computation.1 | async-start | bytes 1048576 | tf_op jit(solution)/shard_map/all_to_all | solution.py:115
  85.0 2.7 %reshape.112 = bf16[48,112,112]{2,1,0:T(8,128)(2,1)S(1)} reshape(bf16[48,12544]{1,0:T(8,128)(2,1)S(1)} %squeeze.30) | data formatting | bytes 2408448 | tf_op jit(solution)/shard_map/reshape | solution.py:121
  87.8 1.2 reshape.110
  89.4 0.2 copy.27
  89.6 0.6 copy.28
  90.2 1.2 reshape.113
  91.7 1.2 slice_bitcast_fusion.1.b_ref
  93.0 5.6 %shard_map.64.acc_ref = f32[896,112]{1,0:T(8,128)S(1)} custom-call(bf16[3584,112]{1,0:T(8,128)(2,1)S(1)} %bitcast.49, bf16[112,1024]{1,0:T(8,128)(2,1)S(1)} %bitcast.54, bf16[16,112,256]{2,1,0:T(8,128)(2,1)S(1)} %slice_bitcast_fusion.1.b_ref, f32[896,112]{1,0:T(8,128)S(1)} %broadcast_in_dim.34.clone.acc_ref), custom_call_target="tpu_custom_call", output_to_operand_aliasing={{}: (3, {})} | custom-call | flops 1541406720 | bytes 2752512 | tf_op jit(solution)/shard_map/pallas_call | solution.py:49
  98.7 2.8 %shard_map.65.acc_ref = f32[896,112]{1,0:T(8,128)S(1)} custom-call(bf16[1792,112]{1,0:T(8,128)(2,1)S(1)} %bitcast.50, bf16[112,1024]{1,0:T(8,128)(2,1)S(1)} %bitcast.52, bf16[8,112,256]{2,1,0:T(8,128)(2,1)S(1)} %get-tuple-element.19.b_ref, f32[896,112]{1,0:T(8,128)S(1)} %shard_map.64.acc_ref), custom_call_target="tpu_custom_call", output_to_operand_aliasing={{}: (3, {})} | custom-call | flops 770703360 | bytes 1892352 | tf_op jit(solution)/shard_map/pallas_call | solution.py:49
  101.5 0.6 all-to-all-done.1
  102.3 1.1 reshape_squeeze.7
  103.6 2.8 %shard_map.66 = f32[896,112]{1,0:T(8,128)S(1)} custom-call(bf16[1792,112]{1,0:T(8,128)(2,1)S(1)} %bitcast.51, bf16[112,1024]{1,0:T(8,128)(2,1)S(1)} %bitcast.53, bf16[8,112,256]{2,1,0:T(8,128)(2,1)S(1)} %get-tuple-element.20.b_ref, f32[896,112]{1,0:T(8,128)S(1)} %shard_map.65.acc_ref), custom_call_target="tpu_custom_call", output_to_operand_aliasing={{}: (3, {})} | custom-call | flops 770703360 | bytes 1892352 | tf_op jit(solution)/shard_map/pallas_call | solution.py:49
  106.6 0.8 reshape.115
  107.5 9.0 %all-to-all-start.2 = ((f32[8,14,896]{2,1,0:T(8,128)}), f32[8,14,896]{2,1,0:T(8,128)S(1)}, u32[]{:S(2)}, u32[]{:S(2)}) async-start(f32[8,14,896]{2,1,0:T(8,128)} %reshape.115), calls=%async_computation.2 | async-start | bytes 917504 | tf_op jit(solution)/shard_map/all_to_all | solution.py:133
  116.5 0.6 iota_compare_fusion
  117.7 11.9 %all-to-all-done.2 = f32[8,14,896]{2,1,0:T(8,128)S(1)} async-done(((f32[8,14,896]{2,1,0:T(8,128)}), f32[8,14,896]{2,1,0:T(8,128)S(1)}, u32[]{:S(2)}, u32[]{:S(2)}) %all-to-all-start.2) | async-done | bytes 401440 | tf_op jit(solution)/shard_map/all_to_all | solution.py:133
  129.6 1.4 %fusion = bf16[1,14,896]{2,1,0:T(8,128)(2,1)} fusion(f32[14,896]{1,0:T(8,128)S(1)} %reduce_sum.38, f32[1,14,896]{2,1,0:T(8,128)S(1)} %sub.28, bf16[1,112,896]{2,1,0:T(8,128)(2,1)} %param.6, s32[]{:T(128)S(6)} %select_n.21, f32[896]{0:T(1024)S(1)} %sub.30), kind=kLoop, calls=%fused_computation.13 | loop fusion | flops 62720 | bytes 154116 | tf_op jit(solution)/shard_map/convert_element_type | solution.py:149
  (36 shorter events, 2.0 us)
Async XLA Ops:
  0.0 2.2 %copy-start.1 = (bf16[64,2,32,196]{3,2,1,0:T(8,128)(2,1)S(1)}, bf16[64,2,32,196]{3,2,1,0:T(8,128)(2,1)}, u32[]{:S(2)}) copy-start(bf16[64,2,32,196]{3,2,1,0:T(8,128)(2,1)} %param.8) | copy-start | bytes 4816900
  0.0 2.3 %copy-start.5 = (s32[64]{0:T(128)S(1)}, s32[64]{0:T(128)}, u32[]{:S(2)}) copy-start(s32[64]{0:T(128)} %param.9) | copy-start | bytes 772
  5.1 22.6 %copy-start.2 = (bf16[64,16,196]{2,1,0:T(8,128)(2,1)S(1)}, bf16[64,16,196]{2,1,0:T(8,128)(2,1)}, u32[]{:S(2)}) copy-start(bf16[64,16,196]{2,1,0:T(8,128)(2,1)} %get-tuple-element.18) | copy-start | bytes 1204228
  5.1 59.8 %all-to-all-start = ((bf16[64,48,196]{2,1,0:T(8,128)(2,1)}), bf16[64,48,196]{2,1,0:T(8,128)(2,1)S(1)}, u32[]{:S(2)}, u32[]{:S(2)}) async-start(bf16[64,48,196]{2,1,0:T(8,128)(2,1)} %gather_fusion.1), calls=%async_computation | async-start | bytes 3145728 | tf_op jit(solution)/shard_map/all_to_all | solution.py:115
  24.8 48.8 %collective-permute-start = (bf16[1,112,896]{2,1,0:T(8,128)(2,1)}, bf16[1,112,896]{2,1,0:T(8,128)(2,1)}, u32[]{:S(2)}, u32[]{:S(2)}) collective-permute-start(bf16[1,112,896]{2,1,0:T(8,128)(2,1)} %param.6), channel_id=1, source_target_pairs={{0,8},{8,16},{16,24},{24,32},{32,40},{40,48},{48,56},{56,64},{64,7... | collective-permute-start | bytes 602120 | tf_op jit(solution)/shard_map/ppermute | solution.py:14
  73.6 28.5 %all-to-all-start.1 = ((bf16[64,16,196]{2,1,0:T(8,128)(2,1)}), bf16[64,16,196]{2,1,0:T(8,128)(2,1)S(1)}, u32[]{:S(2)}, u32[]{:S(2)}) async-start(bf16[64,16,196]{2,1,0:T(8,128)(2,1)} %gather_fusion), calls=%async_computation.1 | async-start | bytes 1048576 | tf_op jit(solution)/shard_map/all_to_all | solution.py:115
  93.0 5.6 %copy-start = (bf16[2,16,112,256]{3,2,1,0:T(8,128)(2,1)S(1)}, bf16[2,16,112,256]{3,2,1,0:T(8,128)(2,1)}, u32[]{:S(2)}) copy-start(bf16[2,16,112,256]{3,2,1,0:T(8,128)(2,1)} %reshape.108) | copy-start | bytes 5505028
  106.4 10.7 %copy-start.3 = (f32[64,112]{1,0:T(8,128)S(1)}, f32[64,112]{1,0:T(8,128)}, u32[]{:S(2)}) copy-start(f32[64,112]{1,0:T(8,128)} %param.10) | copy-start | bytes 86020
  106.4 11.1 %copy-start.4 = (f32[8]{0:T(128)S(1)}, f32[8]{0:T(128)}, u32[]{:S(2)}) copy-start(f32[8]{0:T(128)} %param.11) | copy-start | bytes 100
  107.5 22.1 %all-to-all-start.2 = ((f32[8,14,896]{2,1,0:T(8,128)}), f32[8,14,896]{2,1,0:T(8,128)S(1)}, u32[]{:S(2)}, u32[]{:S(2)}) async-start(f32[8,14,896]{2,1,0:T(8,128)} %reshape.115), calls=%async_computation.2 | async-start | bytes 917504 | tf_op jit(solution)/shard_map/all_to_all | solution.py:133

commit v10 on v9

--- a/solution.py
+++ b/solution.py
@@ -108,9 +108,9 @@
         )
         piece = piece.at[kb_table].get(mode="promise_in_bounds")
         if arrivals:
-            piece, arrivals[-1], bq, blocks = lax.optimization_barrier(
-                (piece, arrivals[-1], bq, blocks)
-            )
+            piece, arrivals[-1], bq = lax.optimization_barrier((piece, arrivals[-1], bq))
+        else:
+            piece, blocks = lax.optimization_barrier((piece, blocks))
         arrivals.append(
             lax.all_to_all(piece, "ka", split_axis=0, concat_axis=2, tiled=True)[0]
         )

time: 132 us -> 135 us (1.023)
  waiting for transfers between devices: 44.1 us -> 51.1 us
  starting transfers between devices: 43 us -> 37 us
  local copies, waits for them, and re-layouts: 29.2 us -> 31 us
    all_to_all x2, starting transfers between devices: 31.1 us -> 23.2 us  [shards(): lax.all_to_all(piece, 'ka', split_axis=0, concat_axis=2, tiled=True)[0]]
    ppermute x1, waiting for transfers between devices: 6.14 us -> 12.4 us  [shifted(): return lax.ppermute(value, axis, pairs)]
    slice x4, local copies, waits for them, and re-layouts: 0.91 us -> 2.68 us  [shards(): ct[at * virtuals:(at + count) * virtuals]]
  transfers between devices with their start and end apart: 4 -> 4, of which waited for: 4 -> 3; matrix products, arithmetic and copies ran while one was open for 18% -> 21% of each run, Pallas kernels for 6% -> 6%
where the time goes in v10:
time: 135 us; the launch traced here: 134 us
  waiting for transfers between devices  51.1 us (38%)
  starting transfers between devices  37 us (27%)
  local copies, waits for them, and re-layouts  31 us (23%)
  Pallas kernels  11.2 us (8%)
  other arithmetic  3.51 us (3%)
    all_to_all x2, waiting for transfers between devices, shards(): lax.all_to_all(piece, 'ka', split_axis=0, concat_axis=2, tiled=True)[0]  26.8 us
    all_to_all x2, starting transfers between devices, shards(): lax.all_to_all(piece, 'ka', split_axis=0, concat_axis=2, tiled=True)[0]  23.2 us
    ppermute x1, waiting for transfers between devices, shifted(): return lax.ppermute(value, axis, pairs)  12.4 us
    all_to_all x1, waiting for transfers between devices, shards(): lax.all_to_all(ladder_sum.reshape(vert, slab_width, -1), 'vert', 0, 0, ti...  11.9 us
    pallas_call x3, Pallas kernels, ladder_transposed(): pl.pallas_call(kernel, out_shape=jax.ShapeDtypeStruct((pairs * nv, nv), j...  11.2 us
    all_to_all x1, starting transfers between devices, shards(): lax.all_to_all(ladder_sum.reshape(vert, slab_width, -1), 'vert', 0, 0, ti...  9.71 us
    another operation x2, local copies, waits for them, and re-layouts, left_pairs(): b = left.reshape(transfers, aux // 2, 2, virtuals, virtuals)  6.15 us
    ppermute x1, starting transfers between devices, shifted(): return lax.ppermute(value, axis, pairs)  4.07 us
  transfers between devices with their start and end apart: 4, of which 3 were waited for; matrix products, arithmetic and copies ran while one was open for 21% of the time, Pallas kernels for 6%

profile of v10, /device:TPU:1, one launch (start us, length us, event | category | flops | bytes accessed | tf_op | source)
XLA Modules:
  0.0 134.1 jit_solution(10402316977095001947)
XLA Ops:
  0.0 4.1 %collective-permute-start = (bf16[1,112,896]{2,1,0:T(8,128)(2,1)}, bf16[1,112,896]{2,1,0:T(8,128)(2,1)S(1)}, u32[]{:S(2)}, u32[]{:S(2)}) collective-permute-start(bf16[1,112,896]{2,1,0:T(8,128)(2,1)} %param.6), channel_id=1, source_target_pairs={{0,8},{8,16},{16,24},{24,32},{32,40},{40,48},{48,56},{56,64},{64,7... | collective-permute-start | bytes 602120 | tf_op jit(solution)/shard_map/ppermute | solution.py:14
  4.1 2.1 %slice_bitcast_fusion.2 = (bf16[64,16,196]{2,1,0:T(8,128)(2,1)}, bf16[64,16,196]{2,1,0:T(8,128)(2,1)S(1)}) fusion(bf16[64,2,32,196]{3,2,1,0:T(8,128)(2,1)} %param.8), kind=kLoop, calls=%fused_computation.6 | loop fusion | bytes 1605632 | tf_op jit(solution)/shard_map/squeeze | solution.py:107
  6.3 0.6 select_reduce_fusion.2
  6.9 1.4 %pad_maximum_fusion = bf16[64,48,196]{2,1,0:T(8,128)(2,1)S(1)} fusion(bf16[64,16,196]{2,1,0:T(8,128)(2,1)} %get-tuple-element.19, bf16[64,32,196]{2,1,0:T(8,128)(2,1)S(1)} %slice_bitcast_fusion), kind=kLoop, calls=%fused_computation.3 | loop fusion | flops 2408448 | bytes 2408448 | tf_op jit(solution)/shard_map/concatenate | solution.py:106
  8.3 1.8 %gather_fusion.1 = bf16[64,48,196]{2,1,0:T(8,128)(2,1)} fusion(bf16[64,48,196]{2,1,0:T(8,128)(2,1)S(1)} %pad_maximum_fusion, s32[1024]{0:T(1024)S(1)} %pad_clamp_fusion), kind=kCustom, calls=%fused_computation.1 | custom fusion | bytes 2408704 | tf_op jit(solution)/shard_map/gather | solution.py:109
  10.1 12.4 %collective-permute-done = bf16[1,112,896]{2,1,0:T(8,128)(2,1)S(1)} collective-permute-done((bf16[1,112,896]{2,1,0:T(8,128)(2,1)}, bf16[1,112,896]{2,1,0:T(8,128)(2,1)S(1)}, u32[]{:S(2)}, u32[]{:S(2)}) %collective-permute-start) | collective-permute-done | bytes 200736 | tf_op jit(solution)/shard_map/ppermute | solution.py:14
  22.5 12.6 %all-to-all-start = ((bf16[64,48,196]{2,1,0:T(8,128)(2,1)}), bf16[64,48,196]{2,1,0:T(8,128)(2,1)S(1)}, u32[]{:S(2)}, u32[]{:S(2)}) async-start(bf16[64,48,196]{2,1,0:T(8,128)(2,1)} %gather_fusion.1), calls=%async_computation | async-start | bytes 3145728 | tf_op jit(solution)/shard_map/all_to_all | solution.py:115
  35.1 1.4 %gather_fusion = bf16[64,16,196]{2,1,0:T(8,128)(2,1)} fusion(bf16[64,16,196]{2,1,0:T(8,128)(2,1)S(1)} %get-tuple-element.20, s32[1024]{0:T(1024)S(1)} %pad_clamp_fusion), kind=kCustom, calls=%fused_computation | custom fusion | bytes 803072 | tf_op jit(solution)/shard_map/gather | solution.py:109
  36.5 4.7 %reshape_squeeze.6 = bf16[2,16,2,112,112]{4,3,2,1,0:T(8,128)(2,1)S(1)} reshape(bf16[1,2,32,12544]{3,2,1,0:T(8,128)(2,1)} %param.7) | data formatting | bytes 3211264 | tf_op jit(solution)/shard_map/reshape;squeeze | solution.py:74
  41.2 1.4 %copy.23 = bf16[2,16,2,112,112]{4,2,3,1,0:T(2,128)(2,1)S(1)} copy(bf16[2,16,2,112,112]{4,3,2,1,0:T(8,128)(2,1)S(1)} %reshape_squeeze.6) | data formatting | bytes 3211264 | tf_op jit(solution)/shard_map/reshape;squeeze | solution.py:74
  42.6 2.0 %pad_bitcast_fusion = bf16[2,16,112,2,128]{4,3,2,1,0:T(2,128)(2,1)S(1)} fusion(bf16[2,16,2,112,112]{4,2,3,1,0:T(2,128)(2,1)S(1)} %copy.23), kind=kLoop, calls=%fused_computation.2 | loop fusion | bytes 3440640 | tf_op jit(solution)/shard_map/transpose | solution.py:76
  44.6 2.2 %reshape.108 = bf16[2,16,112,256]{3,2,1,0:T(8,128)(2,1)} reshape(bf16[2,16,112,2,128]{4,3,2,1,0:T(2,128)(2,1)S(1)} %pad_bitcast_fusion) | data formatting | bytes 3670016 | tf_op jit(solution)/shard_map/reshape | solution.py:77
  46.8 26.8 %all-to-all-done = bf16[64,48,196]{2,1,0:T(8,128)(2,1)S(1)} async-done(((bf16[64,48,196]{2,1,0:T(8,128)(2,1)}), bf16[64,48,196]{2,1,0:T(8,128)(2,1)S(1)}, u32[]{:S(2)}, u32[]{:S(2)}) %all-to-all-start) | async-done | bytes 1204256 | tf_op jit(solution)/shard_map/all_to_all | solution.py:115
  73.6 0.5 copy.22
  74.1 2.1 %squeeze.32 = bf16[48,12544]{1,0:T(8,128)(2,1)S(1)} reshape(bf16[1,48,64,196]{3,2,1,0:T(8,128)(2,1)S(1)} %copy.22) | data formatting | bytes 2408448 | tf_op jit(solution)/shard_map/squeeze | solution.py:115
  76.3 10.6 %all-to-all-start.1 = ((bf16[64,16,196]{2,1,0:T(8,128)(2,1)}), bf16[64,16,196]{2,1,0:T(8,128)(2,1)}, u32[]{:S(2)}, u32[]{:S(2)}) async-start(bf16[64,16,196]{2,1,0:T(8,128)(2,1)} %gather_fusion), calls=%async_computation.1 | async-start | bytes 1048576 | tf_op jit(solution)/shard_map/all_to_all | solution.py:115
  86.9 1.2 reshape.110
  89.0 2.7 %reshape.112 = bf16[48,112,112]{2,1,0:T(8,128)(2,1)S(1)} reshape(bf16[48,12544]{1,0:T(8,128)(2,1)S(1)} %squeeze.32) | data formatting | bytes 2408448 | tf_op jit(solution)/shard_map/reshape | solution.py:121
  91.8 0.8 slice.44
  92.6 1.3 copy.27
  93.9 0.6 copy.28
  94.5 1.2 slice_bitcast_fusion.1.b_ref
  95.7 5.6 %shard_map.64.acc_ref = f32[896,112]{1,0:T(8,128)S(1)} custom-call(bf16[3584,112]{1,0:T(8,128)(2,1)S(1)} %bitcast.49, bf16[112,1024]{1,0:T(8,128)(2,1)S(1)} %bitcast.54, bf16[16,112,256]{2,1,0:T(8,128)(2,1)S(1)} %slice_bitcast_fusion.1.b_ref, f32[896,112]{1,0:T(8,128)S(1)} %broadcast_in_dim.34.clone.acc_ref), custom_call_target="tpu_custom_call", output_to_operand_aliasing={{}: (3, {})} | custom-call | flops 1541406720 | bytes 2752512 | tf_op jit(solution)/shard_map/pallas_call | solution.py:49
  101.4 2.8 %shard_map.65.acc_ref = f32[896,112]{1,0:T(8,128)S(1)} custom-call(bf16[1792,112]{1,0:T(8,128)(2,1)S(1)} %bitcast.50, bf16[112,1024]{1,0:T(8,128)(2,1)S(1)} %bitcast.52, bf16[8,112,256]{2,1,0:T(8,128)(2,1)S(1)} %get-tuple-element.21.b_ref, f32[896,112]{1,0:T(8,128)S(1)} %shard_map.64.acc_ref), custom_call_target="tpu_custom_call", output_to_operand_aliasing={{}: (3, {})} | custom-call | flops 770703360 | bytes 1892352 | tf_op jit(solution)/shard_map/pallas_call | solution.py:49
  104.3 1.2 copy.24
  105.5 1.1 reshape_squeeze.7
  106.8 2.8 %shard_map.66 = f32[896,112]{1,0:T(8,128)S(1)} custom-call(bf16[1792,112]{1,0:T(8,128)(2,1)S(1)} %bitcast.51, bf16[112,1024]{1,0:T(8,128)(2,1)S(1)} %bitcast.53, bf16[8,112,256]{2,1,0:T(8,128)(2,1)S(1)} %get-tuple-element.22.b_ref, f32[896,112]{1,0:T(8,128)S(1)} %shard_map.65.acc_ref), custom_call_target="tpu_custom_call", output_to_operand_aliasing={{}: (3, {})} | custom-call | flops 770703360 | bytes 1892352 | tf_op jit(solution)/shard_map/pallas_call | solution.py:49
  109.8 0.8 reshape.115
  110.6 9.7 %all-to-all-start.2 = ((f32[8,14,896]{2,1,0:T(8,128)}), f32[8,14,896]{2,1,0:T(8,128)S(1)}, u32[]{:S(2)}, u32[]{:S(2)}) async-start(f32[8,14,896]{2,1,0:T(8,128)} %reshape.115), calls=%async_computation.2 | async-start | bytes 917504 | tf_op jit(solution)/shard_map/all_to_all | solution.py:133
  120.3 0.6 iota_compare_fusion
  121.5 11.9 %all-to-all-done.2 = f32[8,14,896]{2,1,0:T(8,128)S(1)} async-done(((f32[8,14,896]{2,1,0:T(8,128)}), f32[8,14,896]{2,1,0:T(8,128)S(1)}, u32[]{:S(2)}, u32[]{:S(2)}) %all-to-all-start.2) | async-done | bytes 401440 | tf_op jit(solution)/shard_map/all_to_all | solution.py:133
  133.5 0.6 fusion
  (37 shorter events, 2.1 us)
Async XLA Ops:
  0.0 6.2 %copy-start.1 = (bf16[64,2,32,196]{3,2,1,0:T(8,128)(2,1)S(1)}, bf16[64,2,32,196]{3,2,1,0:T(8,128)(2,1)}, u32[]{:S(2)}) copy-start(bf16[64,2,32,196]{3,2,1,0:T(8,128)(2,1)} %param.8) | copy-start | bytes 4816900
  0.0 22.5 %collective-permute-start = (bf16[1,112,896]{2,1,0:T(8,128)(2,1)}, bf16[1,112,896]{2,1,0:T(8,128)(2,1)S(1)}, u32[]{:S(2)}, u32[]{:S(2)}) collective-permute-start(bf16[1,112,896]{2,1,0:T(8,128)(2,1)} %param.6), channel_id=1, source_target_pairs={{0,8},{8,16},{16,24},{24,32},{32,40},{40,48},{48,56},{56,64},{64,7... | collective-permute-start | bytes 602120 | tf_op jit(solution)/shard_map/ppermute | solution.py:14
  4.1 2.2 %copy-start.6 = (s32[64]{0:T(128)S(1)}, s32[64]{0:T(128)}, u32[]{:S(2)}) copy-start(s32[64]{0:T(128)} %param.9) | copy-start | bytes 772
  22.5 12.6 %copy-start.3 = (bf16[1,112,896]{2,1,0:T(8,128)(2,1)}, bf16[1,112,896]{2,1,0:T(8,128)(2,1)S(1)}, u32[]{:S(2)}) copy-start(bf16[1,112,896]{2,1,0:T(8,128)(2,1)S(1)} %collective-permute-done) | copy-start | bytes 602116
  22.5 51.1 %all-to-all-start = ((bf16[64,48,196]{2,1,0:T(8,128)(2,1)}), bf16[64,48,196]{2,1,0:T(8,128)(2,1)S(1)}, u32[]{:S(2)}, u32[]{:S(2)}) async-start(bf16[64,48,196]{2,1,0:T(8,128)(2,1)} %gather_fusion.1), calls=%async_computation | async-start | bytes 3145728 | tf_op jit(solution)/shard_map/all_to_all | solution.py:115
  76.3 12.1 %copy-start.2 = (bf16[1,112,896]{2,1,0:T(8,128)(2,1)S(1)}, bf16[1,112,896]{2,1,0:T(8,128)(2,1)}, u32[]{:S(2)}) copy-start(bf16[1,112,896]{2,1,0:T(8,128)(2,1)} %param.6) | copy-start | bytes 602116
  76.3 28.0 %all-to-all-start.1 = ((bf16[64,16,196]{2,1,0:T(8,128)(2,1)}), bf16[64,16,196]{2,1,0:T(8,128)(2,1)}, u32[]{:S(2)}, u32[]{:S(2)}) async-start(bf16[64,16,196]{2,1,0:T(8,128)(2,1)} %gather_fusion), calls=%async_computation.1 | async-start | bytes 1048576 | tf_op jit(solution)/shard_map/all_to_all | solution.py:115
  95.7 5.6 %copy-start = (bf16[2,16,112,256]{3,2,1,0:T(8,128)(2,1)S(1)}, bf16[2,16,112,256]{3,2,1,0:T(8,128)(2,1)}, u32[]{:S(2)}) copy-start(bf16[2,16,112,256]{3,2,1,0:T(8,128)(2,1)} %reshape.108) | copy-start | bytes 5505028
  109.6 11.4 %copy-start.4 = (f32[64,112]{1,0:T(8,128)S(1)}, f32[64,112]{1,0:T(8,128)}, u32[]{:S(2)}) copy-start(f32[64,112]{1,0:T(8,128)} %param.10) | copy-start | bytes 86020
  109.6 11.8 %copy-start.5 = (f32[8]{0:T(128)S(1)}, f32[8]{0:T(128)}, u32[]{:S(2)}) copy-start(f32[8]{0:T(128)} %param.11) | copy-start | bytes 100
  110.6 22.8 %all-to-all-start.2 = ((f32[8,14,896]{2,1,0:T(8,128)}), f32[8,14,896]{2,1,0:T(8,128)S(1)}, u32[]{:S(2)}, u32[]{:S(2)}) async-start(f32[8,14,896]{2,1,0:T(8,128)} %reshape.115), calls=%async_computation.2 | async-start | bytes 917504 | tf_op jit(solution)/shard_map/all_to_all | solution.py:133

commit v11 on v9

--- a/solution.py
+++ b/solution.py
@@ -128,12 +128,13 @@
             )
             at += count
     ladder_sum = ladder_t.T
-    vert = lax.axis_size("vert")
+    vert = lax.axis_size(("zl", "core"))
     slab_width = virtuals // vert
-    ladder = lax.all_to_all(
-        ladder_sum.reshape(vert, slab_width, -1), "vert", 0, 0, tiled=True
-    ).sum(0)
-    offset = lax.axis_index("vert") * slab_width
+    cores = lax.axis_size("core")
+    stacked = ladder_sum.reshape(vert // cores, cores, slab_width, -1)
+    stacked = lax.all_to_all(stacked, "core", 1, 1, tiled=True).sum(1)
+    ladder = lax.all_to_all(stacked, "zl", 0, 0, tiled=True).sum(0)
+    offset = lax.axis_index(("zl", "core")) * slab_width
     labels = jnp.arange(kpoints, dtype=jnp.int32)
     owner_index = lax.axis_index("ka")
     momentum_b = jnp.sum(jnp.where(labels == owner_index, kb_table, 0))
@@ -150,13 +151,19 @@
 
 
 def solution(mesh):
+    kpoints, vert = mesh.devices.shape
+    cores = 2
+    split = jax.sharding.Mesh(
+        mesh.devices.reshape(kpoints, vert // cores, cores), ("ka", "zl", "core")
+    )
+    slab = ("zl", "core")
     in_specs = (
         P("ka", None, None),
-        P("ka", None, "vert", None),
-        P(None, None, "vert", "ka"),
+        P("ka", None, slab, None),
+        P(None, None, slab, "ka"),
         P(),
         P(),
         P(),
     )
-    out_specs = P("ka", "vert", None)
-    return jax.shard_map(shards, mesh=mesh, in_specs=in_specs, out_specs=out_specs, check_vma=False)
+    out_specs = P("ka", slab, None)
+    return jax.shard_map(shards, mesh=split, in_specs=in_specs, out_specs=out_specs, check_vma=False)

time: 132 us -> 130 us (0.985); the launches traced: 131 us -> 128 us
  blocking collectives: 0 us -> 8.43 us
  waiting for transfers between devices: 44.1 us -> 36 us
  starting transfers between devices: 43 us -> 37.7 us
    all_to_all x0 -> x1, blocking collectives: none -> 8.43 us  [shards(): stacked = lax.all_to_all(stacked, 'core', 1, 1, tiled=True).sum(1)]
    all_to_all x1, waiting for transfers between devices: 11.9 us -> 5.49 us  [shards(): ladder = lax.all_to_all(stacked, 'zl', 0, 0, tiled=True).sum(0)]
    all_to_all x1, starting transfers between devices: 9.04 us -> 3.89 us  [shards(): ladder = lax.all_to_all(stacked, 'zl', 0, 0, tiled=True).sum(0)]
    all_to_all x2, waiting for transfers between devices: 26 us -> 24.4 us  [shards(): lax.all_to_all(piece, 'ka', split_axis=0, concat_axis=2, tiled=True)[0]]
  transfers between devices with their start and end apart: 4 -> 4, of which waited for: 4 -> 3; matrix products, arithmetic and copies ran while one was open for 18% -> 19% of each run, Pallas kernels for 6% -> 7%
where the time goes in v11:
time: 130 us; the launch traced here: 128 us
  starting transfers between devices  37.7 us (29%)
  waiting for transfers between devices  36 us (28%)
  local copies, waits for them, and re-layouts  30.4 us (23%)
  Pallas kernels  11.2 us (9%)
  blocking collectives  8.43 us (6%)
  other arithmetic  3.34 us (3%)
    all_to_all x2, starting transfers between devices, shards(): lax.all_to_all(piece, 'ka', split_axis=0, concat_axis=2, tiled=True)[0]  30.9 us
    all_to_all x2, waiting for transfers between devices, shards(): lax.all_to_all(piece, 'ka', split_axis=0, concat_axis=2, tiled=True)[0]  24.4 us
    pallas_call x3, Pallas kernels, ladder_transposed(): pl.pallas_call(kernel, out_shape=jax.ShapeDtypeStruct((pairs * nv, nv), j...  11.2 us
    all_to_all x1, blocking collectives, shards(): stacked = lax.all_to_all(stacked, 'core', 1, 1, tiled=True).sum(1)  8.43 us
    another operation x2, local copies, waits for them, and re-layouts, left_pairs(): b = left.reshape(transfers, aux // 2, 2, virtuals, virtuals)  6.16 us
    ppermute x1, waiting for transfers between devices, shifted(): return lax.ppermute(value, axis, pairs)  6.14 us
    all_to_all x1, waiting for transfers between devices, shards(): ladder = lax.all_to_all(stacked, 'zl', 0, 0, tiled=True).sum(0)  5.49 us
    gather x2, local copies, waits for them, and re-layouts, shards(): piece = piece.at[kb_table].get(mode='promise_in_bounds')  4.22 us
  transfers between devices with their start and end apart: 4, of which 3 were waited for; matrix products, arithmetic and copies ran while one was open for 19% of the time, Pallas kernels for 7%

profile of v11, /device:TPU:1, one launch (start us, length us, event | category | flops | bytes accessed | tf_op | source)
XLA Modules:
  0.0 127.5 jit_solution(14421977799007039801)
XLA Ops:
  0.0 2.2 %slice_bitcast_fusion.2 = (bf16[64,16,196]{2,1,0:T(8,128)(2,1)S(1)}, bf16[64,16,196]{2,1,0:T(8,128)(2,1)}) fusion(bf16[64,2,32,196]{3,2,1,0:T(8,128)(2,1)} %param.8), kind=kLoop, calls=%fused_computation.6 | loop fusion | bytes 1605632 | tf_op jit(solution)/shard_map/squeeze | solution.py:107
  2.3 0.6 select_reduce_fusion.2
  3.0 0.3 pad_maximum_fusion
  3.3 1.8 %gather_fusion.1 = bf16[64,48,196]{2,1,0:T(8,128)(2,1)} fusion(bf16[64,48,196]{2,1,0:T(8,128)(2,1)S(1)} %pad_maximum_fusion, s32[1024]{0:T(1024)S(1)} %pad_clamp_fusion), kind=kCustom, calls=%fused_computation.1 | custom fusion | bytes 2408704 | tf_op jit(solution)/shard_map/gather | solution.py:109
  5.1 19.6 %all-to-all-start = ((bf16[64,48,196]{2,1,0:T(8,128)(2,1)}), bf16[64,48,196]{2,1,0:T(8,128)(2,1)S(1)}, u32[]{:S(2)}, u32[]{:S(2)}) async-start(bf16[64,48,196]{2,1,0:T(8,128)(2,1)} %gather_fusion.1), calls=%async_computation | async-start | bytes 3145728 | tf_op jit(solution)/shard_map/all_to_all | solution.py:115
  24.6 2.9 %collective-permute-start = (bf16[1,112,896]{2,1,0:T(8,128)(2,1)}, bf16[1,112,896]{2,1,0:T(8,128)(2,1)}, u32[]{:S(2)}, u32[]{:S(2)}) collective-permute-start(bf16[1,112,896]{2,1,0:T(8,128)(2,1)} %param.6), channel_id=1, source_target_pairs={{0,8},{8,16},{16,24},{24,32},{32,40},{40,48},{48,56},{56,64},{64,7... | collective-permute-start | bytes 602120 | tf_op jit(solution)/shard_map/ppermute | solution.py:14
  27.6 4.7 %reshape_squeeze.6 = bf16[2,16,2,112,112]{4,3,2,1,0:T(8,128)(2,1)S(1)} reshape(bf16[1,2,32,12544]{3,2,1,0:T(8,128)(2,1)} %param.7) | data formatting | bytes 3211264 | tf_op jit(solution)/shard_map/reshape;squeeze | solution.py:74
  32.3 1.4 %copy.54 = bf16[2,16,2,112,112]{4,2,3,1,0:T(2,128)(2,1)S(1)} copy(bf16[2,16,2,112,112]{4,3,2,1,0:T(8,128)(2,1)S(1)} %reshape_squeeze.6) | data formatting | bytes 3211264 | tf_op jit(solution)/shard_map/reshape;squeeze | solution.py:74
  33.8 2.0 %pad_bitcast_fusion = bf16[2,16,112,2,128]{4,3,2,1,0:T(2,128)(2,1)S(1)} fusion(bf16[2,16,2,112,112]{4,2,3,1,0:T(2,128)(2,1)S(1)} %copy.54), kind=kLoop, calls=%fused_computation.2 | loop fusion | bytes 3440640 | tf_op jit(solution)/shard_map/transpose | solution.py:76
  35.7 2.4 %gather_fusion = bf16[64,16,196]{2,1,0:T(8,128)(2,1)} fusion(bf16[64,16,196]{2,1,0:T(8,128)(2,1)} %get-tuple-element.18, s32[1024]{0:T(1024)S(1)} %pad_clamp_fusion), kind=kCustom, calls=%fused_computation | custom fusion | bytes 803072 | tf_op jit(solution)/shard_map/gather | solution.py:109
  38.2 2.1 %reshape.108 = bf16[2,16,112,256]{3,2,1,0:T(8,128)(2,1)} reshape(bf16[2,16,112,2,128]{4,3,2,1,0:T(2,128)(2,1)S(1)} %pad_bitcast_fusion) | data formatting | bytes 3670016 | tf_op jit(solution)/shard_map/reshape | solution.py:77
  40.3 24.4 %all-to-all-done = bf16[64,48,196]{2,1,0:T(8,128)(2,1)S(1)} async-done(((bf16[64,48,196]{2,1,0:T(8,128)(2,1)}), bf16[64,48,196]{2,1,0:T(8,128)(2,1)S(1)}, u32[]{:S(2)}, u32[]{:S(2)}) %all-to-all-start) | async-done | bytes 1204256 | tf_op jit(solution)/shard_map/all_to_all | solution.py:115
  64.7 0.5 copy.53
  65.2 2.1 %squeeze.30 = bf16[48,12544]{1,0:T(8,128)(2,1)S(1)} reshape(bf16[1,48,64,196]{3,2,1,0:T(8,128)(2,1)S(1)} %copy.53) | data formatting | bytes 2408448 | tf_op jit(solution)/shard_map/squeeze | solution.py:115
  67.3 6.1 %collective-permute-done = bf16[1,112,896]{2,1,0:T(8,128)(2,1)} collective-permute-done((bf16[1,112,896]{2,1,0:T(8,128)(2,1)}, bf16[1,112,896]{2,1,0:T(8,128)(2,1)}, u32[]{:S(2)}, u32[]{:S(2)}) %collective-permute-start) | collective-permute-done | bytes 200736 | tf_op jit(solution)/shard_map/ppermute | solution.py:14
  73.5 11.4 %all-to-all-start.1 = ((bf16[64,16,196]{2,1,0:T(8,128)(2,1)}), bf16[64,16,196]{2,1,0:T(8,128)(2,1)S(1)}, u32[]{:S(2)}, u32[]{:S(2)}) async-start(bf16[64,16,196]{2,1,0:T(8,128)(2,1)} %gather_fusion), calls=%async_computation.1 | async-start | bytes 1048576 | tf_op jit(solution)/shard_map/all_to_all | solution.py:115
  84.8 0.7 iota_compare_fusion
  85.5 2.7 %reshape.112 = bf16[48,112,112]{2,1,0:T(8,128)(2,1)S(1)} reshape(bf16[48,12544]{1,0:T(8,128)(2,1)S(1)} %squeeze.30) | data formatting | bytes 2408448 | tf_op jit(solution)/shard_map/reshape | solution.py:121
  88.4 1.2 reshape.110
  90.2 0.6 copy.59
  90.7 1.2 reshape.113
  92.3 1.2 slice_bitcast_fusion.1.b_ref
  93.6 5.6 %shard_map.64.acc_ref = f32[896,112]{1,0:T(8,128)S(1)} custom-call(bf16[3584,112]{1,0:T(8,128)(2,1)S(1)} %bitcast.49, bf16[112,1024]{1,0:T(8,128)(2,1)S(1)} %bitcast.54, bf16[16,112,256]{2,1,0:T(8,128)(2,1)S(1)} %slice_bitcast_fusion.1.b_ref, f32[896,112]{1,0:T(8,128)S(1)} %broadcast_in_dim.34.clone.acc_ref), custom_call_target="tpu_custom_call", output_to_operand_aliasing={{}: (3, {})} | custom-call | flops 1541406720 | bytes 2752512 | tf_op jit(solution)/shard_map/pallas_call | solution.py:49
  99.2 2.8 %shard_map.65.acc_ref = f32[896,112]{1,0:T(8,128)S(1)} custom-call(bf16[1792,112]{1,0:T(8,128)(2,1)S(1)} %bitcast.50, bf16[112,1024]{1,0:T(8,128)(2,1)S(1)} %bitcast.52, bf16[8,112,256]{2,1,0:T(8,128)(2,1)S(1)} %get-tuple-element.19.b_ref, f32[896,112]{1,0:T(8,128)S(1)} %shard_map.64.acc_ref), custom_call_target="tpu_custom_call", output_to_operand_aliasing={{}: (3, {})} | custom-call | flops 770703360 | bytes 1892352 | tf_op jit(solution)/shard_map/pallas_call | solution.py:49
  102.2 1.1 reshape_squeeze.7
  103.6 2.8 %shard_map.66 = f32[896,112]{1,0:T(8,128)S(1)} custom-call(bf16[1792,112]{1,0:T(8,128)(2,1)S(1)} %bitcast.51, bf16[112,1024]{1,0:T(8,128)(2,1)S(1)} %bitcast.53, bf16[8,112,256]{2,1,0:T(8,128)(2,1)S(1)} %get-tuple-element.20.b_ref, f32[896,112]{1,0:T(8,128)S(1)} %shard_map.65.acc_ref), custom_call_target="tpu_custom_call", output_to_operand_aliasing={{}: (3, {})} | custom-call | flops 770703360 | bytes 1892352 | tf_op jit(solution)/shard_map/pallas_call | solution.py:49
  106.7 0.3 copy.63
  106.9 8.4 %all_to_all.40 = f32[4,2,14,896]{3,0,2,1:T(4,128)S(1)} all-to-all(f32[4,2,14,896]{3,0,2,1:T(4,128)S(1)} %copy.63), channel_id=1, replica_groups=mesh['ka'=64,'zl'=4,'core'=2] {'core'}, dimensions={1} | all-to-all | bytes 802816 | tf_op jit(solution)/shard_map/all_to_all | solution.py:135
  115.5 0.7 copy.64
  116.2 3.9 %all-to-all-start.3 = ((f32[4,14,896]{2,1,0:T(8,128)}), f32[4,14,896]{2,1,0:T(8,128)S(1)}, u32[]{:S(2)}, u32[]{:S(2)}) async-start(f32[4,14,896]{2,1,0:T(8,128)} %copy.64), calls=%async_computation.3 | async-start | bytes 458752 | tf_op jit(solution)/shard_map/all_to_all | solution.py:136
  120.6 5.5 %all-to-all-done.3 = f32[4,14,896]{2,1,0:T(8,128)S(1)} async-done(((f32[4,14,896]{2,1,0:T(8,128)}), f32[4,14,896]{2,1,0:T(8,128)S(1)}, u32[]{:S(2)}, u32[]{:S(2)}) %all-to-all-start.3) | async-done | bytes 200736 | tf_op jit(solution)/shard_map/all_to_all | solution.py:136
  126.1 1.4 %fusion = bf16[1,14,896]{2,1,0:T(8,128)(2,1)} fusion(f32[14,896]{1,0:T(8,128)S(1)} %reduce_sum.48, f32[1,14,896]{2,1,0:T(8,128)S(1)} %sub.28, bf16[1,112,896]{2,1,0:T(8,128)(2,1)} %param.6, s32[]{:T(128)S(6)} %select_n.21, f32[896]{0:T(1024)S(1)} %sub.30), kind=kLoop, calls=%fused_computation.13 | loop fusion | flops 62720 | bytes 154116 | tf_op jit(solution)/shard_map/convert_element_type | solution.py:150
  (38 shorter events, 2.4 us)
Async XLA Ops:
  0.0 2.2 %copy-start.1 = (bf16[64,2,32,196]{3,2,1,0:T(8,128)(2,1)S(1)}, bf16[64,2,32,196]{3,2,1,0:T(8,128)(2,1)}, u32[]{:S(2)}) copy-start(bf16[64,2,32,196]{3,2,1,0:T(8,128)(2,1)} %param.8) | copy-start | bytes 4816900
  0.0 2.3 %copy-start.4 = (s32[64]{0:T(128)S(1)}, s32[64]{0:T(128)}, u32[]{:S(2)}) copy-start(s32[64]{0:T(128)} %param.9) | copy-start | bytes 772
  5.1 59.6 %all-to-all-start = ((bf16[64,48,196]{2,1,0:T(8,128)(2,1)}), bf16[64,48,196]{2,1,0:T(8,128)(2,1)S(1)}, u32[]{:S(2)}, u32[]{:S(2)}) async-start(bf16[64,48,196]{2,1,0:T(8,128)(2,1)} %gather_fusion.1), calls=%async_computation | async-start | bytes 3145728 | tf_op jit(solution)/shard_map/all_to_all | solution.py:115
  24.6 48.8 %collective-permute-start = (bf16[1,112,896]{2,1,0:T(8,128)(2,1)}, bf16[1,112,896]{2,1,0:T(8,128)(2,1)}, u32[]{:S(2)}, u32[]{:S(2)}) collective-permute-start(bf16[1,112,896]{2,1,0:T(8,128)(2,1)} %param.6), channel_id=1, source_target_pairs={{0,8},{8,16},{16,24},{24,32},{32,40},{40,48},{48,56},{56,64},{64,7... | collective-permute-start | bytes 602120 | tf_op jit(solution)/shard_map/ppermute | solution.py:14
  73.5 28.6 %all-to-all-start.1 = ((bf16[64,16,196]{2,1,0:T(8,128)(2,1)}), bf16[64,16,196]{2,1,0:T(8,128)(2,1)S(1)}, u32[]{:S(2)}, u32[]{:S(2)}) async-start(bf16[64,16,196]{2,1,0:T(8,128)(2,1)} %gather_fusion), calls=%async_computation.1 | async-start | bytes 1048576 | tf_op jit(solution)/shard_map/all_to_all | solution.py:115
  93.6 5.6 %copy-start = (bf16[2,16,112,256]{3,2,1,0:T(8,128)(2,1)S(1)}, bf16[2,16,112,256]{3,2,1,0:T(8,128)(2,1)}, u32[]{:S(2)}) copy-start(bf16[2,16,112,256]{3,2,1,0:T(8,128)(2,1)} %reshape.108) | copy-start | bytes 5505028
  106.6 13.5 %copy-start.2 = (f32[64,112]{1,0:T(8,128)S(1)}, f32[64,112]{1,0:T(8,128)}, u32[]{:S(2)}) copy-start(f32[64,112]{1,0:T(8,128)} %param.10) | copy-start | bytes 86020
  106.7 13.8 %copy-start.3 = (f32[8]{0:T(128)S(1)}, f32[8]{0:T(128)}, u32[]{:S(2)}) copy-start(f32[8]{0:T(128)} %param.11) | copy-start | bytes 100
  116.2 9.9 %all-to-all-start.3 = ((f32[4,14,896]{2,1,0:T(8,128)}), f32[4,14,896]{2,1,0:T(8,128)S(1)}, u32[]{:S(2)}, u32[]{:S(2)}) async-start(f32[4,14,896]{2,1,0:T(8,128)} %copy.64), calls=%async_computation.3 | async-start | bytes 458752 | tf_op jit(solution)/shard_map/all_to_all | solution.py:136

commit v12 on v11

--- a/solution.py
+++ b/solution.py
@@ -91,6 +91,21 @@
     aux_local = left_factor.shape[2]
     pair_count = trial_vector.shape[2] // virtuals
     own_block = trial_vector[0]
+    vert = lax.axis_size(("zl", "core"))
+    slab_width = virtuals // vert
+    offset = lax.axis_index(("zl", "core")) * slab_width
+    labels = jnp.arange(kpoints, dtype=jnp.int32)
+    owner_index = lax.axis_index("ka")
+    momentum_b = jnp.sum(jnp.where(labels == owner_index, kb_table, 0))
+    energy_rows = jnp.sum(jnp.where((labels == owner_index)[:, None], vir_energy, 0.0), axis=0)
+    energy_other = jnp.sum(jnp.where((labels == momentum_b)[:, None], vir_energy, 0.0), axis=0)
+    energy_a = lax.dynamic_slice_in_dim(energy_rows, offset, slab_width, 0)
+    own_rows = lax.dynamic_slice_in_dim(own_block, offset, slab_width, 0).astype(jnp.float32)
+    own_rows = own_rows.reshape(slab_width, pair_count, virtuals)
+    shift_energy = (
+        energy_a[:, None, None] + energy_other[None, None, :] - pair_energy[None, :, None]
+    )
+    orbital = (shift_energy * own_rows).reshape(slab_width, pair_count * virtuals)
     bq = left_pairs(left_factor[0], virtuals)
     blocks = [own_block] + [
         shifted(trial_vector, "ka", transfer)[0] for transfer in range(1, transfers)
@@ -108,8 +123,8 @@
         )
         piece = piece.at[kb_table].get(mode="promise_in_bounds")
         if arrivals:
-            piece, arrivals[-1], bq, blocks = lax.optimization_barrier(
-                (piece, arrivals[-1], bq, blocks)
+            piece, arrivals[-1], bq, blocks, orbital = lax.optimization_barrier(
+                (piece, arrivals[-1], bq, blocks, orbital)
             )
         arrivals.append(
             lax.all_to_all(piece, "ka", split_axis=0, concat_axis=2, tiled=True)[0]
@@ -128,25 +143,11 @@
             )
             at += count
     ladder_sum = ladder_t.T
-    vert = lax.axis_size(("zl", "core"))
-    slab_width = virtuals // vert
     cores = lax.axis_size("core")
     stacked = ladder_sum.reshape(vert // cores, cores, slab_width, -1)
     stacked = lax.all_to_all(stacked, "core", 1, 1, tiled=True).sum(1)
     ladder = lax.all_to_all(stacked, "zl", 0, 0, tiled=True).sum(0)
-    offset = lax.axis_index(("zl", "core")) * slab_width
-    labels = jnp.arange(kpoints, dtype=jnp.int32)
-    owner_index = lax.axis_index("ka")
-    momentum_b = jnp.sum(jnp.where(labels == owner_index, kb_table, 0))
-    energy_rows = jnp.sum(jnp.where((labels == owner_index)[:, None], vir_energy, 0.0), axis=0)
-    energy_other = jnp.sum(jnp.where((labels == momentum_b)[:, None], vir_energy, 0.0), axis=0)
-    energy_a = lax.dynamic_slice_in_dim(energy_rows, offset, slab_width, 0)
-    own_rows = lax.dynamic_slice_in_dim(own_block, offset, slab_width, 0).astype(jnp.float32)
-    own_rows = own_rows.reshape(slab_width, pair_count, virtuals)
-    shift_energy = (
-        energy_a[:, None, None] + energy_other[None, None, :] - pair_energy[None, :, None]
-    )
-    combined = ladder + (shift_energy * own_rows).reshape(slab_width, pair_count * virtuals)
+    combined = ladder + orbital
     return combined.astype(jnp.bfloat16)[None]
 
 

time: 130 us -> 128 us (0.985)
  blocking collectives: 8.43 us -> 18.8 us
  waiting for transfers between devices: 36 us -> 29.5 us
  starting transfers between devices: 37.7 us -> 34 us
  local copies, waits for them, and re-layouts: 30.4 us -> 28.7 us
    all_to_all x0 -> x1, blocking collectives: none -> 10.2 us  [shards(): ladder = lax.all_to_all(stacked, 'zl', 0, 0, tiled=True).sum(0)]
    all_to_all x1 -> x0, waiting for transfers between devices: 5.49 us -> none  [shards(): ladder = lax.all_to_all(stacked, 'zl', 0, 0, tiled=True).sum(0)]
    all_to_all x1 -> x0, starting transfers between devices: 3.89 us -> none  [shards(): ladder = lax.all_to_all(stacked, 'zl', 0, 0, tiled=True).sum(0)]
    convert_element_type x1 -> x0, other arithmetic: 1.42 us -> none  [shards(): return combined.astype(jnp.bfloat16)[None]]
    mul x0 -> x1, other arithmetic: none -> 1.42 us  [shards(): shift_energy * own_rows]
  transfers between devices with their start and end apart: 4 -> 3, of which waited for: 3 -> 3; matrix products, arithmetic and copies ran while one was open for 19% -> 20% of each run, Pallas kernels for 7% -> 7%
where the time goes in v12:
time: 128 us; the launch traced here: 127 us
  starting transfers between devices  34 us (27%)
  waiting for transfers between devices  29.5 us (23%)
  local copies, waits for them, and re-layouts  28.7 us (22%)
  blocking collectives  18.8 us (15%)
  Pallas kernels  11.2 us (9%)
  other arithmetic  3.95 us (3%)
    all_to_all x2, starting transfers between devices, shards(): lax.all_to_all(piece, 'ka', split_axis=0, concat_axis=2, tiled=True)[0]  31.1 us
    all_to_all x2, waiting for transfers between devices, shards(): lax.all_to_all(piece, 'ka', split_axis=0, concat_axis=2, tiled=True)[0]  23.4 us
    pallas_call x3, Pallas kernels, ladder_transposed(): pl.pallas_call(kernel, out_shape=jax.ShapeDtypeStruct((pairs * nv, nv), j...  11.2 us
    all_to_all x1, blocking collectives, shards(): ladder = lax.all_to_all(stacked, 'zl', 0, 0, tiled=True).sum(0)  10.2 us
    all_to_all x1, blocking collectives, shards(): stacked = lax.all_to_all(stacked, 'core', 1, 1, tiled=True).sum(1)  8.52 us
    another operation x2, local copies, waits for them, and re-layouts, left_pairs(): b = left.reshape(transfers, aux // 2, 2, virtuals, virtuals)  6.15 us
    ppermute x1, waiting for transfers between devices, shifted(): return lax.ppermute(value, axis, pairs)  6.14 us
    gather x2, local copies, waits for them, and re-layouts, shards(): piece = piece.at[kb_table].get(mode='promise_in_bounds')  3.18 us
  transfers between devices with their start and end apart: 3, of which 3 were waited for; matrix products, arithmetic and copies ran while one was open for 20% of the time, Pallas kernels for 7%

profile of v12, /device:TPU:1, one launch (start us, length us, event | category | flops | bytes accessed | tf_op | source)
XLA Modules:
  0.0 126.5 jit_solution(3325165169712720095)
XLA Ops:
  0.0 2.2 %slice_bitcast_fusion.2 = (bf16[64,16,196]{2,1,0:T(8,128)(2,1)S(1)}, bf16[64,16,196]{2,1,0:T(8,128)(2,1)}) fusion(bf16[64,2,32,196]{3,2,1,0:T(8,128)(2,1)} %param.8), kind=kLoop, calls=%fused_computation.6 | loop fusion | bytes 1605632 | tf_op jit(solution)/shard_map/squeeze | solution.py:122
  2.3 0.6 select_reduce_fusion.2
  3.0 0.3 pad_maximum_fusion
  3.3 1.8 %gather_fusion.1 = bf16[64,48,196]{2,1,0:T(8,128)(2,1)} fusion(bf16[64,48,196]{2,1,0:T(8,128)(2,1)S(1)} %pad_maximum_fusion, s32[1024]{0:T(1024)S(1)} %pad_clamp_fusion), kind=kCustom, calls=%fused_computation.1 | custom fusion | bytes 2408704 | tf_op jit(solution)/shard_map/gather | solution.py:124
  5.1 19.7 %all-to-all-start = ((bf16[64,48,196]{2,1,0:T(8,128)(2,1)}), bf16[64,48,196]{2,1,0:T(8,128)(2,1)S(1)}, u32[]{:S(2)}, u32[]{:S(2)}) async-start(bf16[64,48,196]{2,1,0:T(8,128)(2,1)} %gather_fusion.1), calls=%async_computation | async-start | bytes 3145728 | tf_op jit(solution)/shard_map/all_to_all | solution.py:130
  24.8 2.9 %collective-permute-start = (bf16[1,112,896]{2,1,0:T(8,128)(2,1)}, bf16[1,112,896]{2,1,0:T(8,128)(2,1)}, u32[]{:S(2)}, u32[]{:S(2)}) collective-permute-start(bf16[1,112,896]{2,1,0:T(8,128)(2,1)} %param.6), channel_id=1, source_target_pairs={{0,8},{8,16},{16,24},{24,32},{32,40},{40,48},{48,56},{56,64},{64,7... | collective-permute-start | bytes 602120 | tf_op jit(solution)/shard_map/ppermute | solution.py:14
  27.7 1.4 %gather_fusion = bf16[64,16,196]{2,1,0:T(8,128)(2,1)} fusion(bf16[64,16,196]{2,1,0:T(8,128)(2,1)S(1)} %copy-done.2, s32[1024]{0:T(1024)S(1)} %pad_clamp_fusion), kind=kCustom, calls=%fused_computation | custom fusion | bytes 803072 | tf_op jit(solution)/shard_map/gather | solution.py:124
  29.1 4.7 %reshape_squeeze.6 = bf16[2,16,2,112,112]{4,3,2,1,0:T(8,128)(2,1)S(1)} reshape(bf16[1,2,32,12544]{3,2,1,0:T(8,128)(2,1)} %param.7) | data formatting | bytes 3211264 | tf_op jit(solution)/shard_map/reshape;squeeze | solution.py:74
  33.9 1.4 %copy.54 = bf16[2,16,2,112,112]{4,2,3,1,0:T(2,128)(2,1)S(1)} copy(bf16[2,16,2,112,112]{4,3,2,1,0:T(8,128)(2,1)S(1)} %reshape_squeeze.6) | data formatting | bytes 3211264 | tf_op jit(solution)/shard_map/reshape;squeeze | solution.py:74
  35.3 2.0 %pad_bitcast_fusion = bf16[2,16,112,2,128]{4,3,2,1,0:T(2,128)(2,1)S(1)} fusion(bf16[2,16,2,112,112]{4,2,3,1,0:T(2,128)(2,1)S(1)} %copy.54), kind=kLoop, calls=%fused_computation.2 | loop fusion | bytes 3440640 | tf_op jit(solution)/shard_map/transpose | solution.py:76
  37.3 2.2 %reshape.75 = bf16[2,16,112,256]{3,2,1,0:T(8,128)(2,1)} reshape(bf16[2,16,112,2,128]{4,3,2,1,0:T(2,128)(2,1)S(1)} %pad_bitcast_fusion) | data formatting | bytes 3670016 | tf_op jit(solution)/shard_map/reshape | solution.py:77
  39.4 0.6 iota_compare_fusion
  40.6 1.4 %convert_multiply_fusion = f32[14,896]{1,0:T(8,128)} fusion(f32[14,896]{1,0:T(8,128)S(1)} %sub.21, bf16[1,112,896]{2,1,0:T(8,128)(2,1)} %param.6, s32[]{:T(128)S(6)} %select_n.21, f32[896]{0:T(1024)S(1)} %sub.23), kind=kLoop, calls=%fused_computation.12 | loop fusion | flops 37632 | bytes 129028 | tf_op jit(solution)/shard_map/mul | solution.py:108
  42.0 22.8 %all-to-all-done = bf16[64,48,196]{2,1,0:T(8,128)(2,1)S(1)} async-done(((bf16[64,48,196]{2,1,0:T(8,128)(2,1)}), bf16[64,48,196]{2,1,0:T(8,128)(2,1)S(1)}, u32[]{:S(2)}, u32[]{:S(2)}) %all-to-all-start) | async-done | bytes 1204256 | tf_op jit(solution)/shard_map/all_to_all | solution.py:130
  64.8 0.5 copy.53
  65.4 2.1 %squeeze.30 = bf16[48,12544]{1,0:T(8,128)(2,1)S(1)} reshape(bf16[1,48,64,196]{3,2,1,0:T(8,128)(2,1)S(1)} %copy.53) | data formatting | bytes 2408448 | tf_op jit(solution)/shard_map/squeeze | solution.py:130
  67.5 6.1 %collective-permute-done = bf16[1,112,896]{2,1,0:T(8,128)(2,1)} collective-permute-done((bf16[1,112,896]{2,1,0:T(8,128)(2,1)}, bf16[1,112,896]{2,1,0:T(8,128)(2,1)}, u32[]{:S(2)}, u32[]{:S(2)}) %collective-permute-start) | collective-permute-done | bytes 200736 | tf_op jit(solution)/shard_map/ppermute | solution.py:14
  73.6 11.4 %all-to-all-start.1 = ((bf16[64,16,196]{2,1,0:T(8,128)(2,1)}), bf16[64,16,196]{2,1,0:T(8,128)(2,1)S(1)}, u32[]{:S(2)}, u32[]{:S(2)}) async-start(bf16[64,16,196]{2,1,0:T(8,128)(2,1)} %gather_fusion), calls=%async_computation.1 | async-start | bytes 1048576 | tf_op jit(solution)/shard_map/all_to_all | solution.py:130
  85.0 2.7 %reshape.79 = bf16[48,112,112]{2,1,0:T(8,128)(2,1)S(1)} reshape(bf16[48,12544]{1,0:T(8,128)(2,1)S(1)} %squeeze.30) | data formatting | bytes 2408448 | tf_op jit(solution)/shard_map/reshape | solution.py:136
  87.8 1.2 reshape.77
  89.6 0.6 copy.59
  90.2 1.2 reshape.80
  91.7 1.2 slice_bitcast_fusion.1.b_ref
  93.0 5.6 %shard_map.64.acc_ref = f32[896,112]{1,0:T(8,128)S(1)} custom-call(bf16[3584,112]{1,0:T(8,128)(2,1)S(1)} %bitcast.50, bf16[112,1024]{1,0:T(8,128)(2,1)S(1)} %bitcast.55, bf16[16,112,256]{2,1,0:T(8,128)(2,1)S(1)} %slice_bitcast_fusion.1.b_ref, f32[896,112]{1,0:T(8,128)S(1)} %broadcast_in_dim.39.clone.acc_ref), custom_call_target="tpu_custom_call", output_to_operand_aliasing={{}: (3, {})} | custom-call | flops 1541406720 | bytes 2752512 | tf_op jit(solution)/shard_map/pallas_call | solution.py:49
  98.7 2.8 %shard_map.65.acc_ref = f32[896,112]{1,0:T(8,128)S(1)} custom-call(bf16[1792,112]{1,0:T(8,128)(2,1)S(1)} %bitcast.51, bf16[112,1024]{1,0:T(8,128)(2,1)S(1)} %bitcast.53, bf16[8,112,256]{2,1,0:T(8,128)(2,1)S(1)} %get-tuple-element.21.b_ref, f32[896,112]{1,0:T(8,128)S(1)} %shard_map.64.acc_ref), custom_call_target="tpu_custom_call", output_to_operand_aliasing={{}: (3, {})} | custom-call | flops 770703360 | bytes 1892352 | tf_op jit(solution)/shard_map/pallas_call | solution.py:49
  101.5 0.6 all-to-all-done.1
  102.3 1.1 reshape_squeeze.7
  103.6 2.8 %shard_map.66 = f32[896,112]{1,0:T(8,128)S(1)} custom-call(bf16[1792,112]{1,0:T(8,128)(2,1)S(1)} %bitcast.52, bf16[112,1024]{1,0:T(8,128)(2,1)S(1)} %bitcast.54, bf16[8,112,256]{2,1,0:T(8,128)(2,1)S(1)} %get-tuple-element.22.b_ref, f32[896,112]{1,0:T(8,128)S(1)} %shard_map.65.acc_ref), custom_call_target="tpu_custom_call", output_to_operand_aliasing={{}: (3, {})} | custom-call | flops 770703360 | bytes 1892352 | tf_op jit(solution)/shard_map/pallas_call | solution.py:49
  106.7 0.3 copy.63
  107.0 8.5 %all_to_all.40 = f32[4,2,14,896]{3,0,2,1:T(4,128)S(1)} all-to-all(f32[4,2,14,896]{3,0,2,1:T(4,128)S(1)} %copy.63), channel_id=1, replica_groups=mesh['ka'=64,'zl'=4,'core'=2] {'core'}, dimensions={1} | all-to-all | bytes 802816 | tf_op jit(solution)/shard_map/all_to_all | solution.py:148
  115.6 10.2 %all_to_all.41 = f32[4,14,896]{2,1,0:T(8,128)S(1)} all-to-all(f32[4,14,896]{2,1,0:T(8,128)S(1)} %copy.64), channel_id=1, replica_groups=mesh['ka'=64,'zl'=4,'core'=2] {'zl'}, dimensions={0} | all-to-all | bytes 401408 | tf_op jit(solution)/shard_map/all_to_all | solution.py:149
  125.9 0.6 fusion
  (42 shorter events, 2.5 us)
Async XLA Ops:
  0.0 2.2 %copy-start.1 = (bf16[64,2,32,196]{3,2,1,0:T(8,128)(2,1)S(1)}, bf16[64,2,32,196]{3,2,1,0:T(8,128)(2,1)}, u32[]{:S(2)}) copy-start(bf16[64,2,32,196]{3,2,1,0:T(8,128)(2,1)} %param.8) | copy-start | bytes 4816900
  0.0 2.3 %copy-start.6 = (s32[64]{0:T(128)S(1)}, s32[64]{0:T(128)}, u32[]{:S(2)}) copy-start(s32[64]{0:T(128)} %param.9) | copy-start | bytes 772
  5.1 22.6 %copy-start.2 = (bf16[64,16,196]{2,1,0:T(8,128)(2,1)S(1)}, bf16[64,16,196]{2,1,0:T(8,128)(2,1)}, u32[]{:S(2)}) copy-start(bf16[64,16,196]{2,1,0:T(8,128)(2,1)} %get-tuple-element.20) | copy-start | bytes 1204228
  5.1 59.8 %all-to-all-start = ((bf16[64,48,196]{2,1,0:T(8,128)(2,1)}), bf16[64,48,196]{2,1,0:T(8,128)(2,1)S(1)}, u32[]{:S(2)}, u32[]{:S(2)}) async-start(bf16[64,48,196]{2,1,0:T(8,128)(2,1)} %gather_fusion.1), calls=%async_computation | async-start | bytes 3145728 | tf_op jit(solution)/shard_map/all_to_all | solution.py:130
  24.8 48.8 %collective-permute-start = (bf16[1,112,896]{2,1,0:T(8,128)(2,1)}, bf16[1,112,896]{2,1,0:T(8,128)(2,1)}, u32[]{:S(2)}, u32[]{:S(2)}) collective-permute-start(bf16[1,112,896]{2,1,0:T(8,128)(2,1)} %param.6), channel_id=1, source_target_pairs={{0,8},{8,16},{16,24},{24,32},{32,40},{40,48},{48,56},{56,64},{64,7... | collective-permute-start | bytes 602120 | tf_op jit(solution)/shard_map/ppermute | solution.py:14
  37.3 2.8 %copy-start.4 = (f32[64,112]{1,0:T(8,128)S(1)}, f32[64,112]{1,0:T(8,128)}, u32[]{:S(2)}) copy-start(f32[64,112]{1,0:T(8,128)} %param.10) | copy-start | bytes 86020
  37.3 3.2 %copy-start.5 = (f32[8]{0:T(128)S(1)}, f32[8]{0:T(128)}, u32[]{:S(2)}) copy-start(f32[8]{0:T(128)} %param.11) | copy-start | bytes 100
  73.6 28.5 %all-to-all-start.1 = ((bf16[64,16,196]{2,1,0:T(8,128)(2,1)}), bf16[64,16,196]{2,1,0:T(8,128)(2,1)S(1)}, u32[]{:S(2)}, u32[]{:S(2)}) async-start(bf16[64,16,196]{2,1,0:T(8,128)(2,1)} %gather_fusion), calls=%async_computation.1 | async-start | bytes 1048576 | tf_op jit(solution)/shard_map/all_to_all | solution.py:130
  93.0 5.6 %copy-start = (bf16[2,16,112,256]{3,2,1,0:T(8,128)(2,1)S(1)}, bf16[2,16,112,256]{3,2,1,0:T(8,128)(2,1)}, u32[]{:S(2)}) copy-start(bf16[2,16,112,256]{3,2,1,0:T(8,128)(2,1)} %reshape.75) | copy-start | bytes 5505028
  106.7 19.2 %copy-start.3 = (f32[14,896]{1,0:T(8,128)S(1)}, f32[14,896]{1,0:T(8,128)}, u32[]{:S(2)}) copy-start(f32[14,896]{1,0:T(8,128)} %convert_multiply_fusion) | copy-start | bytes 150532

commit v13 on v12

--- a/solution.py
+++ b/solution.py
@@ -123,8 +123,8 @@
         )
         piece = piece.at[kb_table].get(mode="promise_in_bounds")
         if arrivals:
-            piece, arrivals[-1], bq, blocks, orbital = lax.optimization_barrier(
-                (piece, arrivals[-1], bq, blocks, orbital)
+            piece, arrivals[-1], bq, orbital = lax.optimization_barrier(
+                (piece, arrivals[-1], bq, orbital)
             )
         arrivals.append(
             lax.all_to_all(piece, "ka", split_axis=0, concat_axis=2, tiled=True)[0]

time: 128 us -> 130 us (1.016)
  starting transfers between devices: 34 us -> 40.2 us
  waiting for transfers between devices: 29.5 us -> 23.8 us
    all_to_all x2, starting transfers between devices: 31.1 us -> 37.3 us  [shards(): lax.all_to_all(piece, 'ka', split_axis=0, concat_axis=2, tiled=True)[0]]
    ppermute x1, waiting for transfers between devices: 6.14 us -> 0.01 us  [shifted(): return lax.ppermute(value, axis, pairs)]
    another operation x0 -> x4, local copies, waits for them, and re-layouts: none -> 2.86 us  [trial_transposed(): t = block.reshape(virtuals, pair_count, virtuals)]
    reshape x4 -> x0, local copies, waits for them, and re-layouts: 2.86 us -> none  [trial_transposed(): t = block.reshape(virtuals, pair_count, virtuals)]
  transfers between devices with their start and end apart: 3 -> 3, of which waited for: 3 -> 2; matrix products, arithmetic and copies ran while one was open for 20% -> 19% of each run, Pallas kernels for 7% -> 7%
where the time goes in v13:
time: 130 us; the launch traced here: 129 us
  starting transfers between devices  40.2 us (31%)
  local copies, waits for them, and re-layouts  29.8 us (23%)
  waiting for transfers between devices  23.8 us (18%)
  blocking collectives  18.8 us (14%)
  Pallas kernels  11.2 us (9%)
  other arithmetic  4.4 us (3%)
    all_to_all x2, starting transfers between devices, shards(): lax.all_to_all(piece, 'ka', split_axis=0, concat_axis=2, tiled=True)[0]  37.3 us
    all_to_all x2, waiting for transfers between devices, shards(): lax.all_to_all(piece, 'ka', split_axis=0, concat_axis=2, tiled=True)[0]  23.8 us
    pallas_call x3, Pallas kernels, ladder_transposed(): pl.pallas_call(kernel, out_shape=jax.ShapeDtypeStruct((pairs * nv, nv), j...  11.2 us
    all_to_all x1, blocking collectives, shards(): ladder = lax.all_to_all(stacked, 'zl', 0, 0, tiled=True).sum(0)  10.2 us
    all_to_all x1, blocking collectives, shards(): stacked = lax.all_to_all(stacked, 'core', 1, 1, tiled=True).sum(1)  8.52 us
    another operation x2, local copies, waits for them, and re-layouts, left_pairs(): b = left.reshape(transfers, aux // 2, 2, virtuals, virtuals)  6.15 us
    gather x2, local copies, waits for them, and re-layouts, shards(): piece = piece.at[kb_table].get(mode='promise_in_bounds')  3.18 us
    ppermute x1, starting transfers between devices, shifted(): return lax.ppermute(value, axis, pairs)  2.92 us
  transfers between devices with their start and end apart: 3, of which 2 were waited for; matrix products, arithmetic and copies ran while one was open for 19% of the time, Pallas kernels for 7%

profile of v13, /device:TPU:1, one launch (start us, length us, event | category | flops | bytes accessed | tf_op | source)
XLA Modules:
  0.0 128.6 jit_solution(1877221345825776530)
XLA Ops:
  0.0 2.2 %slice_bitcast_fusion.2 = (bf16[64,16,196]{2,1,0:T(8,128)(2,1)}, bf16[64,16,196]{2,1,0:T(8,128)(2,1)S(1)}) fusion(bf16[64,2,32,196]{3,2,1,0:T(8,128)(2,1)} %param.8), kind=kLoop, calls=%fused_computation.6 | loop fusion | bytes 1605632 | tf_op jit(solution)/shard_map/squeeze | solution.py:122
  2.3 0.6 select_reduce_fusion.2
  3.0 1.4 %pad_maximum_fusion = bf16[64,48,196]{2,1,0:T(8,128)(2,1)S(1)} fusion(bf16[64,16,196]{2,1,0:T(8,128)(2,1)} %get-tuple-element.15, bf16[64,32,196]{2,1,0:T(8,128)(2,1)S(1)} %slice_bitcast_fusion), kind=kLoop, calls=%fused_computation.3 | loop fusion | flops 2408448 | bytes 2408448 | tf_op jit(solution)/shard_map/concatenate | solution.py:121
  4.4 1.8 %gather_fusion.1 = bf16[64,48,196]{2,1,0:T(8,128)(2,1)} fusion(bf16[64,48,196]{2,1,0:T(8,128)(2,1)S(1)} %pad_maximum_fusion, s32[1024]{0:T(1024)S(1)} %pad_clamp_fusion), kind=kCustom, calls=%fused_computation.1 | custom fusion | bytes 2408704 | tf_op jit(solution)/shard_map/gather | solution.py:124
  6.1 19.6 %all-to-all-start = ((bf16[64,48,196]{2,1,0:T(8,128)(2,1)}), bf16[64,48,196]{2,1,0:T(8,128)(2,1)S(1)}, u32[]{:S(2)}, u32[]{:S(2)}) async-start(bf16[64,48,196]{2,1,0:T(8,128)(2,1)} %gather_fusion.1), calls=%async_computation | async-start | bytes 3145728 | tf_op jit(solution)/shard_map/all_to_all | solution.py:130
  25.7 2.9 %collective-permute-start = (bf16[1,112,896]{2,1,0:T(8,128)(2,1)}, bf16[1,112,896]{2,1,0:T(8,128)(2,1)}, u32[]{:S(2)}, u32[]{:S(2)}) collective-permute-start(bf16[1,112,896]{2,1,0:T(8,128)(2,1)} %param.6), channel_id=1, source_target_pairs={{0,8},{8,16},{16,24},{24,32},{32,40},{40,48},{48,56},{56,64},{64,7... | collective-permute-start | bytes 602120 | tf_op jit(solution)/shard_map/ppermute | solution.py:14
  28.6 1.4 %gather_fusion = bf16[64,16,196]{2,1,0:T(8,128)(2,1)} fusion(bf16[64,16,196]{2,1,0:T(8,128)(2,1)S(1)} %get-tuple-element.16, s32[1024]{0:T(1024)S(1)} %pad_clamp_fusion), kind=kCustom, calls=%fused_computation | custom fusion | bytes 803072 | tf_op jit(solution)/shard_map/gather | solution.py:124
  30.0 4.7 %reshape_squeeze.12 = bf16[2,16,2,112,112]{4,3,2,1,0:T(8,128)(2,1)S(1)} reshape(bf16[1,2,32,12544]{3,2,1,0:T(8,128)(2,1)} %param.7) | data formatting | bytes 3211264 | tf_op jit(solution)/shard_map/reshape;squeeze | solution.py:74
  34.8 1.4 %copy.54 = bf16[2,16,2,112,112]{4,2,3,1,0:T(2,128)(2,1)S(1)} copy(bf16[2,16,2,112,112]{4,3,2,1,0:T(8,128)(2,1)S(1)} %reshape_squeeze.12) | data formatting | bytes 3211264 | tf_op jit(solution)/shard_map/reshape;squeeze | solution.py:74
  36.2 2.0 %pad_bitcast_fusion = bf16[2,16,112,2,128]{4,3,2,1,0:T(2,128)(2,1)S(1)} fusion(bf16[2,16,2,112,112]{4,2,3,1,0:T(2,128)(2,1)S(1)} %copy.54), kind=kLoop, calls=%fused_computation.2 | loop fusion | bytes 3440640 | tf_op jit(solution)/shard_map/transpose | solution.py:76
  38.2 2.2 %reshape.69 = bf16[2,16,112,256]{3,2,1,0:T(8,128)(2,1)} reshape(bf16[2,16,112,2,128]{4,3,2,1,0:T(2,128)(2,1)S(1)} %pad_bitcast_fusion) | data formatting | bytes 3670016 | tf_op jit(solution)/shard_map/reshape | solution.py:77
  40.4 0.6 iota_compare_fusion
  41.6 0.8 convert_multiply_fusion
  42.4 23.4 %all-to-all-done = bf16[64,48,196]{2,1,0:T(8,128)(2,1)S(1)} async-done(((bf16[64,48,196]{2,1,0:T(8,128)(2,1)}), bf16[64,48,196]{2,1,0:T(8,128)(2,1)S(1)}, u32[]{:S(2)}, u32[]{:S(2)}) %all-to-all-start) | async-done | bytes 1204256 | tf_op jit(solution)/shard_map/all_to_all | solution.py:130
  65.8 0.5 copy.53
  66.3 2.1 %squeeze.25 = bf16[48,12544]{1,0:T(8,128)(2,1)S(1)} reshape(bf16[1,48,64,196]{3,2,1,0:T(8,128)(2,1)S(1)} %copy.53) | data formatting | bytes 2408448 | tf_op jit(solution)/shard_map/squeeze | solution.py:130
  68.4 17.8 %all-to-all-start.1 = ((bf16[64,16,196]{2,1,0:T(8,128)(2,1)}), bf16[64,16,196]{2,1,0:T(8,128)(2,1)}, u32[]{:S(2)}, u32[]{:S(2)}) async-start(bf16[64,16,196]{2,1,0:T(8,128)(2,1)} %gather_fusion), calls=%async_computation.1 | async-start | bytes 1048576 | tf_op jit(solution)/shard_map/all_to_all | solution.py:130
  86.2 1.2 reshape_squeeze.15
  87.7 1.2 reshape_squeeze.14
  89.3 2.7 %reshape.72 = bf16[48,112,112]{2,1,0:T(8,128)(2,1)S(1)} reshape(bf16[48,12544]{1,0:T(8,128)(2,1)S(1)} %squeeze.25) | data formatting | bytes 2408448 | tf_op jit(solution)/shard_map/reshape | solution.py:136
  92.4 0.6 copy.59
  93.0 1.2 slice_bitcast_fusion.1.b_ref
  94.3 5.6 %shard_map.64.acc_ref = f32[896,112]{1,0:T(8,128)S(1)} custom-call(bf16[3584,112]{1,0:T(8,128)(2,1)S(1)} %bitcast.48, bf16[112,1024]{1,0:T(8,128)(2,1)S(1)} %bitcast.53, bf16[16,112,256]{2,1,0:T(8,128)(2,1)S(1)} %slice_bitcast_fusion.1.b_ref, f32[896,112]{1,0:T(8,128)S(1)} %broadcast_in_dim.39.clone.acc_ref), custom_call_target="tpu_custom_call", output_to_operand_aliasing={{}: (3, {})} | custom-call | flops 1541406720 | bytes 2752512 | tf_op jit(solution)/shard_map/pallas_call | solution.py:49
  99.9 2.8 %shard_map.65.acc_ref = f32[896,112]{1,0:T(8,128)S(1)} custom-call(bf16[1792,112]{1,0:T(8,128)(2,1)S(1)} %bitcast.49, bf16[112,1024]{1,0:T(8,128)(2,1)S(1)} %bitcast.51, bf16[8,112,256]{2,1,0:T(8,128)(2,1)S(1)} %get-tuple-element.17.b_ref, f32[896,112]{1,0:T(8,128)S(1)} %shard_map.64.acc_ref), custom_call_target="tpu_custom_call", output_to_operand_aliasing={{}: (3, {})} | custom-call | flops 770703360 | bytes 1892352 | tf_op jit(solution)/shard_map/pallas_call | solution.py:49
  102.8 0.4 all-to-all-done.1
  103.2 1.2 copy.55
  104.4 1.1 reshape_squeeze.13
  105.7 2.8 %shard_map.66 = f32[896,112]{1,0:T(8,128)S(1)} custom-call(bf16[1792,112]{1,0:T(8,128)(2,1)S(1)} %bitcast.50, bf16[112,1024]{1,0:T(8,128)(2,1)S(1)} %bitcast.52, bf16[8,112,256]{2,1,0:T(8,128)(2,1)S(1)} %get-tuple-element.18.b_ref, f32[896,112]{1,0:T(8,128)S(1)} %shard_map.65.acc_ref), custom_call_target="tpu_custom_call", output_to_operand_aliasing={{}: (3, {})} | custom-call | flops 770703360 | bytes 1892352 | tf_op jit(solution)/shard_map/pallas_call | solution.py:49
  108.8 0.3 copy.63
  109.0 8.5 %all_to_all.40 = f32[4,2,14,896]{3,0,2,1:T(4,128)S(1)} all-to-all(f32[4,2,14,896]{3,0,2,1:T(4,128)S(1)} %copy.63), channel_id=1, replica_groups=mesh['ka'=64,'zl'=4,'core'=2] {'core'}, dimensions={1} | all-to-all | bytes 802816 | tf_op jit(solution)/shard_map/all_to_all | solution.py:148
  117.7 10.2 %all_to_all.41 = f32[4,14,896]{2,1,0:T(8,128)S(1)} all-to-all(f32[4,14,896]{2,1,0:T(8,128)S(1)} %copy.64), channel_id=1, replica_groups=mesh['ka'=64,'zl'=4,'core'=2] {'zl'}, dimensions={0} | all-to-all | bytes 401408 | tf_op jit(solution)/shard_map/all_to_all | solution.py:149
  128.0 0.6 fusion
  (38 shorter events, 2.3 us)
Async XLA Ops:
  0.0 2.2 %copy-start.1 = (bf16[64,2,32,196]{3,2,1,0:T(8,128)(2,1)S(1)}, bf16[64,2,32,196]{3,2,1,0:T(8,128)(2,1)}, u32[]{:S(2)}) copy-start(bf16[64,2,32,196]{3,2,1,0:T(8,128)(2,1)} %param.8) | copy-start | bytes 4816900
  0.0 2.3 %copy-start.4 = (s32[64]{0:T(128)S(1)}, s32[64]{0:T(128)}, u32[]{:S(2)}) copy-start(s32[64]{0:T(128)} %param.9) | copy-start | bytes 772
  6.1 59.6 %all-to-all-start = ((bf16[64,48,196]{2,1,0:T(8,128)(2,1)}), bf16[64,48,196]{2,1,0:T(8,128)(2,1)S(1)}, u32[]{:S(2)}, u32[]{:S(2)}) async-start(bf16[64,48,196]{2,1,0:T(8,128)(2,1)} %gather_fusion.1), calls=%async_computation | async-start | bytes 3145728 | tf_op jit(solution)/shard_map/all_to_all | solution.py:130
  25.7 62.0 %collective-permute-start = (bf16[1,112,896]{2,1,0:T(8,128)(2,1)}, bf16[1,112,896]{2,1,0:T(8,128)(2,1)}, u32[]{:S(2)}, u32[]{:S(2)}) collective-permute-start(bf16[1,112,896]{2,1,0:T(8,128)(2,1)} %param.6), channel_id=1, source_target_pairs={{0,8},{8,16},{16,24},{24,32},{32,40},{40,48},{48,56},{56,64},{64,7... | collective-permute-start | bytes 602120 | tf_op jit(solution)/shard_map/ppermute | solution.py:14
  38.2 2.9 %copy-start.2 = (f32[64,112]{1,0:T(8,128)S(1)}, f32[64,112]{1,0:T(8,128)}, u32[]{:S(2)}) copy-start(f32[64,112]{1,0:T(8,128)} %param.10) | copy-start | bytes 86020
  38.2 3.2 %copy-start.3 = (f32[8]{0:T(128)S(1)}, f32[8]{0:T(128)}, u32[]{:S(2)}) copy-start(f32[8]{0:T(128)} %param.11) | copy-start | bytes 100
  68.4 34.7 %all-to-all-start.1 = ((bf16[64,16,196]{2,1,0:T(8,128)(2,1)}), bf16[64,16,196]{2,1,0:T(8,128)(2,1)}, u32[]{:S(2)}, u32[]{:S(2)}) async-start(bf16[64,16,196]{2,1,0:T(8,128)(2,1)} %gather_fusion), calls=%async_computation.1 | async-start | bytes 1048576 | tf_op jit(solution)/shard_map/all_to_all | solution.py:130
  94.3 5.6 %copy-start = (bf16[2,16,112,256]{3,2,1,0:T(8,128)(2,1)S(1)}, bf16[2,16,112,256]{3,2,1,0:T(8,128)(2,1)}, u32[]{:S(2)}) copy-start(bf16[2,16,112,256]{3,2,1,0:T(8,128)(2,1)} %reshape.69) | copy-start | bytes 5505028

commit v14 on v12

--- a/solution.py
+++ b/solution.py
@@ -38,11 +38,12 @@
     out_ref[...] = acc
 
 
-def ladder_transposed(ct, tt, bpair, acc, chunk=8):
+def ladder_transposed(ct, tt, bpair, acc):
     rows, nv = ct.shape
     aux = 2 * bpair.shape[0]
     lanes = 128
     pairs = tt.shape[1] // lanes
+    chunk = max(c for c in (8, 6, 4, 2) if aux % c == 0)
     steps = aux // chunk
     kernel = functools.partial(ladder_kernel, chunk=chunk, nv=nv, pairs=pairs, lanes=lanes)
     flops = 2 * aux * nv * nv * (pairs * lanes + pairs * nv)
@@ -110,7 +111,7 @@
     blocks = [own_block] + [
         shifted(trial_vector, "ka", transfer)[0] for transfer in range(1, transfers)
     ]
-    tail = aux_local // 2
+    tail = (3 * aux_local) // 8
     last = transfers - 1
     groups = [
         [(t, 0, aux_local) for t in range(last)] + [(last, 0, aux_local - tail)],

time: 128 us -> 141 us (1.10)
  local copies, waits for them, and re-layouts: 28.7 us -> 46.8 us
  waiting for transfers between devices: 29.5 us -> 24.6 us
  blocking collectives: 18.8 us -> 15.8 us
  starting transfers between devices: 34 us -> 35.9 us
    slice x4, local copies, waits for them, and re-layouts: 0.91 us -> 5.87 us  [shards(): ct[at * virtuals:(at + count) * virtuals]]
    reshape x1, local copies, waits for them, and re-layouts: 2.15 us -> 5.29 us  [left_pairs(): return b.reshape(transfers, aux // 2, virtuals, 256)]
    all_to_all x1, blocking collectives: 8.52 us -> 5.39 us  [shards(): stacked = lax.all_to_all(stacked, 'core', 1, 1, tiled=True).sum(1)]
    all_to_all x2, waiting for transfers between devices: 23.4 us -> 20.6 us  [shards(): lax.all_to_all(piece, 'ka', split_axis=0, concat_axis=2, tiled=True)[0]]
    squeeze x2 -> x3, local copies, waits for them, and re-layouts: 2.3 us -> 4.63 us  [shards(): right_factor[:, t, start:start + count]]
    another operation x2, local copies, waits for them, and re-layouts: 6.15 us -> 8.46 us  [left_pairs(): b = left.reshape(transfers, aux // 2, 2, virtuals, virtuals)]
    ppermute x1, waiting for transfers between devices: 6.14 us -> 3.97 us  [shifted(): return lax.ppermute(value, axis, pairs)]
    squeeze x1, local copies, waits for them, and re-layouts: 2.1 us -> 4.22 us  [shards(): lax.all_to_all(piece, 'ka', split_axis=0, concat_axis=2, tiled=True)[0]]
  transfers between devices with their start and end apart: 3 -> 3, of which waited for: 3 -> 2; matrix products, arithmetic and copies ran while one was open for 20% -> 29% of each run, Pallas kernels for 7% -> 6%
where the time goes in v14:
time: 141 us; the launch traced here: 139 us
  local copies, waits for them, and re-layouts  46.8 us (33%)
  starting transfers between devices  35.9 us (25%)
  waiting for transfers between devices  24.6 us (17%)
  blocking collectives  15.8 us (11%)
  Pallas kernels  10.8 us (8%)
  other arithmetic  5.11 us (4%)
    all_to_all x2, starting transfers between devices, shards(): lax.all_to_all(piece, 'ka', split_axis=0, concat_axis=2, tiled=True)[0]  33 us
    all_to_all x2, waiting for transfers between devices, shards(): lax.all_to_all(piece, 'ka', split_axis=0, concat_axis=2, tiled=True)[0]  20.6 us
    pallas_call x3, Pallas kernels, ladder_transposed(): pl.pallas_call(kernel, out_shape=jax.ShapeDtypeStruct((pairs * nv, nv), j...  10.8 us
    all_to_all x1, blocking collectives, shards(): ladder = lax.all_to_all(stacked, 'zl', 0, 0, tiled=True).sum(0)  10.4 us
    another operation x2, local copies, waits for them, and re-layouts, left_pairs(): b = left.reshape(transfers, aux // 2, 2, virtuals, virtuals)  8.46 us
    slice x4, local copies, waits for them, and re-layouts, shards(): ct[at * virtuals:(at + count) * virtuals]  5.87 us
    all_to_all x1, blocking collectives, shards(): stacked = lax.all_to_all(stacked, 'core', 1, 1, tiled=True).sum(1)  5.39 us
    reshape x1, local copies, waits for them, and re-layouts, left_pairs(): return b.reshape(transfers, aux // 2, virtuals, 256)  5.29 us
  transfers between devices with their start and end apart: 3, of which 2 were waited for; matrix products, arithmetic and copies ran while one was open for 29% of the time, Pallas kernels for 6%

profile of v14, /device:TPU:1, one launch (start us, length us, event | category | flops | bytes accessed | tf_op | source)
XLA Modules:
  0.0 139.3 jit_solution(4198408840659154010)
XLA Ops:
  0.0 2.1 %slice_bitcast_fusion.2 = bf16[64,20,196]{2,1,0:T(8,128)(2,1)} fusion(bf16[64,2,32,196]{3,2,1,0:T(8,128)(2,1)} %param.8), kind=kLoop, calls=%fused_computation.6 | loop fusion | bytes 1003520 | tf_op jit(solution)/shard_map/squeeze | solution.py:123
  2.1 1.3 slice_bitcast_fusion
  4.0 1.5 %pad_maximum_fusion = bf16[64,52,196]{2,1,0:T(8,128)(2,1)S(1)} fusion(bf16[64,20,196]{2,1,0:T(8,128)(2,1)} %slice_bitcast_fusion.2, bf16[64,32,196]{2,1,0:T(8,128)(2,1)S(1)} %slice_bitcast_fusion), kind=kLoop, calls=%fused_computation.2 | loop fusion | flops 2609152 | bytes 2609152 | tf_op jit(solution)/shard_map/concatenate | solution.py:122
  5.5 1.9 %gather_fusion.1 = bf16[64,52,196]{2,1,0:T(8,128)(2,1)} fusion(bf16[64,52,196]{2,1,0:T(8,128)(2,1)S(1)} %pad_maximum_fusion, s32[1024]{0:T(1024)S(1)} %pad_clamp_fusion), kind=kCustom, calls=%fused_computation.1 | custom fusion | bytes 2609408 | tf_op jit(solution)/shard_map/gather | solution.py:125
  7.4 19.6 %all-to-all-start = ((bf16[64,52,196]{2,1,0:T(8,128)(2,1)}), bf16[64,52,196]{2,1,0:T(8,128)(2,1)S(1)}, u32[]{:S(2)}, u32[]{:S(2)}) async-start(bf16[64,52,196]{2,1,0:T(8,128)(2,1)} %gather_fusion.1), calls=%async_computation | async-start | bytes 3670016 | tf_op jit(solution)/shard_map/all_to_all | solution.py:131
  27.0 2.9 %collective-permute-start = (bf16[1,112,896]{2,1,0:T(8,128)(2,1)}, bf16[1,112,896]{2,1,0:T(8,128)(2,1)}, u32[]{:S(2)}, u32[]{:S(2)}) collective-permute-start(bf16[1,112,896]{2,1,0:T(8,128)(2,1)} %param.6), channel_id=1, source_target_pairs={{0,8},{8,16},{16,24},{24,32},{32,40},{40,48},{48,56},{56,64},{64,7... | collective-permute-start | bytes 602120 | tf_op jit(solution)/shard_map/ppermute | solution.py:14
  29.9 1.3 slice_bitcast_fusion.4
  31.2 1.4 %gather_fusion = bf16[64,12,196]{2,1,0:T(8,128)(2,1)} fusion(bf16[64,12,196]{2,1,0:T(8,128)(2,1)S(1)} %slice_bitcast_fusion.4, s32[1024]{0:T(1024)S(1)} %pad_clamp_fusion), kind=kCustom, calls=%fused_computation | custom fusion | bytes 602368 | tf_op jit(solution)/shard_map/gather | solution.py:125
  32.6 5.5 %reshape_squeeze.6 = bf16[2,16,2,112,112]{4,3,2,1,0:T(8,128)(2,1)} reshape(bf16[1,2,32,12544]{3,2,1,0:T(8,128)(2,1)} %param.7) | data formatting | bytes 3211264 | tf_op jit(solution)/shard_map/reshape;squeeze | solution.py:75
  38.1 2.9 %copy.54 = bf16[2,16,2,112,112]{4,2,3,1,0:T(2,128)(2,1)S(1)} copy(bf16[2,16,2,112,112]{4,3,2,1,0:T(8,128)(2,1)} %reshape_squeeze.6) | data formatting | bytes 3211264 | tf_op jit(solution)/shard_map/reshape;squeeze | solution.py:75
  41.1 3.3 %pad_bitcast_fusion = bf16[2,16,112,2,128]{4,3,2,1,0:T(2,128)(2,1)} fusion(bf16[2,16,2,112,112]{4,2,3,1,0:T(2,128)(2,1)S(1)} %copy.54), kind=kLoop, calls=%fused_computation.3 | loop fusion | bytes 3440640 | tf_op jit(solution)/shard_map/transpose | solution.py:77
  44.3 5.3 %reshape.75 = bf16[2,16,112,256]{3,2,1,0:T(8,128)(2,1)} reshape(bf16[2,16,112,2,128]{4,3,2,1,0:T(2,128)(2,1)} %pad_bitcast_fusion) | data formatting | bytes 3670016 | tf_op jit(solution)/shard_map/reshape | solution.py:78
  50.8 1.4 %convert_multiply_fusion = f32[14,896]{1,0:T(8,128)} fusion(f32[14,896]{1,0:T(8,128)S(1)} %sub.21, bf16[1,112,896]{2,1,0:T(8,128)(2,1)} %param.6, s32[]{:T(128)S(6)} %select_n.21, f32[896]{0:T(1024)S(1)} %sub.23), kind=kLoop, calls=%fused_computation.12 | loop fusion | flops 37632 | bytes 129028 | tf_op jit(solution)/shard_map/mul | solution.py:109
  52.2 20.6 %all-to-all-done = bf16[64,52,196]{2,1,0:T(8,128)(2,1)S(1)} async-done(((bf16[64,52,196]{2,1,0:T(8,128)(2,1)}), bf16[64,52,196]{2,1,0:T(8,128)(2,1)S(1)}, u32[]{:S(2)}, u32[]{:S(2)}) %all-to-all-start) | async-done | bytes 1304608 | tf_op jit(solution)/shard_map/all_to_all | solution.py:131
  73.2 4.2 %squeeze.30 = bf16[52,12544]{1,0:T(8,128)(2,1)} reshape(bf16[1,52,64,196]{3,2,1,0:T(8,128)(2,1)S(1)} %copy.53) | data formatting | bytes 2609152 | tf_op jit(solution)/shard_map/squeeze | solution.py:131
  77.4 4.0 %collective-permute-done = bf16[1,112,896]{2,1,0:T(8,128)(2,1)} collective-permute-done((bf16[1,112,896]{2,1,0:T(8,128)(2,1)}, bf16[1,112,896]{2,1,0:T(8,128)(2,1)}, u32[]{:S(2)}, u32[]{:S(2)}) %collective-permute-start) | collective-permute-done | bytes 200736 | tf_op jit(solution)/shard_map/ppermute | solution.py:14
  81.4 13.4 %all-to-all-start.1 = ((bf16[64,12,196]{2,1,0:T(8,128)(2,1)}), bf16[64,12,196]{2,1,0:T(8,128)(2,1)}, u32[]{:S(2)}, u32[]{:S(2)}) async-start(bf16[64,12,196]{2,1,0:T(8,128)(2,1)} %gather_fusion), calls=%async_computation.1 | async-start | bytes 1048576 | tf_op jit(solution)/shard_map/all_to_all | solution.py:131
  94.8 4.1 %reshape.79 = bf16[52,112,112]{2,1,0:T(8,128)(2,1)S(1)} reshape(bf16[52,12544]{1,0:T(8,128)(2,1)} %squeeze.30) | data formatting | bytes 2609152 | tf_op jit(solution)/shard_map/reshape | solution.py:137
  98.9 1.1 copy-done.1
  100.0 1.0 slice.45
  101.0 1.6 %copy.59 = bf16[32,112,112]{2,1,0:T(8,128)(2,1)S(1)} copy(bf16[32,112,112]{1,2,0:T(8,128)(2,1)} %slice.45) | data formatting | bytes 1605632 | tf_op jit(solution)/shard_map/slice | solution.py:142
  102.6 1.2 reshape.80
  104.3 5.6 %shard_map.64.acc_ref = f32[896,112]{1,0:T(8,128)S(1)} custom-call(bf16[3584,112]{1,0:T(8,128)(2,1)S(1)} %bitcast.50, bf16[112,1024]{1,0:T(8,128)(2,1)S(1)} %bitcast.55, bf16[16,112,256]{2,1,0:T(8,128)(2,1)S(1)} %slice_bitcast_fusion.1.b_ref, f32[896,112]{1,0:T(8,128)S(1)} %broadcast_in_dim.39.clone.acc_ref), custom_call_target="tpu_custom_call", output_to_operand_aliasing={{}: (3, {})} | custom-call | flops 1541406720 | bytes 2752512 | tf_op jit(solution)/shard_map/pallas_call | solution.py:50
  109.9 1.9 %slice.44 = bf16[20,112,112]{1,2,0:T(8,128)(2,1)} slice(bf16[52,112,112]{1,2,0:T(8,128)(2,1)} %bitcast.58), slice={[32:52], [0:112], [0:112]} | slice | bytes 1003520 | tf_op jit(solution)/shard_map/slice | solution.py:142
  111.8 1.2 reshape.77
  113.3 1.3 copy.58
  114.7 3.2 %shard_map.65.acc_ref = f32[896,112]{1,0:T(8,128)S(1)} custom-call(bf16[2240,112]{1,0:T(8,128)(2,1)S(1)} %bitcast.51, bf16[112,1024]{1,0:T(8,128)(2,1)S(1)} %bitcast.53, bf16[10,112,256]{2,1,0:T(8,128)(2,1)S(1)} %slice_bitcast_fusion.3.b_ref, f32[896,112]{1,0:T(8,128)S(1)} %shard_map.64.acc_ref), custom_call_target="tpu_custom_call", output_to_operand_aliasing={{}: (3, {})} | custom-call | flops 963379200 | bytes 2107392 | tf_op jit(solution)/shard_map/pallas_call | solution.py:50
  118.0 1.2 copy.55
  119.1 0.8 reshape_squeeze.7
  120.1 2.0 %shard_map.66 = f32[896,112]{1,0:T(8,128)S(1)} custom-call(bf16[1344,112]{1,0:T(8,128)(2,1)S(1)} %bitcast.52, bf16[112,1024]{1,0:T(8,128)(2,1)S(1)} %bitcast.54, bf16[6,112,256]{2,1,0:T(8,128)(2,1)S(1)} %slice_bitcast_fusion.5.b_ref, f32[896,112]{1,0:T(8,128)S(1)} %shard_map.65.acc_ref), custom_call_target="tpu_custom_call", output_to_operand_aliasing={{}: (3, {})} | custom-call | flops 578027520 | bytes 1677312 | tf_op jit(solution)/shard_map/pallas_call | solution.py:50
  122.7 5.4 %all_to_all.40 = f32[4,2,14,896]{3,0,2,1:T(4,128)S(1)} all-to-all(f32[4,2,14,896]{3,0,2,1:T(4,128)S(1)} %copy.63), channel_id=1, replica_groups=mesh['ka'=64,'zl'=4,'core'=2] {'core'}, dimensions={1} | all-to-all | bytes 802816 | tf_op jit(solution)/shard_map/all_to_all | solution.py:149
  128.2 10.4 %all_to_all.41 = f32[4,14,896]{2,1,0:T(8,128)S(1)} all-to-all(f32[4,14,896]{2,1,0:T(8,128)S(1)} %copy.64), channel_id=1, replica_groups=mesh['ka'=64,'zl'=4,'core'=2] {'zl'}, dimensions={0} | all-to-all | bytes 401408 | tf_op jit(solution)/shard_map/all_to_all | solution.py:150
  (42 shorter events, 4.5 us)
Async XLA Ops:
  0.0 3.4 %copy-start.5 = (s32[64]{0:T(128)S(1)}, s32[64]{0:T(128)}, u32[]{:S(2)}) copy-start(s32[64]{0:T(128)} %param.9) | copy-start | bytes 772
  7.4 65.4 %all-to-all-start = ((bf16[64,52,196]{2,1,0:T(8,128)(2,1)}), bf16[64,52,196]{2,1,0:T(8,128)(2,1)S(1)}, u32[]{:S(2)}, u32[]{:S(2)}) async-start(bf16[64,52,196]{2,1,0:T(8,128)(2,1)} %gather_fusion.1), calls=%async_computation | async-start | bytes 3670016 | tf_op jit(solution)/shard_map/all_to_all | solution.py:131
  27.0 54.4 %collective-permute-start = (bf16[1,112,896]{2,1,0:T(8,128)(2,1)}, bf16[1,112,896]{2,1,0:T(8,128)(2,1)}, u32[]{:S(2)}, u32[]{:S(2)}) collective-permute-start(bf16[1,112,896]{2,1,0:T(8,128)(2,1)} %param.6), channel_id=1, source_target_pairs={{0,8},{8,16},{16,24},{24,32},{32,40},{40,48},{48,56},{56,64},{64,7... | collective-permute-start | bytes 602120 | tf_op jit(solution)/shard_map/ppermute | solution.py:14
  44.3 6.0 %copy-start.3 = (f32[64,112]{1,0:T(8,128)S(1)}, f32[64,112]{1,0:T(8,128)}, u32[]{:S(2)}) copy-start(f32[64,112]{1,0:T(8,128)} %param.10) | copy-start | bytes 86020
  44.3 6.3 %copy-start.4 = (f32[8]{0:T(128)S(1)}, f32[8]{0:T(128)}, u32[]{:S(2)}) copy-start(f32[8]{0:T(128)} %param.11) | copy-start | bytes 100
  81.4 36.6 %all-to-all-start.1 = ((bf16[64,12,196]{2,1,0:T(8,128)(2,1)}), bf16[64,12,196]{2,1,0:T(8,128)(2,1)}, u32[]{:S(2)}, u32[]{:S(2)}) async-start(bf16[64,12,196]{2,1,0:T(8,128)(2,1)} %gather_fusion), calls=%async_computation.1 | async-start | bytes 1048576 | tf_op jit(solution)/shard_map/all_to_all | solution.py:131
  98.9 1.1 copy-start.1
  101.0 3.2 %copy-start = (bf16[2,16,112,256]{3,2,1,0:T(8,128)(2,1)S(1)}, bf16[2,16,112,256]{3,2,1,0:T(8,128)(2,1)}, u32[]{:S(2)}) copy-start(bf16[2,16,112,256]{3,2,1,0:T(8,128)(2,1)} %reshape.75) | copy-start | bytes 5505028
  122.4 16.3 %copy-start.2 = (f32[14,896]{1,0:T(8,128)S(1)}, f32[14,896]{1,0:T(8,128)}, u32[]{:S(2)}) copy-start(f32[14,896]{1,0:T(8,128)} %convert_multiply_fusion) | copy-start | bytes 150532

commit v15 on v12

--- a/solution.py
+++ b/solution.py
@@ -38,7 +38,7 @@
     out_ref[...] = acc
 
 
-def ladder_transposed(ct, tt, bpair, acc, chunk=8):
+def ladder_transposed(ct, tt, bpair, acc, chunk=16):
     rows, nv = ct.shape
     aux = 2 * bpair.shape[0]
     lanes = 128

time: 128 us -> 129 us (level)
  Pallas kernels: 11.2 us -> 13.9 us
  blocking collectives: 18.8 us -> 17.3 us
    pallas_call x3, Pallas kernels: 11.2 us -> 13.9 us  [ladder_transposed(): pl.pallas_call(kernel, out_shape=jax.ShapeDtypeStruct((pairs * nv, nv), j...]
    all_to_all x1, blocking collectives: 8.52 us -> 7.08 us  [shards(): stacked = lax.all_to_all(stacked, 'core', 1, 1, tiled=True).sum(1)]
  transfers between devices with their start and end apart: 3 -> 3, of which waited for: 3 -> 2; matrix products, arithmetic and copies ran while one was open for 20% -> 20% of each run, Pallas kernels for 7% -> 8%
where the time goes in v15:
time: 129 us; the launch traced here: 127 us
  starting transfers between devices  34 us (26%)
  waiting for transfers between devices  28.9 us (22%)
  local copies, waits for them, and re-layouts  28.7 us (22%)
  blocking collectives  17.3 us (13%)
  Pallas kernels  13.9 us (11%)
  other arithmetic  3.95 us (3%)
    all_to_all x2, starting transfers between devices, shards(): lax.all_to_all(piece, 'ka', split_axis=0, concat_axis=2, tiled=True)[0]  31.1 us
    all_to_all x2, waiting for transfers between devices, shards(): lax.all_to_all(piece, 'ka', split_axis=0, concat_axis=2, tiled=True)[0]  22.8 us
    pallas_call x3, Pallas kernels, ladder_transposed(): pl.pallas_call(kernel, out_shape=jax.ShapeDtypeStruct((pairs * nv, nv), j...  13.9 us
    all_to_all x1, blocking collectives, shards(): ladder = lax.all_to_all(stacked, 'zl', 0, 0, tiled=True).sum(0)  10.2 us
    all_to_all x1, blocking collectives, shards(): stacked = lax.all_to_all(stacked, 'core', 1, 1, tiled=True).sum(1)  7.08 us
    another operation x2, local copies, waits for them, and re-layouts, left_pairs(): b = left.reshape(transfers, aux // 2, 2, virtuals, virtuals)  6.15 us
    ppermute x1, waiting for transfers between devices, shifted(): return lax.ppermute(value, axis, pairs)  6.14 us
    gather x2, local copies, waits for them, and re-layouts, shards(): piece = piece.at[kb_table].get(mode='promise_in_bounds')  3.18 us
  transfers between devices with their start and end apart: 3, of which 2 were waited for; matrix products, arithmetic and copies ran while one was open for 20% of the time, Pallas kernels for 8%

profile of v15, /device:TPU:1, one launch (start us, length us, event | category | flops | bytes accessed | tf_op | source)
XLA Modules:
  0.0 127.2 jit_solution(1527712658400875972)
XLA Ops:
  0.0 2.2 %slice_bitcast_fusion.2 = (bf16[64,16,196]{2,1,0:T(8,128)(2,1)S(1)}, bf16[64,16,196]{2,1,0:T(8,128)(2,1)}) fusion(bf16[64,2,32,196]{3,2,1,0:T(8,128)(2,1)} %param.8), kind=kLoop, calls=%fused_computation.6 | loop fusion | bytes 1605632 | tf_op jit(solution)/shard_map/squeeze | solution.py:122
  2.3 0.6 select_reduce_fusion.2
  3.0 0.3 pad_maximum_fusion
  3.3 1.8 %gather_fusion.1 = bf16[64,48,196]{2,1,0:T(8,128)(2,1)} fusion(bf16[64,48,196]{2,1,0:T(8,128)(2,1)S(1)} %pad_maximum_fusion, s32[1024]{0:T(1024)S(1)} %pad_clamp_fusion), kind=kCustom, calls=%fused_computation.1 | custom fusion | bytes 2408704 | tf_op jit(solution)/shard_map/gather | solution.py:124
  5.1 19.7 %all-to-all-start = ((bf16[64,48,196]{2,1,0:T(8,128)(2,1)}), bf16[64,48,196]{2,1,0:T(8,128)(2,1)S(1)}, u32[]{:S(2)}, u32[]{:S(2)}) async-start(bf16[64,48,196]{2,1,0:T(8,128)(2,1)} %gather_fusion.1), calls=%async_computation | async-start | bytes 3145728 | tf_op jit(solution)/shard_map/all_to_all | solution.py:130
  24.8 2.9 %collective-permute-start = (bf16[1,112,896]{2,1,0:T(8,128)(2,1)}, bf16[1,112,896]{2,1,0:T(8,128)(2,1)}, u32[]{:S(2)}, u32[]{:S(2)}) collective-permute-start(bf16[1,112,896]{2,1,0:T(8,128)(2,1)} %param.6), channel_id=1, source_target_pairs={{0,8},{8,16},{16,24},{24,32},{32,40},{40,48},{48,56},{56,64},{64,7... | collective-permute-start | bytes 602120 | tf_op jit(solution)/shard_map/ppermute | solution.py:14
  27.7 1.4 %gather_fusion = bf16[64,16,196]{2,1,0:T(8,128)(2,1)} fusion(bf16[64,16,196]{2,1,0:T(8,128)(2,1)S(1)} %copy-done.2, s32[1024]{0:T(1024)S(1)} %pad_clamp_fusion), kind=kCustom, calls=%fused_computation | custom fusion | bytes 803072 | tf_op jit(solution)/shard_map/gather | solution.py:124
  29.1 4.7 %reshape_squeeze.6 = bf16[2,16,2,112,112]{4,3,2,1,0:T(8,128)(2,1)S(1)} reshape(bf16[1,2,32,12544]{3,2,1,0:T(8,128)(2,1)} %param.7) | data formatting | bytes 3211264 | tf_op jit(solution)/shard_map/reshape;squeeze | solution.py:74
  33.9 1.4 %copy.54 = bf16[2,16,2,112,112]{4,2,3,1,0:T(2,128)(2,1)S(1)} copy(bf16[2,16,2,112,112]{4,3,2,1,0:T(8,128)(2,1)S(1)} %reshape_squeeze.6) | data formatting | bytes 3211264 | tf_op jit(solution)/shard_map/reshape;squeeze | solution.py:74
  35.3 2.0 %pad_bitcast_fusion = bf16[2,16,112,2,128]{4,3,2,1,0:T(2,128)(2,1)S(1)} fusion(bf16[2,16,2,112,112]{4,2,3,1,0:T(2,128)(2,1)S(1)} %copy.54), kind=kLoop, calls=%fused_computation.2 | loop fusion | bytes 3440640 | tf_op jit(solution)/shard_map/transpose | solution.py:76
  37.3 2.2 %reshape.75 = bf16[2,16,112,256]{3,2,1,0:T(8,128)(2,1)} reshape(bf16[2,16,112,2,128]{4,3,2,1,0:T(2,128)(2,1)S(1)} %pad_bitcast_fusion) | data formatting | bytes 3670016 | tf_op jit(solution)/shard_map/reshape | solution.py:77
  39.4 0.6 iota_compare_fusion
  40.6 1.4 %convert_multiply_fusion = f32[14,896]{1,0:T(8,128)} fusion(f32[14,896]{1,0:T(8,128)S(1)} %sub.21, bf16[1,112,896]{2,1,0:T(8,128)(2,1)} %param.6, s32[]{:T(128)S(6)} %select_n.21, f32[896]{0:T(1024)S(1)} %sub.23), kind=kLoop, calls=%fused_computation.12 | loop fusion | flops 37632 | bytes 129028 | tf_op jit(solution)/shard_map/mul | solution.py:108
  42.0 22.8 %all-to-all-done = bf16[64,48,196]{2,1,0:T(8,128)(2,1)S(1)} async-done(((bf16[64,48,196]{2,1,0:T(8,128)(2,1)}), bf16[64,48,196]{2,1,0:T(8,128)(2,1)S(1)}, u32[]{:S(2)}, u32[]{:S(2)}) %all-to-all-start) | async-done | bytes 1204256 | tf_op jit(solution)/shard_map/all_to_all | solution.py:130
  64.8 0.5 copy.53
  65.4 2.1 %squeeze.30 = bf16[48,12544]{1,0:T(8,128)(2,1)S(1)} reshape(bf16[1,48,64,196]{3,2,1,0:T(8,128)(2,1)S(1)} %copy.53) | data formatting | bytes 2408448 | tf_op jit(solution)/shard_map/squeeze | solution.py:130
  67.5 6.1 %collective-permute-done = bf16[1,112,896]{2,1,0:T(8,128)(2,1)} collective-permute-done((bf16[1,112,896]{2,1,0:T(8,128)(2,1)}, bf16[1,112,896]{2,1,0:T(8,128)(2,1)}, u32[]{:S(2)}, u32[]{:S(2)}) %collective-permute-start) | collective-permute-done | bytes 200736 | tf_op jit(solution)/shard_map/ppermute | solution.py:14
  73.6 11.4 %all-to-all-start.1 = ((bf16[64,16,196]{2,1,0:T(8,128)(2,1)}), bf16[64,16,196]{2,1,0:T(8,128)(2,1)S(1)}, u32[]{:S(2)}, u32[]{:S(2)}) async-start(bf16[64,16,196]{2,1,0:T(8,128)(2,1)} %gather_fusion), calls=%async_computation.1 | async-start | bytes 1048576 | tf_op jit(solution)/shard_map/all_to_all | solution.py:130
  85.0 2.7 %reshape.79 = bf16[48,112,112]{2,1,0:T(8,128)(2,1)S(1)} reshape(bf16[48,12544]{1,0:T(8,128)(2,1)S(1)} %squeeze.30) | data formatting | bytes 2408448 | tf_op jit(solution)/shard_map/reshape | solution.py:136
  87.8 1.2 reshape.77
  89.4 0.2 copy.58
  89.6 0.6 copy.59
  90.2 1.2 reshape.80
  91.7 1.2 slice_bitcast_fusion.1.b_ref
  93.0 7.0 %shard_map.64.acc_ref = f32[896,112]{1,0:T(8,128)S(1)} custom-call(bf16[3584,112]{1,0:T(8,128)(2,1)S(1)} %bitcast.50, bf16[112,1024]{1,0:T(8,128)(2,1)S(1)} %bitcast.55, bf16[16,112,256]{2,1,0:T(8,128)(2,1)S(1)} %slice_bitcast_fusion.1.b_ref, f32[896,112]{1,0:T(8,128)S(1)} %broadcast_in_dim.39.clone.acc_ref), custom_call_target="tpu_custom_call", output_to_operand_aliasing={{}: (3, {})} | custom-call | flops 1541406720 | bytes 2752512 | tf_op jit(solution)/shard_map/pallas_call | solution.py:49
  100.1 3.5 %shard_map.65.acc_ref = f32[896,112]{1,0:T(8,128)S(1)} custom-call(bf16[1792,112]{1,0:T(8,128)(2,1)S(1)} %bitcast.51, bf16[112,1024]{1,0:T(8,128)(2,1)S(1)} %bitcast.53, bf16[8,112,256]{2,1,0:T(8,128)(2,1)S(1)} %get-tuple-element.21.b_ref, f32[896,112]{1,0:T(8,128)S(1)} %shard_map.64.acc_ref), custom_call_target="tpu_custom_call", output_to_operand_aliasing={{}: (3, {})} | custom-call | flops 770703360 | bytes 1892352 | tf_op jit(solution)/shard_map/pallas_call | solution.py:49
  103.7 1.1 reshape_squeeze.7
  105.0 3.5 %shard_map.66 = f32[896,112]{1,0:T(8,128)S(1)} custom-call(bf16[1792,112]{1,0:T(8,128)(2,1)S(1)} %bitcast.52, bf16[112,1024]{1,0:T(8,128)(2,1)S(1)} %bitcast.54, bf16[8,112,256]{2,1,0:T(8,128)(2,1)S(1)} %get-tuple-element.22.b_ref, f32[896,112]{1,0:T(8,128)S(1)} %shard_map.65.acc_ref), custom_call_target="tpu_custom_call", output_to_operand_aliasing={{}: (3, {})} | custom-call | flops 770703360 | bytes 1892352 | tf_op jit(solution)/shard_map/pallas_call | solution.py:49
  108.8 0.3 copy.63
  109.0 7.1 %all_to_all.40 = f32[4,2,14,896]{3,0,2,1:T(4,128)S(1)} all-to-all(f32[4,2,14,896]{3,0,2,1:T(4,128)S(1)} %copy.63), channel_id=1, replica_groups=mesh['ka'=64,'zl'=4,'core'=2] {'core'}, dimensions={1} | all-to-all | bytes 802816 | tf_op jit(solution)/shard_map/all_to_all | solution.py:148
  116.3 10.2 %all_to_all.41 = f32[4,14,896]{2,1,0:T(8,128)S(1)} all-to-all(f32[4,14,896]{2,1,0:T(8,128)S(1)} %copy.64), channel_id=1, replica_groups=mesh['ka'=64,'zl'=4,'core'=2] {'zl'}, dimensions={0} | all-to-all | bytes 401408 | tf_op jit(solution)/shard_map/all_to_all | solution.py:149
  126.5 0.6 fusion
  (42 shorter events, 2.2 us)
Async XLA Ops:
  0.0 2.2 %copy-start.1 = (bf16[64,2,32,196]{3,2,1,0:T(8,128)(2,1)S(1)}, bf16[64,2,32,196]{3,2,1,0:T(8,128)(2,1)}, u32[]{:S(2)}) copy-start(bf16[64,2,32,196]{3,2,1,0:T(8,128)(2,1)} %param.8) | copy-start | bytes 4816900
  0.0 2.3 %copy-start.6 = (s32[64]{0:T(128)S(1)}, s32[64]{0:T(128)}, u32[]{:S(2)}) copy-start(s32[64]{0:T(128)} %param.9) | copy-start | bytes 772
  5.1 22.6 %copy-start.2 = (bf16[64,16,196]{2,1,0:T(8,128)(2,1)S(1)}, bf16[64,16,196]{2,1,0:T(8,128)(2,1)}, u32[]{:S(2)}) copy-start(bf16[64,16,196]{2,1,0:T(8,128)(2,1)} %get-tuple-element.20) | copy-start | bytes 1204228
  5.1 59.8 %all-to-all-start = ((bf16[64,48,196]{2,1,0:T(8,128)(2,1)}), bf16[64,48,196]{2,1,0:T(8,128)(2,1)S(1)}, u32[]{:S(2)}, u32[]{:S(2)}) async-start(bf16[64,48,196]{2,1,0:T(8,128)(2,1)} %gather_fusion.1), calls=%async_computation | async-start | bytes 3145728 | tf_op jit(solution)/shard_map/all_to_all | solution.py:130
  24.8 48.8 %collective-permute-start = (bf16[1,112,896]{2,1,0:T(8,128)(2,1)}, bf16[1,112,896]{2,1,0:T(8,128)(2,1)}, u32[]{:S(2)}, u32[]{:S(2)}) collective-permute-start(bf16[1,112,896]{2,1,0:T(8,128)(2,1)} %param.6), channel_id=1, source_target_pairs={{0,8},{8,16},{16,24},{24,32},{32,40},{40,48},{48,56},{56,64},{64,7... | collective-permute-start | bytes 602120 | tf_op jit(solution)/shard_map/ppermute | solution.py:14
  37.3 2.8 %copy-start.4 = (f32[64,112]{1,0:T(8,128)S(1)}, f32[64,112]{1,0:T(8,128)}, u32[]{:S(2)}) copy-start(f32[64,112]{1,0:T(8,128)} %param.10) | copy-start | bytes 86020
  37.3 3.2 %copy-start.5 = (f32[8]{0:T(128)S(1)}, f32[8]{0:T(128)}, u32[]{:S(2)}) copy-start(f32[8]{0:T(128)} %param.11) | copy-start | bytes 100
  73.6 29.9 %all-to-all-start.1 = ((bf16[64,16,196]{2,1,0:T(8,128)(2,1)}), bf16[64,16,196]{2,1,0:T(8,128)(2,1)S(1)}, u32[]{:S(2)}, u32[]{:S(2)}) async-start(bf16[64,16,196]{2,1,0:T(8,128)(2,1)} %gather_fusion), calls=%async_computation.1 | async-start | bytes 1048576 | tf_op jit(solution)/shard_map/all_to_all | solution.py:130
  93.0 7.0 %copy-start = (bf16[2,16,112,256]{3,2,1,0:T(8,128)(2,1)S(1)}, bf16[2,16,112,256]{3,2,1,0:T(8,128)(2,1)}, u32[]{:S(2)}) copy-start(bf16[2,16,112,256]{3,2,1,0:T(8,128)(2,1)} %reshape.75) | copy-start | bytes 5505028
  108.8 17.8 %copy-start.3 = (f32[14,896]{1,0:T(8,128)S(1)}, f32[14,896]{1,0:T(8,128)}, u32[]{:S(2)}) copy-start(f32[14,896]{1,0:T(8,128)} %convert_multiply_fusion) | copy-start | bytes 150532

commit v16 on v15

--- a/solution.py
+++ b/solution.py
@@ -38,7 +38,7 @@
     out_ref[...] = acc
 
 
-def ladder_transposed(ct, tt, bpair, acc, chunk=16):
+def ladder_transposed(ct, tt, bpair, acc, chunk=4):
     rows, nv = ct.shape
     aux = 2 * bpair.shape[0]
     lanes = 128

time: 129 us -> 128 us (level)
  Pallas kernels: 13.9 us -> 10.3 us
  blocking collectives: 17.3 us -> 18.8 us
  waiting for transfers between devices: 28.9 us -> 30.2 us
    pallas_call x3, Pallas kernels: 13.9 us -> 10.3 us  [ladder_transposed(): pl.pallas_call(kernel, out_shape=jax.ShapeDtypeStruct((pairs * nv, nv), j...]
    all_to_all x1, blocking collectives: 7.08 us -> 8.52 us  [shards(): stacked = lax.all_to_all(stacked, 'core', 1, 1, tiled=True).sum(1)]
  transfers between devices with their start and end apart: 3 -> 3, of which waited for: 2 -> 3; matrix products, arithmetic and copies ran while one was open for 20% -> 20% of each run, Pallas kernels for 8% -> 6%
where the time goes in v16:
time: 128 us; the launch traced here: 126 us
  starting transfers between devices  34 us (27%)
  waiting for transfers between devices  30.2 us (24%)
  local copies, waits for them, and re-layouts  28.7 us (22%)
  blocking collectives  18.8 us (15%)
  Pallas kernels  10.3 us (8%)
  other arithmetic  3.95 us (3%)
    all_to_all x2, starting transfers between devices, shards(): lax.all_to_all(piece, 'ka', split_axis=0, concat_axis=2, tiled=True)[0]  31.1 us
    all_to_all x2, waiting for transfers between devices, shards(): lax.all_to_all(piece, 'ka', split_axis=0, concat_axis=2, tiled=True)[0]  24 us
    pallas_call x3, Pallas kernels, ladder_transposed(): pl.pallas_call(kernel, out_shape=jax.ShapeDtypeStruct((pairs * nv, nv), j...  10.3 us
    all_to_all x1, blocking collectives, shards(): ladder = lax.all_to_all(stacked, 'zl', 0, 0, tiled=True).sum(0)  10.2 us
    all_to_all x1, blocking collectives, shards(): stacked = lax.all_to_all(stacked, 'core', 1, 1, tiled=True).sum(1)  8.52 us
    another operation x2, local copies, waits for them, and re-layouts, left_pairs(): b = left.reshape(transfers, aux // 2, 2, virtuals, virtuals)  6.15 us
    ppermute x1, waiting for transfers between devices, shifted(): return lax.ppermute(value, axis, pairs)  6.14 us
    gather x2, local copies, waits for them, and re-layouts, shards(): piece = piece.at[kb_table].get(mode='promise_in_bounds')  3.18 us
  transfers between devices with their start and end apart: 3, of which 3 were waited for; matrix products, arithmetic and copies ran while one was open for 20% of the time, Pallas kernels for 6%

profile of v16, /device:TPU:1, one launch (start us, length us, event | category | flops | bytes accessed | tf_op | source)
XLA Modules:
  0.0 126.3 jit_solution(7964172429435546166)
XLA Ops:
  0.0 2.2 %slice_bitcast_fusion.2 = (bf16[64,16,196]{2,1,0:T(8,128)(2,1)S(1)}, bf16[64,16,196]{2,1,0:T(8,128)(2,1)}) fusion(bf16[64,2,32,196]{3,2,1,0:T(8,128)(2,1)} %param.8), kind=kLoop, calls=%fused_computation.6 | loop fusion | bytes 1605632 | tf_op jit(solution)/shard_map/squeeze | solution.py:122
  2.3 0.6 select_reduce_fusion.2
  3.0 0.3 pad_maximum_fusion
  3.3 1.8 %gather_fusion.1 = bf16[64,48,196]{2,1,0:T(8,128)(2,1)} fusion(bf16[64,48,196]{2,1,0:T(8,128)(2,1)S(1)} %pad_maximum_fusion, s32[1024]{0:T(1024)S(1)} %pad_clamp_fusion), kind=kCustom, calls=%fused_computation.1 | custom fusion | bytes 2408704 | tf_op jit(solution)/shard_map/gather | solution.py:124
  5.1 19.7 %all-to-all-start = ((bf16[64,48,196]{2,1,0:T(8,128)(2,1)}), bf16[64,48,196]{2,1,0:T(8,128)(2,1)S(1)}, u32[]{:S(2)}, u32[]{:S(2)}) async-start(bf16[64,48,196]{2,1,0:T(8,128)(2,1)} %gather_fusion.1), calls=%async_computation | async-start | bytes 3145728 | tf_op jit(solution)/shard_map/all_to_all | solution.py:130
  24.8 2.9 %collective-permute-start = (bf16[1,112,896]{2,1,0:T(8,128)(2,1)}, bf16[1,112,896]{2,1,0:T(8,128)(2,1)}, u32[]{:S(2)}, u32[]{:S(2)}) collective-permute-start(bf16[1,112,896]{2,1,0:T(8,128)(2,1)} %param.6), channel_id=1, source_target_pairs={{0,8},{8,16},{16,24},{24,32},{32,40},{40,48},{48,56},{56,64},{64,7... | collective-permute-start | bytes 602120 | tf_op jit(solution)/shard_map/ppermute | solution.py:14
  27.7 1.4 %gather_fusion = bf16[64,16,196]{2,1,0:T(8,128)(2,1)} fusion(bf16[64,16,196]{2,1,0:T(8,128)(2,1)S(1)} %copy-done.2, s32[1024]{0:T(1024)S(1)} %pad_clamp_fusion), kind=kCustom, calls=%fused_computation | custom fusion | bytes 803072 | tf_op jit(solution)/shard_map/gather | solution.py:124
  29.1 4.7 %reshape_squeeze.6 = bf16[2,16,2,112,112]{4,3,2,1,0:T(8,128)(2,1)S(1)} reshape(bf16[1,2,32,12544]{3,2,1,0:T(8,128)(2,1)} %param.7) | data formatting | bytes 3211264 | tf_op jit(solution)/shard_map/reshape;squeeze | solution.py:74
  33.9 1.4 %copy.54 = bf16[2,16,2,112,112]{4,2,3,1,0:T(2,128)(2,1)S(1)} copy(bf16[2,16,2,112,112]{4,3,2,1,0:T(8,128)(2,1)S(1)} %reshape_squeeze.6) | data formatting | bytes 3211264 | tf_op jit(solution)/shard_map/reshape;squeeze | solution.py:74
  35.3 2.0 %pad_bitcast_fusion = bf16[2,16,112,2,128]{4,3,2,1,0:T(2,128)(2,1)S(1)} fusion(bf16[2,16,2,112,112]{4,2,3,1,0:T(2,128)(2,1)S(1)} %copy.54), kind=kLoop, calls=%fused_computation.2 | loop fusion | bytes 3440640 | tf_op jit(solution)/shard_map/transpose | solution.py:76
  37.3 2.2 %reshape.75 = bf16[2,16,112,256]{3,2,1,0:T(8,128)(2,1)} reshape(bf16[2,16,112,2,128]{4,3,2,1,0:T(2,128)(2,1)S(1)} %pad_bitcast_fusion) | data formatting | bytes 3670016 | tf_op jit(solution)/shard_map/reshape | solution.py:77
  39.4 0.6 iota_compare_fusion
  40.6 1.4 %convert_multiply_fusion = f32[14,896]{1,0:T(8,128)} fusion(f32[14,896]{1,0:T(8,128)S(1)} %sub.21, bf16[1,112,896]{2,1,0:T(8,128)(2,1)} %param.6, s32[]{:T(128)S(6)} %select_n.21, f32[896]{0:T(1024)S(1)} %sub.23), kind=kLoop, calls=%fused_computation.12 | loop fusion | flops 37632 | bytes 129028 | tf_op jit(solution)/shard_map/mul | solution.py:108
  42.0 22.8 %all-to-all-done = bf16[64,48,196]{2,1,0:T(8,128)(2,1)S(1)} async-done(((bf16[64,48,196]{2,1,0:T(8,128)(2,1)}), bf16[64,48,196]{2,1,0:T(8,128)(2,1)S(1)}, u32[]{:S(2)}, u32[]{:S(2)}) %all-to-all-start) | async-done | bytes 1204256 | tf_op jit(solution)/shard_map/all_to_all | solution.py:130
  64.8 0.5 copy.53
  65.4 2.1 %squeeze.30 = bf16[48,12544]{1,0:T(8,128)(2,1)S(1)} reshape(bf16[1,48,64,196]{3,2,1,0:T(8,128)(2,1)S(1)} %copy.53) | data formatting | bytes 2408448 | tf_op jit(solution)/shard_map/squeeze | solution.py:130
  67.5 6.1 %collective-permute-done = bf16[1,112,896]{2,1,0:T(8,128)(2,1)} collective-permute-done((bf16[1,112,896]{2,1,0:T(8,128)(2,1)}, bf16[1,112,896]{2,1,0:T(8,128)(2,1)}, u32[]{:S(2)}, u32[]{:S(2)}) %collective-permute-start) | collective-permute-done | bytes 200736 | tf_op jit(solution)/shard_map/ppermute | solution.py:14
  73.6 11.4 %all-to-all-start.1 = ((bf16[64,16,196]{2,1,0:T(8,128)(2,1)}), bf16[64,16,196]{2,1,0:T(8,128)(2,1)S(1)}, u32[]{:S(2)}, u32[]{:S(2)}) async-start(bf16[64,16,196]{2,1,0:T(8,128)(2,1)} %gather_fusion), calls=%async_computation.1 | async-start | bytes 1048576 | tf_op jit(solution)/shard_map/all_to_all | solution.py:130
  85.0 2.7 %reshape.79 = bf16[48,112,112]{2,1,0:T(8,128)(2,1)S(1)} reshape(bf16[48,12544]{1,0:T(8,128)(2,1)S(1)} %squeeze.30) | data formatting | bytes 2408448 | tf_op jit(solution)/shard_map/reshape | solution.py:136
  87.8 1.2 reshape.77
  89.6 0.6 copy.59
  90.2 1.2 reshape.80
  91.7 1.2 slice_bitcast_fusion.1.b_ref
  93.0 5.1 %shard_map.64.acc_ref = f32[896,112]{1,0:T(8,128)S(1)} custom-call(bf16[3584,112]{1,0:T(8,128)(2,1)S(1)} %bitcast.50, bf16[112,1024]{1,0:T(8,128)(2,1)S(1)} %bitcast.55, bf16[16,112,256]{2,1,0:T(8,128)(2,1)S(1)} %slice_bitcast_fusion.1.b_ref, f32[896,112]{1,0:T(8,128)S(1)} %broadcast_in_dim.39.clone.acc_ref), custom_call_target="tpu_custom_call", output_to_operand_aliasing={{}: (3, {})} | custom-call | flops 1541406720 | bytes 2752512 | tf_op jit(solution)/shard_map/pallas_call | solution.py:49
  98.3 2.6 %shard_map.65.acc_ref = f32[896,112]{1,0:T(8,128)S(1)} custom-call(bf16[1792,112]{1,0:T(8,128)(2,1)S(1)} %bitcast.51, bf16[112,1024]{1,0:T(8,128)(2,1)S(1)} %bitcast.53, bf16[8,112,256]{2,1,0:T(8,128)(2,1)S(1)} %get-tuple-element.21.b_ref, f32[896,112]{1,0:T(8,128)S(1)} %shard_map.64.acc_ref), custom_call_target="tpu_custom_call", output_to_operand_aliasing={{}: (3, {})} | custom-call | flops 770703360 | bytes 1892352 | tf_op jit(solution)/shard_map/pallas_call | solution.py:49
  100.9 1.2 all-to-all-done.1
  102.3 1.1 reshape_squeeze.7
  103.6 2.6 %shard_map.66 = f32[896,112]{1,0:T(8,128)S(1)} custom-call(bf16[1792,112]{1,0:T(8,128)(2,1)S(1)} %bitcast.52, bf16[112,1024]{1,0:T(8,128)(2,1)S(1)} %bitcast.54, bf16[8,112,256]{2,1,0:T(8,128)(2,1)S(1)} %get-tuple-element.22.b_ref, f32[896,112]{1,0:T(8,128)S(1)} %shard_map.65.acc_ref), custom_call_target="tpu_custom_call", output_to_operand_aliasing={{}: (3, {})} | custom-call | flops 770703360 | bytes 1892352 | tf_op jit(solution)/shard_map/pallas_call | solution.py:49
  106.5 0.3 copy.63
  106.7 8.5 %all_to_all.40 = f32[4,2,14,896]{3,0,2,1:T(4,128)S(1)} all-to-all(f32[4,2,14,896]{3,0,2,1:T(4,128)S(1)} %copy.63), channel_id=1, replica_groups=mesh['ka'=64,'zl'=4,'core'=2] {'core'}, dimensions={1} | all-to-all | bytes 802816 | tf_op jit(solution)/shard_map/all_to_all | solution.py:148
  115.4 10.2 %all_to_all.41 = f32[4,14,896]{2,1,0:T(8,128)S(1)} all-to-all(f32[4,14,896]{2,1,0:T(8,128)S(1)} %copy.64), channel_id=1, replica_groups=mesh['ka'=64,'zl'=4,'core'=2] {'zl'}, dimensions={0} | all-to-all | bytes 401408 | tf_op jit(solution)/shard_map/all_to_all | solution.py:149
  125.7 0.6 fusion
  (42 shorter events, 2.5 us)
Async XLA Ops:
  0.0 2.2 %copy-start.1 = (bf16[64,2,32,196]{3,2,1,0:T(8,128)(2,1)S(1)}, bf16[64,2,32,196]{3,2,1,0:T(8,128)(2,1)}, u32[]{:S(2)}) copy-start(bf16[64,2,32,196]{3,2,1,0:T(8,128)(2,1)} %param.8) | copy-start | bytes 4816900
  0.0 2.3 %copy-start.6 = (s32[64]{0:T(128)S(1)}, s32[64]{0:T(128)}, u32[]{:S(2)}) copy-start(s32[64]{0:T(128)} %param.9) | copy-start | bytes 772
  5.1 22.6 %copy-start.2 = (bf16[64,16,196]{2,1,0:T(8,128)(2,1)S(1)}, bf16[64,16,196]{2,1,0:T(8,128)(2,1)}, u32[]{:S(2)}) copy-start(bf16[64,16,196]{2,1,0:T(8,128)(2,1)} %get-tuple-element.20) | copy-start | bytes 1204228
  5.1 59.8 %all-to-all-start = ((bf16[64,48,196]{2,1,0:T(8,128)(2,1)}), bf16[64,48,196]{2,1,0:T(8,128)(2,1)S(1)}, u32[]{:S(2)}, u32[]{:S(2)}) async-start(bf16[64,48,196]{2,1,0:T(8,128)(2,1)} %gather_fusion.1), calls=%async_computation | async-start | bytes 3145728 | tf_op jit(solution)/shard_map/all_to_all | solution.py:130
  24.8 48.8 %collective-permute-start = (bf16[1,112,896]{2,1,0:T(8,128)(2,1)}, bf16[1,112,896]{2,1,0:T(8,128)(2,1)}, u32[]{:S(2)}, u32[]{:S(2)}) collective-permute-start(bf16[1,112,896]{2,1,0:T(8,128)(2,1)} %param.6), channel_id=1, source_target_pairs={{0,8},{8,16},{16,24},{24,32},{32,40},{40,48},{48,56},{56,64},{64,7... | collective-permute-start | bytes 602120 | tf_op jit(solution)/shard_map/ppermute | solution.py:14
  37.3 2.8 %copy-start.4 = (f32[64,112]{1,0:T(8,128)S(1)}, f32[64,112]{1,0:T(8,128)}, u32[]{:S(2)}) copy-start(f32[64,112]{1,0:T(8,128)} %param.10) | copy-start | bytes 86020
  37.3 3.2 %copy-start.5 = (f32[8]{0:T(128)S(1)}, f32[8]{0:T(128)}, u32[]{:S(2)}) copy-start(f32[8]{0:T(128)} %param.11) | copy-start | bytes 100
  73.6 28.5 %all-to-all-start.1 = ((bf16[64,16,196]{2,1,0:T(8,128)(2,1)}), bf16[64,16,196]{2,1,0:T(8,128)(2,1)S(1)}, u32[]{:S(2)}, u32[]{:S(2)}) async-start(bf16[64,16,196]{2,1,0:T(8,128)(2,1)} %gather_fusion), calls=%async_computation.1 | async-start | bytes 1048576 | tf_op jit(solution)/shard_map/all_to_all | solution.py:130
  93.0 5.2 %copy-start = (bf16[2,16,112,256]{3,2,1,0:T(8,128)(2,1)S(1)}, bf16[2,16,112,256]{3,2,1,0:T(8,128)(2,1)}, u32[]{:S(2)}) copy-start(bf16[2,16,112,256]{3,2,1,0:T(8,128)(2,1)} %reshape.75) | copy-start | bytes 5505028
  106.5 19.2 %copy-start.3 = (f32[14,896]{1,0:T(8,128)S(1)}, f32[14,896]{1,0:T(8,128)}, u32[]{:S(2)}) copy-start(f32[14,896]{1,0:T(8,128)} %convert_multiply_fusion) | copy-start | bytes 150532
